TPU v7x, 1024 devices: a whole 8x8x8 slice. The times are simulated.
1024 devices in a mesh: gx: 32 (over z, y_lo, core), gy: 32 (over x, y_hi).
Axes of the slice: x: 8, y: 8 (y_hi: 4, y_lo: 2; y = y_hi * 2 + y_lo), z: 8, core: 2. Of those that a mesh axis runs over, the one named last changes fastest.
Arguments:
- load_field: float32 [128, 256, 64, 128], P('gx', 'gy'), may hold values from -6 to 6
- stiffness: float32 [128, 256], P('gx', 'gy'), may hold values from 0.5 to 2
- fault_mask: int32 [128, 256], P('gx', 'gy'), may hold values 0 or 1
- column_operator: float32 [64, 64], replicated
- patch_inverse: bfloat16 [32, 32, 8, 256, 256], P('gx', 'gy')
- patch_anchor: int32 [32, 32, 8], P('gx', 'gy'), may hold values from 0 to 20, as said below
- patch_count: int32 [32, 32], P('gx', 'gy'), may hold values from 1 to 8, as said below
Outputs:
- smoothed: float32 [128, 256, 64, 128], P('gx', 'gy')
Inputs may be any that keep to these rules, and one draw needn't show every extreme that they name: `patch_anchor`: the anchors of one device are distinct. `patch_count`: all devices of one gy index below the last, drawn from the seed, have exactly 8 live slots; every other device has at most 4.
All inputs are finite; a program needn't handle non-finite values. No bound on the sum of `fault_mask` on one device may be relied on, other than what follows from the above.
Results may differ from a plain program's by a relative error of at most 0.0027.
Values may be sent and summed in bfloat16 or wider, within the bound.
No kernel may reach another device: no remote copies, remote signals or barrier semaphores. Data moves between devices by JAX's collectives and lax.ppermute only.
A program may use at most 32 MiB of HBM per device.

v0:
```python
import jax
import jax.numpy as jnp
from jax import lax
from jax.sharding import PartitionSpec as P

SWEEPS = 2


damping = 0.5


def extended(cells, sides, width):
    for axis, dim in sides:
        count = lax.axis_size(axis)
        ends = count - 1
        head = lax.slice_in_dim(cells, 0, width, axis=dim)
        tail = lax.slice_in_dim(cells, cells.shape[dim] - width, cells.shape[dim], axis=dim)
        cells = jnp.concatenate(
            [
                lax.ppermute(tail, axis, [(i, (i + 1) % count) for i in range(ends)]),
                cells,
                lax.ppermute(head, axis, [((i + 1) % count, i) for i in range(ends)]),
            ],
            axis=dim,
        )
    return cells


def per_device(
    load_field, stiffness, fault_mask, column_operator, patch_inverse, patch_anchor, patch_count
):
    rows, columns, depth, loads = load_field.shape
    patch_rows = 4 * depth
    weight = 1.0 - 0.6 * fault_mask.astype(jnp.float32)
    inverse = patch_inverse[0, 0]
    anchors = patch_anchor[0, 0]
    count = patch_count[0, 0]
    zero = jnp.int32(0)

    def residual_of(field):
        padded, wide = (
            extended(field, (("gx", 0), ("gy", 1)), 1),
            extended(weight, (("gx", 0), ("gy", 1)), 1),
        )
        local = jnp.einsum("kl,xylr->xykr", column_operator, field, precision=lax.Precision.HIGHEST)
        beside = wide[2:, 1:-1, None, None] * padded[2:, 1:-1]
        beside = beside + wide[:-2, 1:-1, None, None] * padded[:-2, 1:-1]
        beside = beside + wide[1:-1, 2:, None, None] * padded[1:-1, 2:]
        beside = beside + wide[1:-1, :-2, None, None] * padded[1:-1, :-2]
        return load_field - (
            stiffness[:, :, None, None] * local - weight[:, :, None, None] * beside
        )

    def corner(number):
        anchor = anchors[number]
        return (anchor // (columns - 1), anchor % (columns - 1))

    def take(packed, number):
        row, column = corner(number)
        return lax.dynamic_slice(packed, (row, column, zero, zero), (2, 2, depth, loads)).reshape(
            patch_rows, loads
        )

    def apply_patch(matrix, piece):
        return damping * jnp.dot(matrix, piece, preferred_element_type=jnp.float32)

    def deposit(delta, number, term):
        row, column = corner(number)
        current = lax.dynamic_slice(delta, (row, column, zero, zero), (2, 2, depth, loads))
        return lax.dynamic_update_slice(
            delta, current + term.reshape(2, 2, depth, loads), (row, column, zero, zero)
        )

    field = jnp.zeros(load_field.shape, jnp.float32)
    for sweep in range(SWEEPS):
        residual = load_field if sweep == 0 else residual_of(field)
        packed = residual.astype(jnp.bfloat16)
        empty = jnp.zeros(load_field.shape, jnp.float32)

        def visit(number, total):
            return deposit(total, number, apply_patch(inverse[number], take(packed, number)))

        delta = lax.fori_loop(0, count, visit, empty)
        field = field + delta
    return field


def solution(mesh):
    return jax.shard_map(
        per_device,
        mesh=mesh,
        in_specs=(
            P("gx", "gy", None, None),
            P("gx", "gy"),
            P("gx", "gy"),
            P(),
            P("gx", "gy", None, None, None),
            P("gx", "gy", None),
            P("gx", "gy"),
        ),
        out_specs=P("gx", "gy", None, None),
        check_vma=False,
    )
```

profile of v0, /device:TPU:436, one launch (start us, length us, event | category | flops | bytes accessed | tf_op | source)
XLA Modules:
  0.0 115.2 jit_solution(4666887341070391755)
XLA Ops:
  0.0 0.7 multiply_subtract_fusion
  0.7 1.9 %collective-permute-start = (f32[1,8]{1,0:T(1,128)S(1)}, f32[1,8]{1,0:T(1,128)S(1)}, u32[]{:S(2)}, u32[]{:S(2)}) collective-permute-start(f32[1,8]{1,0:T(1,128)S(1)} %get-tuple-element.208), channel_id=1, source_target_pairs={{32,0},{64,32},{96,64},{128,96},{160,128},{192,160},{224,192},{256... | collective-permute-start | bytes 104 | tf_op jit(solution)/shard_map/ppermute | solution.py:22
  2.6 2.4 %collective-permute-start.2 = (f32[1,8]{1,0:T(1,128)S(1)}, f32[1,8]{1,0:T(1,128)S(1)}, u32[]{:S(2)}, u32[]{:S(2)}) collective-permute-start(f32[1,8]{1,0:T(1,128)S(1)} %get-tuple-element.207), channel_id=1, source_target_pairs={{0,32},{32,64},{64,96},{96,128},{128,160},{160,192},{192,224},{224... | collective-permute-start | bytes 104 | tf_op jit(solution)/shard_map/ppermute | solution.py:20
  5.0 1.3 %convert_element_type.9 = bf16[4,8,64,128]{3,2,1,0:T(8,128)(2,1)S(1)} convert(f32[4,8,64,128]{3,2,1,0:T(8,128)} %param.11) | non-fusion elementwise | flops 262144 | bytes 1572864 | tf_op jit(solution)/shard_map/convert_element_type | solution.py:77
  6.4 0.1 broadcast.22.clone
  6.5 0.0 copy-done.3
  6.5 37.4 %while.24 = (s32[]{:T(128)}, f32[4,8,64,128]{3,2,1,0:T(8,128)S(1)}, s32[]{:T(128)}, s32[8]{0:T(128)S(1)}, bf16[8,256,256]{2,1,0:T(8,128)(2,1)}, /*index=5*/bf16[...) while((s32[]{:T(128)}, f32[4,8,64,128]{3,2,1,0:T(8,128)S(1)}, ...), condition=%wide.region_1.2_spmd, body=%wide.region_0.1_spmd.sunk | while | flops 16842776 | bytes 852350 | solution.py:83
  7.2 0.7 dynamic_slice.73
  10.0 1.1 convolution_multiply_fusion.5
  11.7 0.7 dynamic_slice.73
  14.6 1.1 convolution_multiply_fusion.5
  16.3 0.7 dynamic_slice.73
  19.1 1.1 convolution_multiply_fusion.5
  20.9 0.7 dynamic_slice.73
  23.7 1.1 convolution_multiply_fusion.5
  25.5 0.7 dynamic_slice.73
  28.3 1.1 convolution_multiply_fusion.5
  30.1 0.7 dynamic_slice.73
  32.9 1.1 convolution_multiply_fusion.5
  34.7 0.7 dynamic_slice.73
  37.5 1.1 convolution_multiply_fusion.5
  39.3 0.7 dynamic_slice.73
  42.1 1.1 convolution_multiply_fusion.5
  43.9 5.8 %collective-permute-start.3 = (f32[1,8,64,128]{3,2,1,0:T(8,128)S(1)}, f32[1,8,64,128]{3,2,1,0:T(8,128)S(1)}, u32[]{:S(2)}, u32[]{:S(2)}) collective-permute-start(f32[1,8,64,128]{3,2,1,0:T(8,128)S(1)} %get-tuple-element.200), channel_id=1, source_target_pairs={{0,32},{32,64},{64,96},{96,128},{128,160},{160,192},{192,224},{224... | collective-permute-start | bytes 786440 | tf_op jit(solution)/shard_map/ppermute | solution.py:20
  49.7 1.9 %collective-permute-start.1 = (f32[1,8,64,128]{3,2,1,0:T(8,128)S(1)}, f32[1,8,64,128]{3,2,1,0:T(8,128)S(1)}, u32[]{:S(2)}, u32[]{:S(2)}) collective-permute-start(f32[1,8,64,128]{3,2,1,0:T(8,128)S(1)} %get-tuple-element.199), channel_id=1, source_target_pairs={{32,0},{64,32},{96,64},{128,96},{160,128},{192,160},{224,192},{256... | collective-permute-start | bytes 786440 | tf_op jit(solution)/shard_map/ppermute | solution.py:22
  51.6 0.0 collective-permute-done
  51.6 0.0 collective-permute-done.2
  51.7 0.1 fusion.21
  51.7 1.9 %collective-permute-start.4 = (f32[6,1]{1,0:T(8,128)S(1)}, f32[6,1]{1,0:T(8,128)S(1)}, u32[]{:S(2)}, u32[]{:S(2)}) collective-permute-start(f32[6,1]{1,0:T(8,128)S(1)} %get-tuple-element.201), channel_id=1, source_target_pairs={{1,0},{2,1},{3,2},{4,3},{5,4},{6,5},{7,6},{8,7},{9,8},{10,9},{11,1... | collective-permute-start | bytes 80 | tf_op jit(solution)/shard_map/ppermute | solution.py:22
  53.7 6.0 %collective-permute-start.6 = (f32[6,1]{1,0:T(8,128)S(1)}, f32[6,1]{1,0:T(8,128)S(1)}, u32[]{:S(2)}, u32[]{:S(2)}) collective-permute-start(f32[6,1]{1,0:T(8,128)S(1)} %get-tuple-element.202), channel_id=1, source_target_pairs={{0,1},{1,2},{2,3},{3,4},{4,5},{5,6},{6,7},{7,8},{8,9},{9,10},{10,1... | collective-permute-start | bytes 80 | tf_op jit(solution)/shard_map/ppermute | solution.py:20
  59.7 0.0 collective-permute-done.3
  59.7 0.0 copy-start.1
  59.8 0.0 copy-start.2
  59.8 0.1 constant_dynamic-update-slice_fusion.1
  59.8 0.0 collective-permute-done.1
  59.9 2.1 %collective-permute-start.5 = (f32[6,1,64,128]{3,2,1,0:T(8,128)S(1)}, f32[6,1,64,128]{3,2,1,0:T(8,128)S(1)}, u32[]{:S(2)}, u32[]{:S(2)}) collective-permute-start(f32[6,1,64,128]{3,2,1,0:T(8,128)S(1)} %get-tuple-element.197), channel_id=1, source_target_pairs={{1,0},{2,1},{3,2},{4,3},{5,4},{6,5},{7,6},{8,7},{9,8},{10,9},{11,1... | collective-permute-start | bytes 589832 | tf_op jit(solution)/shard_map/ppermute | solution.py:22
  62.0 6.0 %collective-permute-start.7 = (f32[6,1,64,128]{3,2,1,0:T(8,128)S(1)}, f32[6,1,64,128]{3,2,1,0:T(8,128)S(1)}, u32[]{:S(2)}, u32[]{:S(2)}) collective-permute-start(f32[6,1,64,128]{3,2,1,0:T(8,128)S(1)} %get-tuple-element.198), channel_id=1, source_target_pairs={{0,1},{1,2},{2,3},{3,4},{4,5},{5,6},{6,7},{7,8},{8,9},{9,10},{10,1... | collective-permute-start | bytes 589832 | tf_op jit(solution)/shard_map/ppermute | solution.py:20
  68.1 0.0 collective-permute-done.4
  68.1 0.0 collective-permute-done.6
  68.1 0.1 pad_maximum_fusion.7
  68.2 0.1 slice.65
  68.2 3.1 %collective-permute-done.5 = f32[6,1,64,128]{3,2,1,0:T(8,128)S(1)} collective-permute-done((f32[6,1,64,128]{3,2,1,0:T(8,128)S(1)}, f32[6,1,64,128]{3,2,1,0:T(8,128)S(1)}, u32[]{:S(2)}, u32[]{:S(2)}) %collective-permute-start.5) | collective-permute-done | bytes 196640 | tf_op jit(solution)/shard_map/ppermute | solution.py:22
  71.3 3.8 %collective-permute-done.7 = f32[6,1,64,128]{3,2,1,0:T(8,128)S(1)} collective-permute-done((f32[6,1,64,128]{3,2,1,0:T(8,128)S(1)}, f32[6,1,64,128]{3,2,1,0:T(8,128)S(1)}, u32[]{:S(2)}, u32[]{:S(2)}) %collective-permute-start.7) | collective-permute-done | bytes 196640 | tf_op jit(solution)/shard_map/ppermute | solution.py:20
  75.1 0.0 copy-done.1
  75.1 1.5 %fusion.12 = bf16[4,8,64,128]{3,2,1,0:T(8,128)(2,1)S(1)} fusion(f32[4,8,64,128]{3,2,1,0:T(8,128)S(1)} %copy-done.1, f32[6,8,64,128]{3,2,1,0:T(8,128)S(1)} %constant_dynamic-update-slice_fusion, f32[6,1,64,128]{3,2,1,0:T(8,128)S(1)} %collective-permute-done.7, f32[6,1,64,128]{3,2,1,0:T(8,128)S(1)} %collective-permute-done.5, ...), kind=kOutput, calls=%fused_computation.20 | convolution fusion | flops 205520896 | bytes 5128960 | tf_op jit(solution)/shard_map/kl,xylr->xykr/dot_general | solution.py:45
  76.6 0.1 broadcast.22
  76.7 37.4 %while.25 = (s32[]{:T(128)}, f32[4,8,64,128]{3,2,1,0:T(8,128)S(1)}, s32[]{:T(128)}, s32[8]{0:T(128)S(1)}, bf16[8,256,256]{2,1,0:T(8,128)(2,1)}, /*index=5*/bf16[...) while((s32[]{:T(128)}, f32[4,8,64,128]{3,2,1,0:T(8,128)S(1)}, ...), condition=%wide.region_3.4_spmd, body=%wide.region_2.3_spmd.sunk | while | flops 16842776 | bytes 852350 | solution.py:83
  77.4 0.7 dynamic_slice.77
  80.2 1.1 convolution_multiply_fusion.6
  82.0 0.7 dynamic_slice.77
  84.8 1.1 convolution_multiply_fusion.6
  86.6 0.7 dynamic_slice.77
  89.4 1.1 convolution_multiply_fusion.6
  91.2 0.7 dynamic_slice.77
  94.0 1.1 convolution_multiply_fusion.6
  95.8 0.7 dynamic_slice.77
  98.6 1.1 convolution_multiply_fusion.6
  100.3 0.7 dynamic_slice.77
  103.1 1.1 convolution_multiply_fusion.6
  104.9 0.7 dynamic_slice.77
  107.7 1.1 convolution_multiply_fusion.6
  109.5 0.7 dynamic_slice.77
  112.3 1.1 convolution_multiply_fusion.6
  114.1 1.1 add.110
  (46 shorter events, 0.8 us)
Async XLA Ops:
  0.0 75.1 %copy-start = (f32[64,64]{1,0:T(8,128)S(1)}, f32[64,64]{1,0:T(8,128)}, u32[]{:S(2)}) copy-start(f32[64,64]{1,0:T(8,128)} %param.14) | copy-start | bytes 49156
  0.0 6.5 %copy-start.3 = (s32[1,1,8]{2,1,0:T(1,128)S(1)}, s32[1,1,8]{2,1,0:T(1,128)}, u32[]{:S(2)}) copy-start(s32[1,1,8]{2,1,0:T(1,128)} %param.16) | copy-start | bytes 100
  0.7 50.9 %collective-permute-start = (f32[1,8]{1,0:T(1,128)S(1)}, f32[1,8]{1,0:T(1,128)S(1)}, u32[]{:S(2)}, u32[]{:S(2)}) collective-permute-start(f32[1,8]{1,0:T(1,128)S(1)} %get-tuple-element.208), channel_id=1, source_target_pairs={{32,0},{64,32},{96,64},{128,96},{160,128},{192,160},{224,192},{256... | collective-permute-start | bytes 104 | tf_op jit(solution)/shard_map/ppermute | solution.py:22
  2.6 49.0 %collective-permute-start.2 = (f32[1,8]{1,0:T(1,128)S(1)}, f32[1,8]{1,0:T(1,128)S(1)}, u32[]{:S(2)}, u32[]{:S(2)}) collective-permute-start(f32[1,8]{1,0:T(1,128)S(1)} %get-tuple-element.207), channel_id=1, source_target_pairs={{0,32},{32,64},{64,96},{96,128},{128,160},{160,192},{192,224},{224... | collective-permute-start | bytes 104 | tf_op jit(solution)/shard_map/ppermute | solution.py:20
  43.9 15.8 %collective-permute-start.3 = (f32[1,8,64,128]{3,2,1,0:T(8,128)S(1)}, f32[1,8,64,128]{3,2,1,0:T(8,128)S(1)}, u32[]{:S(2)}, u32[]{:S(2)}) collective-permute-start(f32[1,8,64,128]{3,2,1,0:T(8,128)S(1)} %get-tuple-element.200), channel_id=1, source_target_pairs={{0,32},{32,64},{64,96},{96,128},{128,160},{160,192},{192,224},{224... | collective-permute-start | bytes 786440 | tf_op jit(solution)/shard_map/ppermute | solution.py:20
  49.7 10.1 %collective-permute-start.1 = (f32[1,8,64,128]{3,2,1,0:T(8,128)S(1)}, f32[1,8,64,128]{3,2,1,0:T(8,128)S(1)}, u32[]{:S(2)}, u32[]{:S(2)}) collective-permute-start(f32[1,8,64,128]{3,2,1,0:T(8,128)S(1)} %get-tuple-element.199), channel_id=1, source_target_pairs={{32,0},{64,32},{96,64},{128,96},{160,128},{192,160},{224,192},{256... | collective-permute-start | bytes 786440 | tf_op jit(solution)/shard_map/ppermute | solution.py:22
  51.7 16.3 %collective-permute-start.4 = (f32[6,1]{1,0:T(8,128)S(1)}, f32[6,1]{1,0:T(8,128)S(1)}, u32[]{:S(2)}, u32[]{:S(2)}) collective-permute-start(f32[6,1]{1,0:T(8,128)S(1)} %get-tuple-element.201), channel_id=1, source_target_pairs={{1,0},{2,1},{3,2},{4,3},{5,4},{6,5},{7,6},{8,7},{9,8},{10,9},{11,1... | collective-permute-start | bytes 80 | tf_op jit(solution)/shard_map/ppermute | solution.py:22
  53.7 14.4 %collective-permute-start.6 = (f32[6,1]{1,0:T(8,128)S(1)}, f32[6,1]{1,0:T(8,128)S(1)}, u32[]{:S(2)}, u32[]{:S(2)}) collective-permute-start(f32[6,1]{1,0:T(8,128)S(1)} %get-tuple-element.202), channel_id=1, source_target_pairs={{0,1},{1,2},{2,3},{3,4},{4,5},{5,6},{6,7},{7,8},{8,9},{9,10},{10,1... | collective-permute-start | bytes 80 | tf_op jit(solution)/shard_map/ppermute | solution.py:20
  59.7 15.4 %copy-start.1 = (f32[4,8,64,128]{3,2,1,0:T(8,128)S(1)}, f32[4,8,64,128]{3,2,1,0:T(8,128)}, u32[]{:S(2)}) copy-start(f32[4,8,64,128]{3,2,1,0:T(8,128)} %param.11) | copy-start | bytes 3145732
  59.8 15.4 %copy-start.2 = (f32[4,8]{1,0:T(4,128)S(1)}, f32[4,8]{1,0:T(4,128)}, u32[]{:S(2)}) copy-start(f32[4,8]{1,0:T(4,128)} %param.12) | copy-start | bytes 388
  59.9 11.4 %collective-permute-start.5 = (f32[6,1,64,128]{3,2,1,0:T(8,128)S(1)}, f32[6,1,64,128]{3,2,1,0:T(8,128)S(1)}, u32[]{:S(2)}, u32[]{:S(2)}) collective-permute-start(f32[6,1,64,128]{3,2,1,0:T(8,128)S(1)} %get-tuple-element.197), channel_id=1, source_target_pairs={{1,0},{2,1},{3,2},{4,3},{5,4},{6,5},{7,6},{8,7},{9,8},{10,9},{11,1... | collective-permute-start | bytes 589832 | tf_op jit(solution)/shard_map/ppermute | solution.py:22
  62.0 13.1 %collective-permute-start.7 = (f32[6,1,64,128]{3,2,1,0:T(8,128)S(1)}, f32[6,1,64,128]{3,2,1,0:T(8,128)S(1)}, u32[]{:S(2)}, u32[]{:S(2)}) collective-permute-start(f32[6,1,64,128]{3,2,1,0:T(8,128)S(1)} %get-tuple-element.198), channel_id=1, source_target_pairs={{0,1},{1,2},{2,3},{3,4},{4,5},{5,6},{6,7},{7,8},{8,9},{9,10},{10,1... | collective-permute-start | bytes 589832 | tf_op jit(solution)/shard_map/ppermute | solution.py:20
where the time goes:
time: 117 us; the launch traced here: 115 us
  loops' own time  46.2 us (39%)
  starting transfers between devices  28 us (24%)
  matrix products  18.7 us (16%)
  local copies, waits for them, and re-layouts  11.4 us (10%)
  waiting for transfers between devices  6.9 us (6%)
  other arithmetic  3.66 us (3%)
    another operation x2, loops' own time, per_device(): delta = lax.fori_loop(0, count, visit, empty)  46.2 us
    ppermute x4, starting transfers between devices, extended(): lax.ppermute(tail, axis, [(i, (i + 1) % count) for i in range(ends)])  20.3 us
    dot_general x16, matrix products, apply_patch(): return damping * jnp.dot(matrix, piece, preferred_element_type=jnp.float32)  17.2 us
    dynamic_slice x16, local copies, waits for them, and re-layouts, corner(): anchor = anchors[number]  10.6 us
    ppermute x4, starting transfers between devices, extended(): lax.ppermute(head, axis, [((i + 1) % count, i) for i in range(ends)])  7.79 us
    ppermute x4, waiting for transfers between devices, extended(): lax.ppermute(tail, axis, [(i, (i + 1) % count) for i in range(ends)])  3.79 us
    ppermute x4, waiting for transfers between devices, extended(): lax.ppermute(head, axis, [((i + 1) % count, i) for i in range(ends)])  3.11 us
  transfers between devices with their start and end apart: 8, of which 2 were waited for; matrix products, arithmetic and copies ran while one was open for 14% of the time, Pallas kernels for 0%

commit v1 on v0

v1 whole, which is shorter than its diff:
```python
import jax
import jax.numpy as jnp
from jax import lax
from jax.experimental import pallas as pl
from jax.experimental.pallas import tpu as pltpu
from jax.sharding import PartitionSpec as P

SWEEPS = 2


damping = 0.5


def patch_kernel(anchor_ref, count_ref, src_ref, inv_ref, *rest):
    if len(rest) == 3:
        base_ref, out_ref, acc_ref = rest
    else:
        base_ref = None
        out_ref, acc_ref = rest
    rows, columns, depth, loads = src_ref.shape
    slots = inv_ref.shape[0]
    count = count_ref[0]
    acc_ref[...] = jnp.zeros(acc_ref.shape, jnp.float32)
    for number in range(slots):

        @pl.when(number < count)
        def _():
            anchor = anchor_ref[number]
            row = anchor // (columns - 1)
            column = anchor % (columns - 1)
            pieces = [
                src_ref[row + i, column + j].astype(jnp.bfloat16)
                for i in range(2)
                for j in range(2)
            ]
            piece = jnp.concatenate(pieces, axis=0)
            term = damping * jnp.dot(
                inv_ref[number], piece, preferred_element_type=jnp.float32
            )
            for k in range(4):
                i, j = divmod(k, 2)
                acc_ref[row + i, column + j] += term[k * depth : (k + 1) * depth]

    if base_ref is None:
        out_ref[...] = acc_ref[...]
    else:
        out_ref[...] = base_ref[...] + acc_ref[...]


def patches(src, inverse, anchors, count, base=None):
    smem = pl.BlockSpec(memory_space=pltpu.SMEM)
    vmem = pl.BlockSpec(memory_space=pltpu.VMEM)
    operands = [anchors, count.reshape(1), src, inverse]
    if base is not None:
        operands.append(base)
    return pl.pallas_call(
        patch_kernel,
        out_shape=jax.ShapeDtypeStruct(src.shape, jnp.float32),
        in_specs=[smem, smem] + [vmem] * (len(operands) - 2),
        out_specs=vmem,
        scratch_shapes=[pltpu.VMEM(src.shape, jnp.float32)],
    )(*operands)


def shifted_in(edge, axis, forward):
    count = lax.axis_size(axis)
    if forward:
        pairs = [(i, i + 1) for i in range(count - 1)]
    else:
        pairs = [(i + 1, i) for i in range(count - 1)]
    return lax.ppermute(edge, axis, pairs)


def per_device(
    load_field, stiffness, fault_mask, column_operator, patch_inverse, patch_anchor, patch_count
):
    weight = 1.0 - 0.6 * fault_mask.astype(jnp.float32)
    inverse = patch_inverse[0, 0]
    anchors = patch_anchor[0, 0]
    count = patch_count[0, 0]

    def residual_of(field):
        weighted = weight[:, :, None, None] * field
        above = shifted_in(weighted[-1:], "gx", True)
        below = shifted_in(weighted[:1], "gx", False)
        left = shifted_in(weighted[:, -1:], "gy", True)
        right = shifted_in(weighted[:, :1], "gy", False)
        local = jnp.einsum("kl,xylr->xykr", column_operator, field, precision=lax.Precision.HIGHEST)
        next_x = jnp.concatenate([weighted[1:], below], axis=0)
        prev_x = jnp.concatenate([above, weighted[:-1]], axis=0)
        next_y = jnp.concatenate([weighted[:, 1:], right], axis=1)
        prev_y = jnp.concatenate([left, weighted[:, :-1]], axis=1)
        beside = next_x + prev_x + next_y + prev_y
        return load_field - (
            stiffness[:, :, None, None] * local - weight[:, :, None, None] * beside
        )

    field = patches(load_field, inverse, anchors, count)
    for sweep in range(1, SWEEPS):
        packed = residual_of(field).astype(jnp.bfloat16)
        field = patches(packed, inverse, anchors, count, base=field)
    return field


def solution(mesh):
    return jax.shard_map(
        per_device,
        mesh=mesh,
        in_specs=(
            P("gx", "gy", None, None),
            P("gx", "gy"),
            P("gx", "gy"),
            P(),
            P("gx", "gy", None, None, None),
            P("gx", "gy", None),
            P("gx", "gy"),
        ),
        out_specs=P("gx", "gy", None, None),
        check_vma=False,
    )
```

time: 117 us -> 39.7 us (0.34)
  the two profiles are of different devices: /device:TPU:436 before, /device:TPU:475 now
where the time goes in v1:
time: 39.7 us; the launch traced here: 39.3 us
  starting transfers between devices  17.2 us (43%)
  Pallas kernels  8.45 us (21%)
  waiting for transfers between devices  7.44 us (19%)
  matrix products  2.23 us (6%)
  other arithmetic  2.04 us (5%)
  local copies, waits for them, and re-layouts  1.12 us (3%)
  between operations  0.77 us (2%)
    ppermute x4, starting transfers between devices, shifted_in(): return lax.ppermute(edge, axis, pairs)  17.2 us
    pallas_call x2, Pallas kernels, patches(): pl.pallas_call(patch_kernel, out_shape=jax.ShapeDtypeStruct(src.shape, jn...  8.45 us
    ppermute x4, waiting for transfers between devices, shifted_in(): return lax.ppermute(edge, axis, pairs)  7.44 us
    dot_general x1, matrix products, residual_of(): jnp.einsum('kl,xylr->xykr', column_operator, field, precision=lax.Precisi...  2.23 us
    mul x1, other arithmetic, residual_of(): weighted = weight[:, :, None, None] * field  1.36 us
  transfers between devices with their start and end apart: 4, of which 2 were waited for; matrix products, arithmetic and copies ran while one was open for 1% of the time, Pallas kernels for 0%

profile of v1, /device:TPU:475, one launch (start us, length us, event | category | flops | bytes accessed | tf_op | source)
XLA Modules:
  0.0 39.3 jit_solution(3754151538025446481)
XLA Ops:
  0.0 0.0 copy-start
  0.7 0.7 %multiply_subtract_fusion = f32[4,8]{1,0:T(4,128)S(1)} fusion(s32[4,8]{1,0:T(4,128)} %param.9), kind=kLoop, calls=%fused_computation.11 | loop fusion | flops 96 | bytes 256 | tf_op jit(solution)/shard_map/sub | solution.py:77
  1.4 4.1 %shard_map.73.rest_0_ = f32[4,8,64,128]{3,2,1,0:T(8,128)} custom-call(s32[8]{0:T(128)} %bitcast.17, s32[1]{0:T(128)} %bitcast.13.count_ref, f32[4,8,64,128]{3,2,1,0:T(8,128)} %src_ref.1, bf16[8,256,256]{2,1,0:T(8,128)(2,1)} %bitcast.15), custom_call_target="tpu_custom_call" | custom-call | tf_op jit(solution)/shard_map/pallas_call | solution.py:56
  5.5 1.4 %broadcast_multiply_fusion = f32[4,8,64,128]{3,2,1,0:T(8,128)S(1)} fusion(f32[4,8,64,128]{3,2,1,0:T(8,128)} %shard_map.73.rest_0_, f32[4,8]{1,0:T(4,128)S(1)} %multiply_subtract_fusion), kind=kLoop, calls=%fused_computation.9 | loop fusion | flops 262144 | bytes 2097280 | tf_op jit(solution)/shard_map/mul | solution.py:83
  6.9 1.9 %collective-permute-start.3 = (f32[4,1,64,128]{3,2,1,0:T(8,128)S(1)}, f32[4,1,64,128]{3,2,1,0:T(8,128)S(1)}, u32[]{:S(2)}, u32[]{:S(2)}) collective-permute-start(f32[4,1,64,128]{3,2,1,0:T(8,128)S(1)} %get-tuple-element.5), channel_id=1, source_target_pairs={{0,1},{1,2},{2,3},{3,4},{4,5},{5,6},{6,7},{7,8},{8,9},{9,10},{10,1... | collective-permute-start | bytes 393224 | tf_op jit(solution)/shard_map/ppermute | solution.py:71
  8.8 5.5 %collective-permute-start.2 = (f32[4,1,64,128]{3,2,1,0:T(8,128)S(1)}, f32[4,1,64,128]{3,2,1,0:T(8,128)S(1)}, u32[]{:S(2)}, u32[]{:S(2)}) collective-permute-start(f32[4,1,64,128]{3,2,1,0:T(8,128)S(1)} %get-tuple-element.6), channel_id=1, source_target_pairs={{1,0},{2,1},{3,2},{4,3},{5,4},{6,5},{7,6},{8,7},{9,8},{10,9},{11,1... | collective-permute-start | bytes 393224 | tf_op jit(solution)/shard_map/ppermute | solution.py:71
  14.3 7.9 %collective-permute-start.1 = (f32[1,8,64,128]{3,2,1,0:T(8,128)S(1)}, f32[1,8,64,128]{3,2,1,0:T(8,128)S(1)}, u32[]{:S(2)}, u32[]{:S(2)}) collective-permute-start(f32[1,8,64,128]{3,2,1,0:T(8,128)S(1)} %get-tuple-element.9), channel_id=1, source_target_pairs={{0,32},{32,64},{64,96},{96,128},{128,160},{160,192},{192,224},{224... | collective-permute-start | bytes 786440 | tf_op jit(solution)/shard_map/ppermute | solution.py:71
  22.3 1.9 %collective-permute-start = (f32[1,8,64,128]{3,2,1,0:T(8,128)S(1)}, f32[1,8,64,128]{3,2,1,0:T(8,128)S(1)}, u32[]{:S(2)}, u32[]{:S(2)}) collective-permute-start(f32[1,8,64,128]{3,2,1,0:T(8,128)S(1)} %get-tuple-element.10), channel_id=1, source_target_pairs={{32,0},{64,32},{96,64},{128,96},{160,128},{192,160},{224,192},{256... | collective-permute-start | bytes 786440 | tf_op jit(solution)/shard_map/ppermute | solution.py:71
  24.2 0.2 fusion.9
  24.4 0.0 copy-start.1
  24.4 0.0 copy-start.2
  24.4 0.2 fusion.11
  24.6 0.0 collective-permute-done.3
  24.6 0.0 collective-permute-done.2
  24.6 2.8 %collective-permute-done.1 = f32[1,8,64,128]{3,2,1,0:T(8,128)S(1)} collective-permute-done((f32[1,8,64,128]{3,2,1,0:T(8,128)S(1)}, f32[1,8,64,128]{3,2,1,0:T(8,128)S(1)}, u32[]{:S(2)}, u32[]{:S(2)}) %collective-permute-start.1) | collective-permute-done | bytes 262176 | tf_op jit(solution)/shard_map/ppermute | solution.py:71
  27.4 4.6 %collective-permute-done = f32[1,8,64,128]{3,2,1,0:T(8,128)S(1)} collective-permute-done((f32[1,8,64,128]{3,2,1,0:T(8,128)S(1)}, f32[1,8,64,128]{3,2,1,0:T(8,128)S(1)}, u32[]{:S(2)}, u32[]{:S(2)}) %collective-permute-start) | collective-permute-done | bytes 262176 | tf_op jit(solution)/shard_map/ppermute | solution.py:71
  32.1 0.0 copy-start.3
  32.1 0.0 copy-done
  32.1 0.0 copy-done.1
  32.1 0.0 copy-done.2
  32.1 0.7 %copy-done.3 = f32[4,8]{1,0:T(4,128)S(1)} copy-done((f32[4,8]{1,0:T(4,128)S(1)}, f32[4,8]{1,0:T(4,128)}, u32[]{:S(2)}) %copy-start.3) | copy-done | bytes 152
  32.7 2.2 %fusion.6.src_ref = bf16[4,8,64,128]{3,2,1,0:T(8,128)(2,1)} fusion(f32[4,8,64,128]{3,2,1,0:T(8,128)S(1)} %copy-done.2, f32[1,8,64,128]{3,2,1,0:T(8,128)S(1)} %collective-permute-done, f32[3,8,64,128]{3,2,1,0:T(8,128)S(1)} %get-tuple-element.12, f32[3,8,64,128]{3,2,1,0:T(8,128)S(1)} %get-tuple-element.11, f32[1,8,64,128]{3,2,1,0:T(8,128)S(1)} %collective-permute-done.1, ...), kind=kOutput, calls=%fused_computation.8 | convolution fusion | flops 204472320 | bytes 6832384 | tf_op jit(solution)/shard_map/kl,xylr->xykr/dot_general | solution.py:88
  35.0 4.3 %shard_map.74 = f32[4,8,64,128]{3,2,1,0:T(8,128)} custom-call(s32[8]{0:T(128)} %bitcast.18, s32[1]{0:T(128)} %bitcast.14.count_ref, bf16[4,8,64,128]{3,2,1,0:T(8,128)(2,1)} %fusion.6.src_ref, bf16[8,256,256]{2,1,0:T(8,128)(2,1)} %bitcast.16, f32[4,8,64,128]{3,2,1,0:T(8,128)} %shard_map.73.rest_0_), custom_call_target="tpu_custom_call" | custom-call | tf_op jit(solution)/shard_map/pallas_call | solution.py:56
  (2 shorter events, 0.1 us)
Async XLA Ops:
  0.0 32.1 %copy-start = (f32[64,64]{1,0:T(8,128)S(1)}, f32[64,64]{1,0:T(8,128)}, u32[]{:S(2)}) copy-start(f32[64,64]{1,0:T(8,128)} %param.10) | copy-start | bytes 49156
  6.9 17.7 %collective-permute-start.3 = (f32[4,1,64,128]{3,2,1,0:T(8,128)S(1)}, f32[4,1,64,128]{3,2,1,0:T(8,128)S(1)}, u32[]{:S(2)}, u32[]{:S(2)}) collective-permute-start(f32[4,1,64,128]{3,2,1,0:T(8,128)S(1)} %get-tuple-element.5), channel_id=1, source_target_pairs={{0,1},{1,2},{2,3},{3,4},{4,5},{5,6},{6,7},{7,8},{8,9},{9,10},{10,1... | collective-permute-start | bytes 393224 | tf_op jit(solution)/shard_map/ppermute | solution.py:71
  8.8 15.8 %collective-permute-start.2 = (f32[4,1,64,128]{3,2,1,0:T(8,128)S(1)}, f32[4,1,64,128]{3,2,1,0:T(8,128)S(1)}, u32[]{:S(2)}, u32[]{:S(2)}) collective-permute-start(f32[4,1,64,128]{3,2,1,0:T(8,128)S(1)} %get-tuple-element.6), channel_id=1, source_target_pairs={{1,0},{2,1},{3,2},{4,3},{5,4},{6,5},{7,6},{8,7},{9,8},{10,9},{11,1... | collective-permute-start | bytes 393224 | tf_op jit(solution)/shard_map/ppermute | solution.py:71
  14.3 13.1 %collective-permute-start.1 = (f32[1,8,64,128]{3,2,1,0:T(8,128)S(1)}, f32[1,8,64,128]{3,2,1,0:T(8,128)S(1)}, u32[]{:S(2)}, u32[]{:S(2)}) collective-permute-start(f32[1,8,64,128]{3,2,1,0:T(8,128)S(1)} %get-tuple-element.9), channel_id=1, source_target_pairs={{0,32},{32,64},{64,96},{96,128},{128,160},{160,192},{192,224},{224... | collective-permute-start | bytes 786440 | tf_op jit(solution)/shard_map/ppermute | solution.py:71
  22.3 9.8 %collective-permute-start = (f32[1,8,64,128]{3,2,1,0:T(8,128)S(1)}, f32[1,8,64,128]{3,2,1,0:T(8,128)S(1)}, u32[]{:S(2)}, u32[]{:S(2)}) collective-permute-start(f32[1,8,64,128]{3,2,1,0:T(8,128)S(1)} %get-tuple-element.10), channel_id=1, source_target_pairs={{32,0},{64,32},{96,64},{128,96},{160,128},{192,160},{224,192},{256... | collective-permute-start | bytes 786440 | tf_op jit(solution)/shard_map/ppermute | solution.py:71
  24.4 7.7 %copy-start.1 = (f32[4,8,64,128]{3,2,1,0:T(8,128)S(1)}, f32[4,8,64,128]{3,2,1,0:T(8,128)}, u32[]{:S(2)}) copy-start(f32[4,8,64,128]{3,2,1,0:T(8,128)} %shard_map.73.rest_0_) | copy-start | bytes 3145732
  24.4 7.7 %copy-start.2 = (f32[4,8,64,128]{3,2,1,0:T(8,128)S(1)}, f32[4,8,64,128]{3,2,1,0:T(8,128)}, u32[]{:S(2)}) copy-start(f32[4,8,64,128]{3,2,1,0:T(8,128)} %src_ref.1) | copy-start | bytes 3145732
  32.1 0.7 %copy-start.3 = (f32[4,8]{1,0:T(4,128)S(1)}, f32[4,8]{1,0:T(4,128)}, u32[]{:S(2)}) copy-start(f32[4,8]{1,0:T(4,128)} %param.8) | copy-start | bytes 388

commit v2 on v1

v2 whole, which is shorter than its diff:
```python
import jax
import jax.numpy as jnp
from jax import lax
from jax.experimental import pallas as pl
from jax.experimental.pallas import tpu as pltpu
from jax.sharding import PartitionSpec as P

SWEEPS = 2


damping = 0.5


def deposit_patches(anchor_ref, count_ref, src_ref, inv_ref, acc_ref):
    rows, columns, depth, loads = src_ref.shape
    slots = inv_ref.shape[0]
    count = count_ref[0]
    acc_ref[...] = jnp.zeros(acc_ref.shape, jnp.float32)
    for number in range(slots):

        @pl.when(number < count)
        def _():
            anchor = anchor_ref[number]
            row = anchor // (columns - 1)
            column = anchor % (columns - 1)
            pieces = [
                src_ref[row + i, column + j].astype(jnp.bfloat16)
                for i in range(2)
                for j in range(2)
            ]
            piece = jnp.concatenate(pieces, axis=0)
            term = damping * jnp.dot(
                inv_ref[number], piece, preferred_element_type=jnp.float32
            )
            for k in range(4):
                i, j = divmod(k, 2)
                acc_ref[row + i, column + j] += term[k * depth : (k + 1) * depth]


def first_sweep_kernel(
    anchor_ref, count_ref, weight_ref, src_ref, inv_ref,
    out_ref, top_ref, bottom_ref, left_ref, right_ref, acc_ref,
):
    rows, columns = src_ref.shape[:2]
    deposit_patches(anchor_ref, count_ref, src_ref, inv_ref, acc_ref)
    out_ref[...] = acc_ref[...]
    for y in range(columns):
        top_ref[0, y] = weight_ref[0, y] * acc_ref[0, y]
        bottom_ref[0, y] = weight_ref[rows - 1, y] * acc_ref[rows - 1, y]
    for x in range(rows):
        left_ref[x, 0] = weight_ref[x, 0] * acc_ref[x, 0]
        right_ref[x, 0] = weight_ref[x, columns - 1] * acc_ref[x, columns - 1]


def later_sweep_kernel(
    anchor_ref, count_ref, weight_ref, pre_ref, field_ref, above_ref, below_ref,
    left_ref, right_ref, inv_ref, out_ref, packed_ref, acc_ref,
):
    rows, columns = field_ref.shape[:2]

    def weighted(x, y):
        return weight_ref[x, y] * field_ref[x, y]

    for x in range(rows):
        for y in range(columns):
            next_x = weighted(x + 1, y) if x + 1 < rows else below_ref[0, y]
            prev_x = weighted(x - 1, y) if x > 0 else above_ref[0, y]
            next_y = weighted(x, y + 1) if y + 1 < columns else right_ref[x, 0]
            prev_y = weighted(x, y - 1) if y > 0 else left_ref[x, 0]
            beside = next_x + prev_x + next_y + prev_y
            packed_ref[x, y] = (pre_ref[x, y] + weight_ref[x, y] * beside).astype(
                jnp.bfloat16
            )
    deposit_patches(anchor_ref, count_ref, packed_ref, inv_ref, acc_ref)
    out_ref[...] = field_ref[...] + acc_ref[...]


SMEM = pl.BlockSpec(memory_space=pltpu.SMEM)
VMEM = pl.BlockSpec(memory_space=pltpu.VMEM)


def first_sweep(src, inverse, anchors, count, weight):
    rows, columns, depth, loads = src.shape
    row_edge = jax.ShapeDtypeStruct((1, columns, depth, loads), jnp.float32)
    column_edge = jax.ShapeDtypeStruct((rows, 1, depth, loads), jnp.float32)
    return pl.pallas_call(
        first_sweep_kernel,
        out_shape=(
            jax.ShapeDtypeStruct(src.shape, jnp.float32),
            row_edge, row_edge, column_edge, column_edge,
        ),
        in_specs=[SMEM, SMEM, SMEM, VMEM, VMEM],
        out_specs=(VMEM,) * 5,
        scratch_shapes=[pltpu.VMEM(src.shape, jnp.float32)],
    )(anchors, count.reshape(1), weight, src, inverse)


def later_sweep(pre, field, halos, inverse, anchors, count, weight):
    return pl.pallas_call(
        later_sweep_kernel,
        out_shape=jax.ShapeDtypeStruct(field.shape, jnp.float32),
        in_specs=[SMEM, SMEM, SMEM] + [VMEM] * 7,
        out_specs=VMEM,
        scratch_shapes=[
            pltpu.VMEM(field.shape, jnp.bfloat16),
            pltpu.VMEM(field.shape, jnp.float32),
        ],
    )(anchors, count.reshape(1), weight, pre, field, *halos, inverse)


def shifted_in(edge, axis, forward):
    count = lax.axis_size(axis)
    if forward:
        pairs = [(i, i + 1) for i in range(count - 1)]
    else:
        pairs = [(i + 1, i) for i in range(count - 1)]
    return lax.ppermute(edge, axis, pairs)


def per_device(
    load_field, stiffness, fault_mask, column_operator, patch_inverse, patch_anchor, patch_count
):
    weight = 1.0 - 0.6 * fault_mask.astype(jnp.float32)
    inverse = patch_inverse[0, 0]
    anchors = patch_anchor[0, 0]
    count = patch_count[0, 0]

    field, top, bottom, left, right = first_sweep(load_field, inverse, anchors, count, weight)
    if SWEEPS == 2:
        halos = (
            shifted_in(bottom, "gx", True),
            shifted_in(top, "gx", False),
            shifted_in(right, "gy", True),
            shifted_in(left, "gy", False),
        )
        local = jnp.einsum(
            "kl,xylr->xykr", column_operator, field, precision=lax.Precision.HIGHEST
        )
        pre = load_field - stiffness[:, :, None, None] * local
        field = later_sweep(pre, field, halos, inverse, anchors, count, weight)
    return field


def solution(mesh):
    return jax.shard_map(
        per_device,
        mesh=mesh,
        in_specs=(
            P("gx", "gy", None, None),
            P("gx", "gy"),
            P("gx", "gy"),
            P(),
            P("gx", "gy", None, None, None),
            P("gx", "gy", None),
            P("gx", "gy"),
        ),
        out_specs=P("gx", "gy", None, None),
        check_vma=False,
    )
```

time: 39.7 us -> 37.7 us (0.950)
  the two profiles are of different devices: /device:TPU:475 before, /device:TPU:405 now
where the time goes in v2:
time: 37.7 us; the launch traced here: 37.4 us
  starting transfers between devices  17.2 us (46%)
  Pallas kernels  9.43 us (25%)
  waiting for transfers between devices  4.72 us (13%)
  matrix products  3.31 us (9%)
  other arithmetic  1.26 us (3%)
  between operations  0.75 us (2%)
  local copies, waits for them, and re-layouts  0.71 us (2%)
    ppermute x4, starting transfers between devices, shifted_in(): return lax.ppermute(edge, axis, pairs)  17.2 us
    pallas_call x1, Pallas kernels, later_sweep(): pl.pallas_call(later_sweep_kernel, out_shape=jax.ShapeDtypeStruct(field.s...  5.01 us
    ppermute x4, waiting for transfers between devices, shifted_in(): return lax.ppermute(edge, axis, pairs)  4.72 us
    pallas_call x1, Pallas kernels, first_sweep(): pl.pallas_call(first_sweep_kernel, out_shape=(jax.ShapeDtypeStruct(src.sh...  4.43 us
    dot_general x1, matrix products, per_device(): jnp.einsum('kl,xylr->xykr', column_operator, field, precision=lax.Precisi...  3.31 us
    sub x1, other arithmetic, per_device(): weight = 1.0 - 0.6 * fault_mask.astype(jnp.float32)  1.26 us
  transfers between devices with their start and end apart: 4, of which 2 were waited for; matrix products, arithmetic and copies ran while one was open for 9% of the time, Pallas kernels for 0%

profile of v2, /device:TPU:405, one launch (start us, length us, event | category | flops | bytes accessed | tf_op | source)
XLA Modules:
  0.0 37.4 jit_solution(379375706884879309)
XLA Ops:
  0.0 0.0 copy-start
  0.7 1.3 %multiply_subtract_fusion.weight_ref = f32[4,8]{1,0:T(4,128)} fusion(s32[4,8]{1,0:T(4,128)} %param.9), kind=kLoop, calls=%fused_computation.4 | loop fusion | flops 96 | bytes 256 | tf_op jit(solution)/shard_map/sub | solution.py:123
  1.9 0.0 copy-start.1
  1.9 4.4 %shard_map.73 = (f32[4,8,64,128]{3,2,1,0:T(8,128)}, f32[1,8,64,128]{3,2,1,0:T(8,128)}, f32[1,8,64,128]{3,2,1,0:T(8,128)}, f32[4,1,64,128]{3,2,1,0:T(8,128)}, f32[4,1,64,128]{3,2,1,0:T(8,128)}) custom-call(s32[8]{0:T(128)} %bitcast.17, s32[1]{0:T(128)} %bitcast.13.count_ref, f32[4,8]{1,0:T(4,128)} %multiply_subtract_fusion.weight_ref, ...), custom_call_target="tpu_custom_call" | custom-call | tf_op jit(solution)/shard_map/pallas_call | solution.py:86
  6.4 3.4 %collective-permute-start.2 = (f32[4,1,64,128]{3,2,1,0:T(8,128)}, f32[4,1,64,128]{3,2,1,0:T(8,128)S(1)}, u32[]{:S(2)}, u32[]{:S(2)}) collective-permute-start(f32[4,1,64,128]{3,2,1,0:T(8,128)} %get-tuple-element.13), channel_id=1, source_target_pairs={{0,1},{1,2},{2,3},{3,4},{4,5},{5,6},{6,7},{7,8},{8,9},{9,10},{10,1... | collective-permute-start | bytes 393224 | tf_op jit(solution)/shard_map/ppermute | solution.py:117
  9.7 4.9 %collective-permute-start.3 = (f32[4,1,64,128]{3,2,1,0:T(8,128)}, f32[4,1,64,128]{3,2,1,0:T(8,128)S(1)}, u32[]{:S(2)}, u32[]{:S(2)}) collective-permute-start(f32[4,1,64,128]{3,2,1,0:T(8,128)} %get-tuple-element.14), channel_id=1, source_target_pairs={{1,0},{2,1},{3,2},{4,3},{5,4},{6,5},{7,6},{8,7},{9,8},{10,9},{11,1... | collective-permute-start | bytes 393224 | tf_op jit(solution)/shard_map/ppermute | solution.py:117
  14.6 0.0 copy-start.6
  14.7 7.0 %collective-permute-start = (f32[1,8,64,128]{3,2,1,0:T(8,128)}, f32[1,8,64,128]{3,2,1,0:T(8,128)S(1)}, u32[]{:S(2)}, u32[]{:S(2)}) collective-permute-start(f32[1,8,64,128]{3,2,1,0:T(8,128)} %get-tuple-element.11), channel_id=1, source_target_pairs={{0,32},{32,64},{64,96},{96,128},{128,160},{160,192},{192,224},{224... | collective-permute-start | bytes 786440 | tf_op jit(solution)/shard_map/ppermute | solution.py:117
  21.7 1.9 %collective-permute-start.1 = (f32[1,8,64,128]{3,2,1,0:T(8,128)}, f32[1,8,64,128]{3,2,1,0:T(8,128)S(1)}, u32[]{:S(2)}, u32[]{:S(2)}) collective-permute-start(f32[1,8,64,128]{3,2,1,0:T(8,128)} %get-tuple-element.12), channel_id=1, source_target_pairs={{32,0},{64,32},{96,64},{128,96},{160,128},{192,160},{224,192},{256... | collective-permute-start | bytes 786440 | tf_op jit(solution)/shard_map/ppermute | solution.py:117
  23.6 0.0 copy-done
  23.6 0.0 copy-done.1
  23.6 0.0 copy-done.6
  23.6 3.3 %fusion.1.pre_ref = f32[4,8,64,128]{3,2,1,0:T(8,128)} fusion(f32[4,8,64,128]{3,2,1,0:T(8,128)S(1)} %copy-done.1, f32[4,8,64,128]{3,2,1,0:T(8,128)} %get-tuple-element.10.field_ref, f32[4,8]{1,0:T(4,128)S(1)} %copy-done.6, f32[64,64]{1,0:T(8,128)S(1)} %copy-done), kind=kOutput, calls=%fused_computation.2 | convolution fusion | flops 201850880 | bytes 3162240 | tf_op jit(solution)/shard_map/kl,xylr->xykr/dot_general | solution.py:136
  26.9 0.0 collective-permute-done.2.left_ref
  27.0 0.0 copy-start.4
  27.0 0.0 collective-permute-done.3.right_ref
  27.0 0.0 copy-start.5
  27.0 1.1 %collective-permute-done.above_ref = f32[1,8,64,128]{3,2,1,0:T(8,128)S(1)} collective-permute-done((f32[1,8,64,128]{3,2,1,0:T(8,128)}, f32[1,8,64,128]{3,2,1,0:T(8,128)S(1)}, u32[]{:S(2)}, u32[]{:S(2)}) %collective-permute-start) | collective-permute-done | bytes 262176 | tf_op jit(solution)/shard_map/ppermute | solution.py:117
  28.1 0.0 copy-start.2
  28.1 3.6 %collective-permute-done.1.below_ref = f32[1,8,64,128]{3,2,1,0:T(8,128)S(1)} collective-permute-done((f32[1,8,64,128]{3,2,1,0:T(8,128)}, f32[1,8,64,128]{3,2,1,0:T(8,128)S(1)}, u32[]{:S(2)}, u32[]{:S(2)}) %collective-permute-start.1) | collective-permute-done | bytes 262176 | tf_op jit(solution)/shard_map/ppermute | solution.py:117
  31.7 0.0 copy-start.3
  31.7 0.0 copy-done.4
  31.7 0.0 copy-done.5
  31.7 0.0 copy-done.2
  31.7 0.7 %copy-done.3 = f32[1,8,64,128]{3,2,1,0:T(8,128)} copy-done((f32[1,8,64,128]{3,2,1,0:T(8,128)}, f32[1,8,64,128]{3,2,1,0:T(8,128)S(1)}, u32[]{:S(2)}) %copy-start.3) | copy-done | bytes 262168
  32.4 5.0 %shard_map.74 = f32[4,8,64,128]{3,2,1,0:T(8,128)} custom-call(s32[8]{0:T(128)} %bitcast.18, s32[1]{0:T(128)} %bitcast.14.count_ref, f32[4,8]{1,0:T(4,128)} %multiply_subtract_fusion.weight_ref, f32[4,8,64,128]{3,2,1,0:T(8,128)} %fusion.1.pre_ref, f32[4,8,64,128]{3,2,1,0:T(8,128)} %get-tuple-element.10.field_ref, f32[1,8,64,128]{3,2,1,0:T(8,128)} %copy-done.2, ...), custom_call_target="tpu_custom_call" | custom-call | tf_op jit(solution)/shard_map/pallas_call | solution.py:99
Async XLA Ops:
  0.0 23.6 %copy-start = (f32[64,64]{1,0:T(8,128)S(1)}, f32[64,64]{1,0:T(8,128)}, u32[]{:S(2)}) copy-start(f32[64,64]{1,0:T(8,128)} %param.10) | copy-start | bytes 49156
  1.9 21.7 %copy-start.1 = (f32[4,8,64,128]{3,2,1,0:T(8,128)S(1)}, f32[4,8,64,128]{3,2,1,0:T(8,128)}, u32[]{:S(2)}) copy-start(f32[4,8,64,128]{3,2,1,0:T(8,128)} %src_ref.1) | copy-start | bytes 3145732
  6.4 20.6 %collective-permute-start.2 = (f32[4,1,64,128]{3,2,1,0:T(8,128)}, f32[4,1,64,128]{3,2,1,0:T(8,128)S(1)}, u32[]{:S(2)}, u32[]{:S(2)}) collective-permute-start(f32[4,1,64,128]{3,2,1,0:T(8,128)} %get-tuple-element.13), channel_id=1, source_target_pairs={{0,1},{1,2},{2,3},{3,4},{4,5},{5,6},{6,7},{7,8},{8,9},{9,10},{10,1... | collective-permute-start | bytes 393224 | tf_op jit(solution)/shard_map/ppermute | solution.py:117
  9.7 17.2 %collective-permute-start.3 = (f32[4,1,64,128]{3,2,1,0:T(8,128)}, f32[4,1,64,128]{3,2,1,0:T(8,128)S(1)}, u32[]{:S(2)}, u32[]{:S(2)}) collective-permute-start(f32[4,1,64,128]{3,2,1,0:T(8,128)} %get-tuple-element.14), channel_id=1, source_target_pairs={{1,0},{2,1},{3,2},{4,3},{5,4},{6,5},{7,6},{8,7},{9,8},{10,9},{11,1... | collective-permute-start | bytes 393224 | tf_op jit(solution)/shard_map/ppermute | solution.py:117
  14.6 9.0 %copy-start.6 = (f32[4,8]{1,0:T(4,128)S(1)}, f32[4,8]{1,0:T(4,128)}, u32[]{:S(2)}) copy-start(f32[4,8]{1,0:T(4,128)} %param.8) | copy-start | bytes 388
  14.7 13.4 %collective-permute-start = (f32[1,8,64,128]{3,2,1,0:T(8,128)}, f32[1,8,64,128]{3,2,1,0:T(8,128)S(1)}, u32[]{:S(2)}, u32[]{:S(2)}) collective-permute-start(f32[1,8,64,128]{3,2,1,0:T(8,128)} %get-tuple-element.11), channel_id=1, source_target_pairs={{0,32},{32,64},{64,96},{96,128},{128,160},{160,192},{192,224},{224... | collective-permute-start | bytes 786440 | tf_op jit(solution)/shard_map/ppermute | solution.py:117
  21.7 10.0 %collective-permute-start.1 = (f32[1,8,64,128]{3,2,1,0:T(8,128)}, f32[1,8,64,128]{3,2,1,0:T(8,128)S(1)}, u32[]{:S(2)}, u32[]{:S(2)}) collective-permute-start(f32[1,8,64,128]{3,2,1,0:T(8,128)} %get-tuple-element.12), channel_id=1, source_target_pairs={{32,0},{64,32},{96,64},{128,96},{160,128},{192,160},{224,192},{256... | collective-permute-start | bytes 786440 | tf_op jit(solution)/shard_map/ppermute | solution.py:117
  27.0 4.7 %copy-start.4 = (f32[4,1,64,128]{3,2,1,0:T(8,128)}, f32[4,1,64,128]{3,2,1,0:T(8,128)S(1)}, u32[]{:S(2)}) copy-start(f32[4,1,64,128]{3,2,1,0:T(8,128)S(1)} %collective-permute-done.2.left_ref) | copy-start | bytes 393220
  27.0 4.7 %copy-start.5 = (f32[4,1,64,128]{3,2,1,0:T(8,128)}, f32[4,1,64,128]{3,2,1,0:T(8,128)S(1)}, u32[]{:S(2)}) copy-start(f32[4,1,64,128]{3,2,1,0:T(8,128)S(1)} %collective-permute-done.3.right_ref) | copy-start | bytes 393220
  28.1 3.6 %copy-start.2 = (f32[1,8,64,128]{3,2,1,0:T(8,128)}, f32[1,8,64,128]{3,2,1,0:T(8,128)S(1)}, u32[]{:S(2)}) copy-start(f32[1,8,64,128]{3,2,1,0:T(8,128)S(1)} %collective-permute-done.above_ref) | copy-start | bytes 786436
  31.7 0.7 %copy-start.3 = (f32[1,8,64,128]{3,2,1,0:T(8,128)}, f32[1,8,64,128]{3,2,1,0:T(8,128)S(1)}, u32[]{:S(2)}) copy-start(f32[1,8,64,128]{3,2,1,0:T(8,128)S(1)} %collective-permute-done.1.below_ref) | copy-start | bytes 786436

commit v3 on v2

v3 whole, which is shorter than its diff:
```python
import jax
import jax.numpy as jnp
from jax import lax
from jax.experimental import pallas as pl
from jax.experimental.pallas import tpu as pltpu
from jax.sharding import PartitionSpec as P

SWEEPS = 2


damping = 0.5


def weight_of(mask_ref, x, y):
    return 1.0 - 0.6 * mask_ref[x, y].astype(jnp.float32)


def slot_copies(inv_hbm, inv_ref, sems, count):
    copies = [
        pltpu.make_async_copy(inv_hbm.at[number], inv_ref.at[number], sems.at[number])
        for number in range(inv_ref.shape[0])
    ]
    for number, copy in enumerate(copies):

        @pl.when(number < count)
        def _():
            copy.start()

    return copies


def deposit_patches(anchor_ref, count, src_ref, inv_ref, copies, acc_ref):
    rows, columns, depth, loads = src_ref.shape
    acc_ref[...] = jnp.zeros(acc_ref.shape, jnp.float32)
    for number, copy in enumerate(copies):

        @pl.when(number < count)
        def _():
            anchor = anchor_ref[number]
            row = anchor // (columns - 1)
            column = anchor % (columns - 1)
            pieces = [
                src_ref[row + i, column + j].astype(jnp.bfloat16)
                for i in range(2)
                for j in range(2)
            ]
            piece = jnp.concatenate(pieces, axis=0)
            copy.wait()
            term = damping * jnp.dot(
                inv_ref[number], piece, preferred_element_type=jnp.float32
            )
            for k in range(4):
                i, j = divmod(k, 2)
                acc_ref[row + i, column + j] += term[k * depth : (k + 1) * depth]


def first_sweep_kernel(
    anchor_ref, count_ref, mask_ref, src_ref, inv_hbm,
    out_ref, top_ref, bottom_ref, left_ref, right_ref, inv_ref, sems, acc_ref,
):
    rows, columns = src_ref.shape[:2]
    count = count_ref[0]
    copies = slot_copies(inv_hbm, inv_ref, sems, count)
    deposit_patches(anchor_ref, count, src_ref, inv_ref, copies, acc_ref)
    out_ref[...] = acc_ref[...]
    for y in range(columns):
        top_ref[0, y] = weight_of(mask_ref, 0, y) * acc_ref[0, y]
        bottom_ref[0, y] = weight_of(mask_ref, rows - 1, y) * acc_ref[rows - 1, y]
    for x in range(rows):
        left_ref[x, 0] = weight_of(mask_ref, x, 0) * acc_ref[x, 0]
        right_ref[x, 0] = weight_of(mask_ref, x, columns - 1) * acc_ref[x, columns - 1]


def later_sweep_kernel(
    anchor_ref, count_ref, mask_ref, pre_ref, field_ref, above_hbm, below_hbm,
    left_hbm, right_hbm, inv_hbm, out_ref, above_ref, below_ref, left_ref, right_ref,
    inv_ref, halo_sems, sems, packed_ref, acc_ref,
):
    rows, columns = field_ref.shape[:2]
    count = count_ref[0]
    copies = slot_copies(inv_hbm, inv_ref, sems, count)
    halo_copies = [
        pltpu.make_async_copy(source, target, halo_sems.at[number])
        for number, (source, target) in enumerate(
            [
                (above_hbm, above_ref),
                (below_hbm, below_ref),
                (left_hbm, left_ref),
                (right_hbm, right_ref),
            ]
        )
    ]
    for copy in halo_copies:
        copy.start()

    def weighted(x, y):
        return weight_of(mask_ref, x, y) * field_ref[x, y]

    def residual(x, y):
        next_x = weighted(x + 1, y) if x + 1 < rows else below_ref[0, y]
        prev_x = weighted(x - 1, y) if x > 0 else above_ref[0, y]
        next_y = weighted(x, y + 1) if y + 1 < columns else right_ref[x, 0]
        prev_y = weighted(x, y - 1) if y > 0 else left_ref[x, 0]
        beside = next_x + prev_x + next_y + prev_y
        packed_ref[x, y] = (pre_ref[x, y] + weight_of(mask_ref, x, y) * beside).astype(
            jnp.bfloat16
        )

    vertices = [(x, y) for x in range(rows) for y in range(columns)]
    inner = [(x, y) for x, y in vertices if 0 < x < rows - 1 and 0 < y < columns - 1]
    for x, y in inner:
        residual(x, y)
    for copy in halo_copies:
        copy.wait()
    for x, y in vertices:
        if (x, y) not in inner:
            residual(x, y)
    deposit_patches(anchor_ref, count, packed_ref, inv_ref, copies, acc_ref)
    out_ref[...] = field_ref[...] + acc_ref[...]


SMEM = pl.BlockSpec(memory_space=pltpu.SMEM)
VMEM = pl.BlockSpec(memory_space=pltpu.VMEM)
ANY = pl.BlockSpec(memory_space=pl.ANY)


def first_sweep(src, inverse, anchors, count, mask):
    rows, columns, depth, loads = src.shape
    row_edge = jax.ShapeDtypeStruct((1, columns, depth, loads), jnp.float32)
    column_edge = jax.ShapeDtypeStruct((rows, 1, depth, loads), jnp.float32)
    return pl.pallas_call(
        first_sweep_kernel,
        out_shape=(
            jax.ShapeDtypeStruct(src.shape, jnp.float32),
            row_edge, row_edge, column_edge, column_edge,
        ),
        in_specs=[SMEM, SMEM, SMEM, VMEM, ANY],
        out_specs=(VMEM,) * 5,
        scratch_shapes=[
            pltpu.VMEM(inverse.shape, inverse.dtype),
            pltpu.SemaphoreType.DMA((inverse.shape[0],)),
            pltpu.VMEM(src.shape, jnp.float32),
        ],
    )(anchors, count.reshape(1), mask, src, inverse)


def later_sweep(pre, field, halos, inverse, anchors, count, mask):
    return pl.pallas_call(
        later_sweep_kernel,
        out_shape=jax.ShapeDtypeStruct(field.shape, jnp.float32),
        in_specs=[SMEM, SMEM, SMEM, VMEM, VMEM] + [ANY] * 5,
        out_specs=VMEM,
        scratch_shapes=[pltpu.VMEM(h.shape, h.dtype) for h in halos]
        + [
            pltpu.VMEM(inverse.shape, inverse.dtype),
            pltpu.SemaphoreType.DMA((4,)),
            pltpu.SemaphoreType.DMA((inverse.shape[0],)),
            pltpu.VMEM(field.shape, jnp.bfloat16),
            pltpu.VMEM(field.shape, jnp.float32),
        ],
    )(anchors, count.reshape(1), mask, pre, field, *halos, inverse)


def shifted_in(edge, axis, forward):
    count = lax.axis_size(axis)
    if forward:
        pairs = [(i, i + 1) for i in range(count - 1)]
    else:
        pairs = [(i + 1, i) for i in range(count - 1)]
    return lax.ppermute(edge, axis, pairs)


def per_device(
    load_field, stiffness, fault_mask, column_operator, patch_inverse, patch_anchor, patch_count
):
    inverse = patch_inverse[0, 0]
    anchors = patch_anchor[0, 0]
    count = patch_count[0, 0]

    field, top, bottom, left, right = first_sweep(load_field, inverse, anchors, count, fault_mask)
    if SWEEPS == 2:
        halos = (
            shifted_in(bottom, "gx", True),
            shifted_in(top, "gx", False),
            shifted_in(right, "gy", True),
            shifted_in(left, "gy", False),
        )
        local = jnp.einsum(
            "kl,xylr->xykr", column_operator, field, precision=lax.Precision.HIGHEST
        )
        pre = load_field - stiffness[:, :, None, None] * local
        field = later_sweep(pre, field, halos, inverse, anchors, count, fault_mask)
    return field


def solution(mesh):
    return jax.shard_map(
        per_device,
        mesh=mesh,
        in_specs=(
            P("gx", "gy", None, None),
            P("gx", "gy"),
            P("gx", "gy"),
            P(),
            P("gx", "gy", None, None, None),
            P("gx", "gy", None),
            P("gx", "gy"),
        ),
        out_specs=P("gx", "gy", None, None),
        check_vma=False,
    )
```

time: 37.7 us -> 38.1 us (1.011)
  the two profiles are of different devices: /device:TPU:405 before, /device:TPU:475 now
where the time goes in v3:
time: 38.1 us; the launch traced here: 37.7 us
  starting transfers between devices  17.2 us (45%)
  Pallas kernels  11 us (29%)
  waiting for transfers between devices  4.73 us (12%)
  matrix products  3.31 us (9%)
  between operations  0.76 us (2%)
  local copies, waits for them, and re-layouts  0.71 us (2%)
    ppermute x4, starting transfers between devices, shifted_in(): return lax.ppermute(edge, axis, pairs)  17.2 us
    pallas_call x1, Pallas kernels, later_sweep(): pl.pallas_call(later_sweep_kernel, out_shape=jax.ShapeDtypeStruct(field.s...  5.96 us
    pallas_call x1, Pallas kernels, first_sweep(): pl.pallas_call(first_sweep_kernel, out_shape=(jax.ShapeDtypeStruct(src.sh...  5.04 us
    ppermute x4, waiting for transfers between devices, shifted_in(): return lax.ppermute(edge, axis, pairs)  4.73 us
    dot_general x1, matrix products, per_device(): jnp.einsum('kl,xylr->xykr', column_operator, field, precision=lax.Precisi...  3.31 us
  transfers between devices with their start and end apart: 4, of which 2 were waited for; matrix products, arithmetic and copies ran while one was open for 9% of the time, Pallas kernels for 0%

profile of v3, /device:TPU:475, one launch (start us, length us, event | category | flops | bytes accessed | tf_op | source)
XLA Modules:
  0.0 37.7 jit_solution(12387866385702971389)
XLA Ops:
  0.0 0.0 copy-start
  0.7 0.0 copy-start.1
  0.7 5.0 %shard_map.73 = (f32[4,8,64,128]{3,2,1,0:T(8,128)}, f32[1,8,64,128]{3,2,1,0:T(8,128)}, f32[1,8,64,128]{3,2,1,0:T(8,128)}, f32[4,1,64,128]{3,2,1,0:T(8,128)}, f32[4,1,64,128]{3,2,1,0:T(8,128)}) custom-call(s32[8]{0:T(128)} %bitcast.17, s32[1]{0:T(128)} %bitcast.13.count_ref, s32[4,8]{1,0:T(4,128)} %mask_ref.3, f32[4,8,64,128]{3,2,1,0:T(8,128)} %src_ref.1, ...), custom_call_target="tpu_custom_call" | custom-call | tf_op jit(solution)/shard_map/pallas_call | solution.py:131
  5.7 1.9 %collective-permute-start.2 = (f32[4,1,64,128]{3,2,1,0:T(8,128)}, f32[4,1,64,128]{3,2,1,0:T(8,128)S(1)}, u32[]{:S(2)}, u32[]{:S(2)}) collective-permute-start(f32[4,1,64,128]{3,2,1,0:T(8,128)} %get-tuple-element.13), channel_id=1, source_target_pairs={{0,1},{1,2},{2,3},{3,4},{4,5},{5,6},{6,7},{7,8},{8,9},{9,10},{10,1... | collective-permute-start | bytes 393224 | tf_op jit(solution)/shard_map/ppermute | solution.py:170
  7.6 5.5 %collective-permute-start.3 = (f32[4,1,64,128]{3,2,1,0:T(8,128)}, f32[4,1,64,128]{3,2,1,0:T(8,128)S(1)}, u32[]{:S(2)}, u32[]{:S(2)}) collective-permute-start(f32[4,1,64,128]{3,2,1,0:T(8,128)} %get-tuple-element.14), channel_id=1, source_target_pairs={{1,0},{2,1},{3,2},{4,3},{5,4},{6,5},{7,6},{8,7},{9,8},{10,9},{11,1... | collective-permute-start | bytes 393224 | tf_op jit(solution)/shard_map/ppermute | solution.py:170
  13.1 0.0 copy-start.6
  13.1 7.9 %collective-permute-start = (f32[1,8,64,128]{3,2,1,0:T(8,128)}, f32[1,8,64,128]{3,2,1,0:T(8,128)S(1)}, u32[]{:S(2)}, u32[]{:S(2)}) collective-permute-start(f32[1,8,64,128]{3,2,1,0:T(8,128)} %get-tuple-element.11), channel_id=1, source_target_pairs={{0,32},{32,64},{64,96},{96,128},{128,160},{160,192},{192,224},{224... | collective-permute-start | bytes 786440 | tf_op jit(solution)/shard_map/ppermute | solution.py:170
  21.1 1.9 %collective-permute-start.1 = (f32[1,8,64,128]{3,2,1,0:T(8,128)}, f32[1,8,64,128]{3,2,1,0:T(8,128)S(1)}, u32[]{:S(2)}, u32[]{:S(2)}) collective-permute-start(f32[1,8,64,128]{3,2,1,0:T(8,128)} %get-tuple-element.12), channel_id=1, source_target_pairs={{32,0},{64,32},{96,64},{128,96},{160,128},{192,160},{224,192},{256... | collective-permute-start | bytes 786440 | tf_op jit(solution)/shard_map/ppermute | solution.py:170
  23.0 0.0 copy-done
  23.0 0.0 copy-done.1
  23.0 0.0 copy-done.6
  23.0 3.3 %fusion.1.pre_ref = f32[4,8,64,128]{3,2,1,0:T(8,128)} fusion(f32[4,8,64,128]{3,2,1,0:T(8,128)S(1)} %copy-done.1, f32[4,8,64,128]{3,2,1,0:T(8,128)} %get-tuple-element.10.field_ref, f32[4,8]{1,0:T(4,128)S(1)} %copy-done.6, f32[64,64]{1,0:T(8,128)S(1)} %copy-done), kind=kOutput, calls=%fused_computation.2 | convolution fusion | flops 201850880 | bytes 3162240 | tf_op jit(solution)/shard_map/kl,xylr->xykr/dot_general | solution.py:188
  26.3 0.0 collective-permute-done.2.left_hbm
  26.3 0.0 copy-start.4
  26.3 0.0 collective-permute-done.3.right_hbm
  26.3 0.0 copy-start.5
  26.3 0.2 collective-permute-done.above_hbm
  26.5 0.0 copy-start.2
  26.5 4.5 %collective-permute-done.1.below_hbm = f32[1,8,64,128]{3,2,1,0:T(8,128)S(1)} collective-permute-done((f32[1,8,64,128]{3,2,1,0:T(8,128)}, f32[1,8,64,128]{3,2,1,0:T(8,128)S(1)}, u32[]{:S(2)}, u32[]{:S(2)}) %collective-permute-start.1) | collective-permute-done | bytes 262176 | tf_op jit(solution)/shard_map/ppermute | solution.py:170
  31.1 0.0 copy-start.3
  31.1 0.0 copy-done.4
  31.1 0.0 copy-done.5
  31.1 0.0 copy-done.2
  31.1 0.7 %copy-done.3 = f32[1,8,64,128]{3,2,1,0:T(8,128)} copy-done((f32[1,8,64,128]{3,2,1,0:T(8,128)}, f32[1,8,64,128]{3,2,1,0:T(8,128)S(1)}, u32[]{:S(2)}) %copy-start.3) | copy-done | bytes 262168
  31.8 6.0 %shard_map.74 = f32[4,8,64,128]{3,2,1,0:T(8,128)} custom-call(s32[8]{0:T(128)} %bitcast.18, s32[1]{0:T(128)} %bitcast.14.count_ref, s32[4,8]{1,0:T(4,128)} %mask_ref.3, f32[4,8,64,128]{3,2,1,0:T(8,128)} %fusion.1.pre_ref, f32[4,8,64,128]{3,2,1,0:T(8,128)} %get-tuple-element.10.field_ref, f32[1,8,64,128]{3,2,1,0:T(8,128)} %copy-done.2, ...), custom_call_target="tpu_custom_call" | custom-call | tf_op jit(solution)/shard_map/pallas_call | solution.py:148
Async XLA Ops:
  0.0 23.0 %copy-start = (f32[64,64]{1,0:T(8,128)S(1)}, f32[64,64]{1,0:T(8,128)}, u32[]{:S(2)}) copy-start(f32[64,64]{1,0:T(8,128)} %param.10) | copy-start | bytes 49156
  0.7 22.3 %copy-start.1 = (f32[4,8,64,128]{3,2,1,0:T(8,128)S(1)}, f32[4,8,64,128]{3,2,1,0:T(8,128)}, u32[]{:S(2)}) copy-start(f32[4,8,64,128]{3,2,1,0:T(8,128)} %src_ref.1) | copy-start | bytes 3145732
  5.7 20.6 %collective-permute-start.2 = (f32[4,1,64,128]{3,2,1,0:T(8,128)}, f32[4,1,64,128]{3,2,1,0:T(8,128)S(1)}, u32[]{:S(2)}, u32[]{:S(2)}) collective-permute-start(f32[4,1,64,128]{3,2,1,0:T(8,128)} %get-tuple-element.13), channel_id=1, source_target_pairs={{0,1},{1,2},{2,3},{3,4},{4,5},{5,6},{6,7},{7,8},{8,9},{9,10},{10,1... | collective-permute-start | bytes 393224 | tf_op jit(solution)/shard_map/ppermute | solution.py:170
  7.6 18.7 %collective-permute-start.3 = (f32[4,1,64,128]{3,2,1,0:T(8,128)}, f32[4,1,64,128]{3,2,1,0:T(8,128)S(1)}, u32[]{:S(2)}, u32[]{:S(2)}) collective-permute-start(f32[4,1,64,128]{3,2,1,0:T(8,128)} %get-tuple-element.14), channel_id=1, source_target_pairs={{1,0},{2,1},{3,2},{4,3},{5,4},{6,5},{7,6},{8,7},{9,8},{10,9},{11,1... | collective-permute-start | bytes 393224 | tf_op jit(solution)/shard_map/ppermute | solution.py:170
  13.1 9.9 %copy-start.6 = (f32[4,8]{1,0:T(4,128)S(1)}, f32[4,8]{1,0:T(4,128)}, u32[]{:S(2)}) copy-start(f32[4,8]{1,0:T(4,128)} %param.8) | copy-start | bytes 388
  13.1 13.4 %collective-permute-start = (f32[1,8,64,128]{3,2,1,0:T(8,128)}, f32[1,8,64,128]{3,2,1,0:T(8,128)S(1)}, u32[]{:S(2)}, u32[]{:S(2)}) collective-permute-start(f32[1,8,64,128]{3,2,1,0:T(8,128)} %get-tuple-element.11), channel_id=1, source_target_pairs={{0,32},{32,64},{64,96},{96,128},{128,160},{160,192},{192,224},{224... | collective-permute-start | bytes 786440 | tf_op jit(solution)/shard_map/ppermute | solution.py:170
  21.1 10.0 %collective-permute-start.1 = (f32[1,8,64,128]{3,2,1,0:T(8,128)}, f32[1,8,64,128]{3,2,1,0:T(8,128)S(1)}, u32[]{:S(2)}, u32[]{:S(2)}) collective-permute-start(f32[1,8,64,128]{3,2,1,0:T(8,128)} %get-tuple-element.12), channel_id=1, source_target_pairs={{32,0},{64,32},{96,64},{128,96},{160,128},{192,160},{224,192},{256... | collective-permute-start | bytes 786440 | tf_op jit(solution)/shard_map/ppermute | solution.py:170
  26.3 4.7 %copy-start.4 = (f32[4,1,64,128]{3,2,1,0:T(8,128)}, f32[4,1,64,128]{3,2,1,0:T(8,128)S(1)}, u32[]{:S(2)}) copy-start(f32[4,1,64,128]{3,2,1,0:T(8,128)S(1)} %collective-permute-done.2.left_hbm) | copy-start | bytes 393220
  26.3 4.7 %copy-start.5 = (f32[4,1,64,128]{3,2,1,0:T(8,128)}, f32[4,1,64,128]{3,2,1,0:T(8,128)S(1)}, u32[]{:S(2)}) copy-start(f32[4,1,64,128]{3,2,1,0:T(8,128)S(1)} %collective-permute-done.3.right_hbm) | copy-start | bytes 393220
  26.5 4.5 %copy-start.2 = (f32[1,8,64,128]{3,2,1,0:T(8,128)}, f32[1,8,64,128]{3,2,1,0:T(8,128)S(1)}, u32[]{:S(2)}) copy-start(f32[1,8,64,128]{3,2,1,0:T(8,128)S(1)} %collective-permute-done.above_hbm) | copy-start | bytes 786436
  31.1 0.7 %copy-start.3 = (f32[1,8,64,128]{3,2,1,0:T(8,128)}, f32[1,8,64,128]{3,2,1,0:T(8,128)S(1)}, u32[]{:S(2)}) copy-start(f32[1,8,64,128]{3,2,1,0:T(8,128)S(1)} %collective-permute-done.1.below_hbm) | copy-start | bytes 786436

commit v4 on v2

--- a/solution.py
+++ b/solution.py
@@ -9,6 +9,10 @@
 
 
 damping = 0.5
+
+
+def weight_of(mask_ref, x, y):
+    return 1.0 - 0.6 * mask_ref[x, y].astype(jnp.float32)
 
 
 def deposit_patches(anchor_ref, count_ref, src_ref, inv_ref, acc_ref):
@@ -38,37 +42,37 @@
 
 
 def first_sweep_kernel(
-    anchor_ref, count_ref, weight_ref, src_ref, inv_ref,
+    anchor_ref, count_ref, mask_ref, src_ref, inv_ref,
     out_ref, top_ref, bottom_ref, left_ref, right_ref, acc_ref,
 ):
     rows, columns = src_ref.shape[:2]
     deposit_patches(anchor_ref, count_ref, src_ref, inv_ref, acc_ref)
     out_ref[...] = acc_ref[...]
     for y in range(columns):
-        top_ref[0, y] = weight_ref[0, y] * acc_ref[0, y]
-        bottom_ref[0, y] = weight_ref[rows - 1, y] * acc_ref[rows - 1, y]
+        top_ref[0, y] = (weight_of(mask_ref, 0, y) * acc_ref[0, y]).astype(top_ref.dtype)
+        bottom_ref[0, y] = (weight_of(mask_ref, rows - 1, y) * acc_ref[rows - 1, y]).astype(bottom_ref.dtype)
     for x in range(rows):
-        left_ref[x, 0] = weight_ref[x, 0] * acc_ref[x, 0]
-        right_ref[x, 0] = weight_ref[x, columns - 1] * acc_ref[x, columns - 1]
+        left_ref[x, 0] = (weight_of(mask_ref, x, 0) * acc_ref[x, 0]).astype(left_ref.dtype)
+        right_ref[x, 0] = (weight_of(mask_ref, x, columns - 1) * acc_ref[x, columns - 1]).astype(right_ref.dtype)
 
 
 def later_sweep_kernel(
-    anchor_ref, count_ref, weight_ref, pre_ref, field_ref, above_ref, below_ref,
+    anchor_ref, count_ref, mask_ref, pre_ref, field_ref, above_ref, below_ref,
     left_ref, right_ref, inv_ref, out_ref, packed_ref, acc_ref,
 ):
     rows, columns = field_ref.shape[:2]
 
     def weighted(x, y):
-        return weight_ref[x, y] * field_ref[x, y]
+        return weight_of(mask_ref, x, y) * field_ref[x, y]
 
     for x in range(rows):
         for y in range(columns):
-            next_x = weighted(x + 1, y) if x + 1 < rows else below_ref[0, y]
-            prev_x = weighted(x - 1, y) if x > 0 else above_ref[0, y]
-            next_y = weighted(x, y + 1) if y + 1 < columns else right_ref[x, 0]
-            prev_y = weighted(x, y - 1) if y > 0 else left_ref[x, 0]
+            next_x = weighted(x + 1, y) if x + 1 < rows else below_ref[0, y].astype(jnp.float32)
+            prev_x = weighted(x - 1, y) if x > 0 else above_ref[0, y].astype(jnp.float32)
+            next_y = weighted(x, y + 1) if y + 1 < columns else right_ref[x, 0].astype(jnp.float32)
+            prev_y = weighted(x, y - 1) if y > 0 else left_ref[x, 0].astype(jnp.float32)
             beside = next_x + prev_x + next_y + prev_y
-            packed_ref[x, y] = (pre_ref[x, y] + weight_ref[x, y] * beside).astype(
+            packed_ref[x, y] = (pre_ref[x, y] + weight_of(mask_ref, x, y) * beside).astype(
                 jnp.bfloat16
             )
     deposit_patches(anchor_ref, count_ref, packed_ref, inv_ref, acc_ref)
@@ -79,10 +83,10 @@
 VMEM = pl.BlockSpec(memory_space=pltpu.VMEM)
 
 
-def first_sweep(src, inverse, anchors, count, weight):
+def first_sweep(src, inverse, anchors, count, mask):
     rows, columns, depth, loads = src.shape
-    row_edge = jax.ShapeDtypeStruct((1, columns, depth, loads), jnp.float32)
-    column_edge = jax.ShapeDtypeStruct((rows, 1, depth, loads), jnp.float32)
+    row_edge = jax.ShapeDtypeStruct((1, columns, depth, loads), jnp.bfloat16)
+    column_edge = jax.ShapeDtypeStruct((rows, 1, depth, loads), jnp.bfloat16)
     return pl.pallas_call(
         first_sweep_kernel,
         out_shape=(
@@ -92,10 +96,10 @@
         in_specs=[SMEM, SMEM, SMEM, VMEM, VMEM],
         out_specs=(VMEM,) * 5,
         scratch_shapes=[pltpu.VMEM(src.shape, jnp.float32)],
-    )(anchors, count.reshape(1), weight, src, inverse)
+    )(anchors, count.reshape(1), mask, src, inverse)
 
 
-def later_sweep(pre, field, halos, inverse, anchors, count, weight):
+def later_sweep(pre, field, halos, inverse, anchors, count, mask):
     return pl.pallas_call(
         later_sweep_kernel,
         out_shape=jax.ShapeDtypeStruct(field.shape, jnp.float32),
@@ -105,7 +109,7 @@
             pltpu.VMEM(field.shape, jnp.bfloat16),
             pltpu.VMEM(field.shape, jnp.float32),
         ],
-    )(anchors, count.reshape(1), weight, pre, field, *halos, inverse)
+    )(anchors, count.reshape(1), mask, pre, field, *halos, inverse)
 
 
 def shifted_in(edge, axis, forward):
@@ -120,12 +124,11 @@
 def per_device(
     load_field, stiffness, fault_mask, column_operator, patch_inverse, patch_anchor, patch_count
 ):
-    weight = 1.0 - 0.6 * fault_mask.astype(jnp.float32)
     inverse = patch_inverse[0, 0]
     anchors = patch_anchor[0, 0]
     count = patch_count[0, 0]
 
-    field, top, bottom, left, right = first_sweep(load_field, inverse, anchors, count, weight)
+    field, top, bottom, left, right = first_sweep(load_field, inverse, anchors, count, fault_mask)
     if SWEEPS == 2:
         halos = (
             shifted_in(bottom, "gx", True),
@@ -137,7 +140,7 @@
             "kl,xylr->xykr", column_operator, field, precision=lax.Precision.HIGHEST
         )
         pre = load_field - stiffness[:, :, None, None] * local
-        field = later_sweep(pre, field, halos, inverse, anchors, count, weight)
+        field = later_sweep(pre, field, halos, inverse, anchors, count, fault_mask)
     return field
 
 

time: 37.7 us -> 34.8 us (0.923)
  the two profiles are of different devices: /device:TPU:405 before, /device:TPU:467 now
where the time goes in v4:
time: 34.8 us; the launch traced here: 34.5 us
  starting transfers between devices  17.2 us (49%)
  Pallas kernels  9.21 us (26%)
  matrix products  3.32 us (10%)
  waiting for transfers between devices  3.3 us (9%)
  between operations  0.77 us (2%)
  local copies, waits for them, and re-layouts  0.66 us (2%)
    ppermute x4, starting transfers between devices, shifted_in(): return lax.ppermute(edge, axis, pairs)  17.2 us
    pallas_call x1, Pallas kernels, later_sweep(): pl.pallas_call(later_sweep_kernel, out_shape=jax.ShapeDtypeStruct(field.s...  4.91 us
    pallas_call x1, Pallas kernels, first_sweep(): pl.pallas_call(first_sweep_kernel, out_shape=(jax.ShapeDtypeStruct(src.sh...  4.3 us
    dot_general x1, matrix products, per_device(): jnp.einsum('kl,xylr->xykr', column_operator, field, precision=lax.Precisi...  3.32 us
    ppermute x4, waiting for transfers between devices, shifted_in(): return lax.ppermute(edge, axis, pairs)  3.3 us
  transfers between devices with their start and end apart: 4, of which 1 were waited for; matrix products, arithmetic and copies ran while one was open for 10% of the time, Pallas kernels for 0%

profile of v4, /device:TPU:467, one launch (start us, length us, event | category | flops | bytes accessed | tf_op | source)
XLA Modules:
  0.0 34.5 jit_solution(428300027957605810)
XLA Ops:
  0.0 0.0 copy-start
  0.7 0.0 copy-start.1
  0.7 4.3 %shard_map.73 = (f32[4,8,64,128]{3,2,1,0:T(8,128)}, bf16[1,8,64,128]{3,2,1,0:T(8,128)(2,1)}, bf16[1,8,64,128]{3,2,1,0:T(8,128)(2,1)}, bf16[4,1,64,128]{3,2,1,0:T(8,128)(2,1)}, bf16[4,1,64,128]{3,2,1,0:T(8,128)(2,1)}) custom-call(s32[8]{0:T(128)} %bitcast.17, s32[1]{0:T(128)} %bitcast.13.count_ref, s32[4,8]{1,0:T(4,128)} %mask_ref.3, ...), custom_call_target="tpu_custom_call" | custom-call | tf_op jit(solution)/shard_map/pallas_call | solution.py:90
  5.0 1.9 %collective-permute-start.2 = (bf16[4,1,64,128]{3,2,1,0:T(8,128)(2,1)}, bf16[4,1,64,128]{3,2,1,0:T(8,128)(2,1)S(1)}, u32[]{:S(2)}, u32[]{:S(2)}) collective-permute-start(bf16[4,1,64,128]{3,2,1,0:T(8,128)(2,1)} %get-tuple-element.13), channel_id=1, source_target_pairs={{0,1},{1,2},{2,3},{3,4},{4,5},{5,6},{6,7},{7,8},{8,9},{9,10},{10,1... | collective-permute-start | bytes 196616 | tf_op jit(solution)/shard_map/ppermute | solution.py:121
  6.9 5.5 %collective-permute-start.3 = (bf16[4,1,64,128]{3,2,1,0:T(8,128)(2,1)}, bf16[4,1,64,128]{3,2,1,0:T(8,128)(2,1)S(1)}, u32[]{:S(2)}, u32[]{:S(2)}) collective-permute-start(bf16[4,1,64,128]{3,2,1,0:T(8,128)(2,1)} %get-tuple-element.14), channel_id=1, source_target_pairs={{1,0},{2,1},{3,2},{4,3},{5,4},{6,5},{7,6},{8,7},{9,8},{10,9},{11,1... | collective-permute-start | bytes 196616 | tf_op jit(solution)/shard_map/ppermute | solution.py:121
  12.4 0.0 copy-start.6
  12.4 7.9 %collective-permute-start = (bf16[1,8,64,128]{3,2,1,0:T(8,128)(2,1)}, bf16[1,8,64,128]{3,2,1,0:T(8,128)(2,1)S(1)}, u32[]{:S(2)}, u32[]{:S(2)}) collective-permute-start(bf16[1,8,64,128]{3,2,1,0:T(8,128)(2,1)} %get-tuple-element.11), channel_id=1, source_target_pairs={{0,32},{32,64},{64,96},{96,128},{128,160},{160,192},{192,224},{224... | collective-permute-start | bytes 393224 | tf_op jit(solution)/shard_map/ppermute | solution.py:121
  20.3 1.9 %collective-permute-start.1 = (bf16[1,8,64,128]{3,2,1,0:T(8,128)(2,1)}, bf16[1,8,64,128]{3,2,1,0:T(8,128)(2,1)S(1)}, u32[]{:S(2)}, u32[]{:S(2)}) collective-permute-start(bf16[1,8,64,128]{3,2,1,0:T(8,128)(2,1)} %get-tuple-element.12), channel_id=1, source_target_pairs={{32,0},{64,32},{96,64},{128,96},{160,128},{192,160},{224,192},{256... | collective-permute-start | bytes 393224 | tf_op jit(solution)/shard_map/ppermute | solution.py:121
  22.2 0.0 copy-done
  22.2 0.0 copy-done.1
  22.2 0.0 copy-done.6
  22.3 3.3 %fusion.1.pre_ref = f32[4,8,64,128]{3,2,1,0:T(8,128)} fusion(f32[4,8,64,128]{3,2,1,0:T(8,128)S(1)} %copy-done.1, f32[4,8,64,128]{3,2,1,0:T(8,128)} %get-tuple-element.10.field_ref, f32[4,8]{1,0:T(4,128)S(1)} %copy-done.6, f32[64,64]{1,0:T(8,128)S(1)} %copy-done), kind=kOutput, calls=%fused_computation.2 | convolution fusion | flops 201850880 | bytes 3162240 | tf_op jit(solution)/shard_map/kl,xylr->xykr/dot_general | solution.py:139
  25.6 0.0 collective-permute-done.2.left_ref
  25.6 0.0 copy-start.4
  25.6 0.0 collective-permute-done.3.right_ref
  25.6 0.0 copy-start.5
  25.6 0.0 collective-permute-done.above_ref
  25.6 0.0 copy-start.2
  25.6 3.3 %collective-permute-done.1.below_ref = bf16[1,8,64,128]{3,2,1,0:T(8,128)(2,1)S(1)} collective-permute-done((bf16[1,8,64,128]{3,2,1,0:T(8,128)(2,1)}, bf16[1,8,64,128]{3,2,1,0:T(8,128)(2,1)S(1)}, u32[]{:S(2)}, u32[]{:S(2)}) %collective-permute-start.1) | collective-permute-done | bytes 131104 | tf_op jit(solution)/shard_map/ppermute | solution.py:121
  28.9 0.0 copy-start.3
  28.9 0.0 copy-done.4
  28.9 0.0 copy-done.5
  28.9 0.0 copy-done.2
  28.9 0.6 %copy-done.3 = bf16[1,8,64,128]{3,2,1,0:T(8,128)(2,1)} copy-done((bf16[1,8,64,128]{3,2,1,0:T(8,128)(2,1)}, bf16[1,8,64,128]{3,2,1,0:T(8,128)(2,1)S(1)}, u32[]{:S(2)}) %copy-start.3) | copy-done | bytes 131096
  29.6 4.9 %shard_map.74 = f32[4,8,64,128]{3,2,1,0:T(8,128)} custom-call(s32[8]{0:T(128)} %bitcast.18, s32[1]{0:T(128)} %bitcast.14.count_ref, s32[4,8]{1,0:T(4,128)} %mask_ref.3, f32[4,8,64,128]{3,2,1,0:T(8,128)} %fusion.1.pre_ref, f32[4,8,64,128]{3,2,1,0:T(8,128)} %get-tuple-element.10.field_ref, bf16[1,8,64,128]{3,2,1,0:T(8,128)(2,1)} %copy-done.2, ...), custom_call_target="tpu_custom_call" | custom-call | tf_op jit(solution)/shard_map/pallas_call | solution.py:103
Async XLA Ops:
  0.0 22.2 %copy-start = (f32[64,64]{1,0:T(8,128)S(1)}, f32[64,64]{1,0:T(8,128)}, u32[]{:S(2)}) copy-start(f32[64,64]{1,0:T(8,128)} %param.10) | copy-start | bytes 49156
  0.7 21.6 %copy-start.1 = (f32[4,8,64,128]{3,2,1,0:T(8,128)S(1)}, f32[4,8,64,128]{3,2,1,0:T(8,128)}, u32[]{:S(2)}) copy-start(f32[4,8,64,128]{3,2,1,0:T(8,128)} %src_ref.1) | copy-start | bytes 3145732
  5.0 20.6 %collective-permute-start.2 = (bf16[4,1,64,128]{3,2,1,0:T(8,128)(2,1)}, bf16[4,1,64,128]{3,2,1,0:T(8,128)(2,1)S(1)}, u32[]{:S(2)}, u32[]{:S(2)}) collective-permute-start(bf16[4,1,64,128]{3,2,1,0:T(8,128)(2,1)} %get-tuple-element.13), channel_id=1, source_target_pairs={{0,1},{1,2},{2,3},{3,4},{4,5},{5,6},{6,7},{7,8},{8,9},{9,10},{10,1... | collective-permute-start | bytes 196616 | tf_op jit(solution)/shard_map/ppermute | solution.py:121
  6.9 18.7 %collective-permute-start.3 = (bf16[4,1,64,128]{3,2,1,0:T(8,128)(2,1)}, bf16[4,1,64,128]{3,2,1,0:T(8,128)(2,1)S(1)}, u32[]{:S(2)}, u32[]{:S(2)}) collective-permute-start(bf16[4,1,64,128]{3,2,1,0:T(8,128)(2,1)} %get-tuple-element.14), channel_id=1, source_target_pairs={{1,0},{2,1},{3,2},{4,3},{5,4},{6,5},{7,6},{8,7},{9,8},{10,9},{11,1... | collective-permute-start | bytes 196616 | tf_op jit(solution)/shard_map/ppermute | solution.py:121
  12.4 9.9 %copy-start.6 = (f32[4,8]{1,0:T(4,128)S(1)}, f32[4,8]{1,0:T(4,128)}, u32[]{:S(2)}) copy-start(f32[4,8]{1,0:T(4,128)} %param.8) | copy-start | bytes 388
  12.4 13.2 %collective-permute-start = (bf16[1,8,64,128]{3,2,1,0:T(8,128)(2,1)}, bf16[1,8,64,128]{3,2,1,0:T(8,128)(2,1)S(1)}, u32[]{:S(2)}, u32[]{:S(2)}) collective-permute-start(bf16[1,8,64,128]{3,2,1,0:T(8,128)(2,1)} %get-tuple-element.11), channel_id=1, source_target_pairs={{0,32},{32,64},{64,96},{96,128},{128,160},{160,192},{192,224},{224... | collective-permute-start | bytes 393224 | tf_op jit(solution)/shard_map/ppermute | solution.py:121
  20.3 8.6 %collective-permute-start.1 = (bf16[1,8,64,128]{3,2,1,0:T(8,128)(2,1)}, bf16[1,8,64,128]{3,2,1,0:T(8,128)(2,1)S(1)}, u32[]{:S(2)}, u32[]{:S(2)}) collective-permute-start(bf16[1,8,64,128]{3,2,1,0:T(8,128)(2,1)} %get-tuple-element.12), channel_id=1, source_target_pairs={{32,0},{64,32},{96,64},{128,96},{160,128},{192,160},{224,192},{256... | collective-permute-start | bytes 393224 | tf_op jit(solution)/shard_map/ppermute | solution.py:121
  25.6 3.3 %copy-start.4 = (bf16[4,1,64,128]{3,2,1,0:T(8,128)(2,1)}, bf16[4,1,64,128]{3,2,1,0:T(8,128)(2,1)S(1)}, u32[]{:S(2)}) copy-start(bf16[4,1,64,128]{3,2,1,0:T(8,128)(2,1)S(1)} %collective-permute-done.2.left_ref) | copy-start | bytes 196612
  25.6 3.3 %copy-start.5 = (bf16[4,1,64,128]{3,2,1,0:T(8,128)(2,1)}, bf16[4,1,64,128]{3,2,1,0:T(8,128)(2,1)S(1)}, u32[]{:S(2)}) copy-start(bf16[4,1,64,128]{3,2,1,0:T(8,128)(2,1)S(1)} %collective-permute-done.3.right_ref) | copy-start | bytes 196612
  25.6 3.3 %copy-start.2 = (bf16[1,8,64,128]{3,2,1,0:T(8,128)(2,1)}, bf16[1,8,64,128]{3,2,1,0:T(8,128)(2,1)S(1)}, u32[]{:S(2)}) copy-start(bf16[1,8,64,128]{3,2,1,0:T(8,128)(2,1)S(1)} %collective-permute-done.above_ref) | copy-start | bytes 393220
  28.9 0.6 %copy-start.3 = (bf16[1,8,64,128]{3,2,1,0:T(8,128)(2,1)}, bf16[1,8,64,128]{3,2,1,0:T(8,128)(2,1)S(1)}, u32[]{:S(2)}) copy-start(bf16[1,8,64,128]{3,2,1,0:T(8,128)(2,1)S(1)} %collective-permute-done.1.below_ref) | copy-start | bytes 393220

commit v5 on v4

--- a/solution.py
+++ b/solution.py
@@ -57,10 +57,20 @@
 
 
 def later_sweep_kernel(
-    anchor_ref, count_ref, mask_ref, pre_ref, field_ref, above_ref, below_ref,
-    left_ref, right_ref, inv_ref, out_ref, packed_ref, acc_ref,
+    anchor_ref, count_ref, mask_ref, stiffness_ref, load_ref, field_ref, operator_ref,
+    above_ref, below_ref, left_ref, right_ref, inv_ref, out_ref, packed_ref, acc_ref,
 ):
-    rows, columns = field_ref.shape[:2]
+    rows, columns, depth, loads = field_ref.shape
+    local = []
+    for x in range(rows):
+        wide = jnp.concatenate([field_ref[x, y] for y in range(columns)], axis=1)
+        local.append(
+            jnp.dot(
+                operator_ref[...], wide,
+                precision=lax.Precision.HIGHEST,
+                preferred_element_type=jnp.float32,
+            )
+        )
 
     def weighted(x, y):
         return weight_of(mask_ref, x, y) * field_ref[x, y]
@@ -72,9 +82,10 @@
             next_y = weighted(x, y + 1) if y + 1 < columns else right_ref[x, 0].astype(jnp.float32)
             prev_y = weighted(x, y - 1) if y > 0 else left_ref[x, 0].astype(jnp.float32)
             beside = next_x + prev_x + next_y + prev_y
-            packed_ref[x, y] = (pre_ref[x, y] + weight_of(mask_ref, x, y) * beside).astype(
-                jnp.bfloat16
-            )
+            operated = stiffness_ref[x, y] * local[x][:, y * loads : (y + 1) * loads]
+            packed_ref[x, y] = (
+                load_ref[x, y] - (operated - weight_of(mask_ref, x, y) * beside)
+            ).astype(jnp.bfloat16)
     deposit_patches(anchor_ref, count_ref, packed_ref, inv_ref, acc_ref)
     out_ref[...] = field_ref[...] + acc_ref[...]
 
@@ -99,17 +110,17 @@
     )(anchors, count.reshape(1), mask, src, inverse)
 
 
-def later_sweep(pre, field, halos, inverse, anchors, count, mask):
+def later_sweep(load, field, operator, stiffness, halos, inverse, anchors, count, mask):
     return pl.pallas_call(
         later_sweep_kernel,
         out_shape=jax.ShapeDtypeStruct(field.shape, jnp.float32),
-        in_specs=[SMEM, SMEM, SMEM] + [VMEM] * 7,
+        in_specs=[SMEM, SMEM, SMEM, SMEM] + [VMEM] * 8,
         out_specs=VMEM,
         scratch_shapes=[
             pltpu.VMEM(field.shape, jnp.bfloat16),
             pltpu.VMEM(field.shape, jnp.float32),
         ],
-    )(anchors, count.reshape(1), mask, pre, field, *halos, inverse)
+    )(anchors, count.reshape(1), mask, stiffness, load, field, operator, *halos, inverse)
 
 
 def shifted_in(edge, axis, forward):
@@ -136,11 +147,10 @@
             shifted_in(right, "gy", True),
             shifted_in(left, "gy", False),
         )
-        local = jnp.einsum(
-            "kl,xylr->xykr", column_operator, field, precision=lax.Precision.HIGHEST
+        field = later_sweep(
+            load_field, field, column_operator, stiffness, halos, inverse, anchors, count,
+            fault_mask,
         )
-        pre = load_field - stiffness[:, :, None, None] * local
-        field = later_sweep(pre, field, halos, inverse, anchors, count, fault_mask)
     return field
 
 

time: 34.8 us -> 34.6 us (level)
  the two profiles are of different devices: /device:TPU:467 before, /device:TPU:1 now
where the time goes in v5:
time: 34.6 us; the launch traced here: 34.4 us
  starting transfers between devices  20.1 us (58%)
  Pallas kernels  7.33 us (21%)
  waiting for transfers between devices  5.5 us (16%)
  local copies, waits for them, and re-layouts  0.71 us (2%)
  between operations  0.71 us (2%)
    ppermute x4, starting transfers between devices, shifted_in(): return lax.ppermute(edge, axis, pairs)  20.1 us
    ppermute x4, waiting for transfers between devices, shifted_in(): return lax.ppermute(edge, axis, pairs)  5.5 us
    pallas_call x1, Pallas kernels, later_sweep(): pl.pallas_call(later_sweep_kernel, out_shape=jax.ShapeDtypeStruct(field.s...  4.38 us
    pallas_call x1, Pallas kernels, first_sweep(): pl.pallas_call(first_sweep_kernel, out_shape=(jax.ShapeDtypeStruct(src.sh...  2.95 us
    unnamed x8, local copies, waits for them, and re-layouts  0.71 us
  transfers between devices with their start and end apart: 4, of which 2 were waited for; matrix products, arithmetic and copies ran while one was open for 0% of the time, Pallas kernels for 0%

profile of v5, /device:TPU:1, one launch (start us, length us, event | category | flops | bytes accessed | tf_op | source)
XLA Modules:
  0.0 34.4 jit_solution(7076948883822150884)
XLA Ops:
  0.7 3.0 %shard_map.73 = (f32[4,8,64,128]{3,2,1,0:T(8,128)}, bf16[1,8,64,128]{3,2,1,0:T(8,128)(2,1)}, bf16[1,8,64,128]{3,2,1,0:T(8,128)(2,1)}, bf16[4,1,64,128]{3,2,1,0:T(8,128)(2,1)}, bf16[4,1,64,128]{3,2,1,0:T(8,128)(2,1)}) custom-call(s32[8]{0:T(128)} %bitcast.7, s32[1]{0:T(128)} %bitcast.3.count_ref, s32[4,8]{1,0:T(4,128)} %mask_ref.3, ...), custom_call_target="tpu_custom_call" | custom-call | tf_op jit(solution)/shard_map/pallas_call | solution.py:101
  3.6 5.2 %collective-permute-start = (bf16[1,8,64,128]{3,2,1,0:T(8,128)(2,1)}, bf16[1,8,64,128]{3,2,1,0:T(8,128)(2,1)S(1)}, u32[]{:S(2)}, u32[]{:S(2)}) collective-permute-start(bf16[1,8,64,128]{3,2,1,0:T(8,128)(2,1)} %get-tuple-element.11), channel_id=1, source_target_pairs={{0,32},{32,64},{64,96},{96,128},{128,160},{160,192},{192,224},{224... | collective-permute-start | bytes 393224 | tf_op jit(solution)/shard_map/ppermute | solution.py:132
  8.8 12.3 %collective-permute-start.1 = (bf16[1,8,64,128]{3,2,1,0:T(8,128)(2,1)}, bf16[1,8,64,128]{3,2,1,0:T(8,128)(2,1)S(1)}, u32[]{:S(2)}, u32[]{:S(2)}) collective-permute-start(bf16[1,8,64,128]{3,2,1,0:T(8,128)(2,1)} %get-tuple-element.12), channel_id=1, source_target_pairs={{32,0},{64,32},{96,64},{128,96},{160,128},{192,160},{224,192},{256... | collective-permute-start | bytes 393224 | tf_op jit(solution)/shard_map/ppermute | solution.py:132
  21.1 1.3 %collective-permute-start.2 = (bf16[4,1,64,128]{3,2,1,0:T(8,128)(2,1)}, bf16[4,1,64,128]{3,2,1,0:T(8,128)(2,1)S(1)}, u32[]{:S(2)}, u32[]{:S(2)}) collective-permute-start(bf16[4,1,64,128]{3,2,1,0:T(8,128)(2,1)} %get-tuple-element.13), channel_id=1, source_target_pairs={{0,1},{1,2},{2,3},{3,4},{4,5},{5,6},{6,7},{7,8},{8,9},{9,10},{10,1... | collective-permute-start | bytes 196616 | tf_op jit(solution)/shard_map/ppermute | solution.py:132
  22.4 1.3 %collective-permute-start.3 = (bf16[4,1,64,128]{3,2,1,0:T(8,128)(2,1)}, bf16[4,1,64,128]{3,2,1,0:T(8,128)(2,1)S(1)}, u32[]{:S(2)}, u32[]{:S(2)}) collective-permute-start(bf16[4,1,64,128]{3,2,1,0:T(8,128)(2,1)} %get-tuple-element.14), channel_id=1, source_target_pairs={{1,0},{2,1},{3,2},{4,3},{5,4},{6,5},{7,6},{8,7},{9,8},{10,9},{11,1... | collective-permute-start | bytes 196616 | tf_op jit(solution)/shard_map/ppermute | solution.py:132
  23.7 0.5 %collective-permute-done.2.left_ref = bf16[4,1,64,128]{3,2,1,0:T(8,128)(2,1)S(1)} collective-permute-done((bf16[4,1,64,128]{3,2,1,0:T(8,128)(2,1)}, bf16[4,1,64,128]{3,2,1,0:T(8,128)(2,1)S(1)}, u32[]{:S(2)}, u32[]{:S(2)}) %collective-permute-start.2) | collective-permute-done | bytes 65568 | tf_op jit(solution)/shard_map/ppermute | solution.py:132
  24.2 0.0 copy-start.2
  24.2 5.0 %collective-permute-done.3.right_ref = bf16[4,1,64,128]{3,2,1,0:T(8,128)(2,1)S(1)} collective-permute-done((bf16[4,1,64,128]{3,2,1,0:T(8,128)(2,1)}, bf16[4,1,64,128]{3,2,1,0:T(8,128)(2,1)S(1)}, u32[]{:S(2)}, u32[]{:S(2)}) %collective-permute-start.3) | collective-permute-done | bytes 65568 | tf_op jit(solution)/shard_map/ppermute | solution.py:132
  29.2 0.0 copy-start.3
  29.3 0.0 collective-permute-done.above_ref
  29.3 0.0 copy-start
  29.3 0.0 collective-permute-done.1.below_ref
  29.3 0.0 copy-start.1
  29.3 0.0 copy-done.2
  29.3 0.6 %copy-done.3 = bf16[4,1,64,128]{3,2,1,0:T(8,128)(2,1)} copy-done((bf16[4,1,64,128]{3,2,1,0:T(8,128)(2,1)}, bf16[4,1,64,128]{3,2,1,0:T(8,128)(2,1)S(1)}, u32[]{:S(2)}) %copy-start.3) | copy-done | bytes 65560
  29.9 0.1 copy-done
  29.9 0.1 copy-done.1
  30.0 4.4 %shard_map.74 = f32[4,8,64,128]{3,2,1,0:T(8,128)} custom-call(s32[8]{0:T(128)} %bitcast.8, s32[1]{0:T(128)} %bitcast.4.count_ref, s32[4,8]{1,0:T(4,128)} %mask_ref.3, f32[4,8]{1,0:T(4,128)} %stiffness_ref.1, f32[4,8,64,128]{3,2,1,0:T(8,128)} %load_ref.1, f32[4,8,64,128]{3,2,1,0:T(8,128)} %get-tuple-element.10.field_ref, f32[64,64]{1,0:T(8,128)} %operator_ref.1, ...), custom_call_target="tpu_custom_call" | custom-call | tf_op jit(solution)/shard_map/pallas_call | solution.py:114
Async XLA Ops:
  3.6 25.7 %collective-permute-start = (bf16[1,8,64,128]{3,2,1,0:T(8,128)(2,1)}, bf16[1,8,64,128]{3,2,1,0:T(8,128)(2,1)S(1)}, u32[]{:S(2)}, u32[]{:S(2)}) collective-permute-start(bf16[1,8,64,128]{3,2,1,0:T(8,128)(2,1)} %get-tuple-element.11), channel_id=1, source_target_pairs={{0,32},{32,64},{64,96},{96,128},{128,160},{160,192},{192,224},{224... | collective-permute-start | bytes 393224 | tf_op jit(solution)/shard_map/ppermute | solution.py:132
  8.8 20.4 %collective-permute-start.1 = (bf16[1,8,64,128]{3,2,1,0:T(8,128)(2,1)}, bf16[1,8,64,128]{3,2,1,0:T(8,128)(2,1)S(1)}, u32[]{:S(2)}, u32[]{:S(2)}) collective-permute-start(bf16[1,8,64,128]{3,2,1,0:T(8,128)(2,1)} %get-tuple-element.12), channel_id=1, source_target_pairs={{32,0},{64,32},{96,64},{128,96},{160,128},{192,160},{224,192},{256... | collective-permute-start | bytes 393224 | tf_op jit(solution)/shard_map/ppermute | solution.py:132
  21.1 3.1 %collective-permute-start.2 = (bf16[4,1,64,128]{3,2,1,0:T(8,128)(2,1)}, bf16[4,1,64,128]{3,2,1,0:T(8,128)(2,1)S(1)}, u32[]{:S(2)}, u32[]{:S(2)}) collective-permute-start(bf16[4,1,64,128]{3,2,1,0:T(8,128)(2,1)} %get-tuple-element.13), channel_id=1, source_target_pairs={{0,1},{1,2},{2,3},{3,4},{4,5},{5,6},{6,7},{7,8},{8,9},{9,10},{10,1... | collective-permute-start | bytes 196616 | tf_op jit(solution)/shard_map/ppermute | solution.py:132
  22.4 6.8 %collective-permute-start.3 = (bf16[4,1,64,128]{3,2,1,0:T(8,128)(2,1)}, bf16[4,1,64,128]{3,2,1,0:T(8,128)(2,1)S(1)}, u32[]{:S(2)}, u32[]{:S(2)}) collective-permute-start(bf16[4,1,64,128]{3,2,1,0:T(8,128)(2,1)} %get-tuple-element.14), channel_id=1, source_target_pairs={{1,0},{2,1},{3,2},{4,3},{5,4},{6,5},{7,6},{8,7},{9,8},{10,9},{11,1... | collective-permute-start | bytes 196616 | tf_op jit(solution)/shard_map/ppermute | solution.py:132
  24.2 5.1 %copy-start.2 = (bf16[4,1,64,128]{3,2,1,0:T(8,128)(2,1)}, bf16[4,1,64,128]{3,2,1,0:T(8,128)(2,1)S(1)}, u32[]{:S(2)}) copy-start(bf16[4,1,64,128]{3,2,1,0:T(8,128)(2,1)S(1)} %collective-permute-done.2.left_ref) | copy-start | bytes 196612
  29.2 0.6 %copy-start.3 = (bf16[4,1,64,128]{3,2,1,0:T(8,128)(2,1)}, bf16[4,1,64,128]{3,2,1,0:T(8,128)(2,1)S(1)}, u32[]{:S(2)}) copy-start(bf16[4,1,64,128]{3,2,1,0:T(8,128)(2,1)S(1)} %collective-permute-done.3.right_ref) | copy-start | bytes 196612
  29.3 0.7 %copy-start = (bf16[1,8,64,128]{3,2,1,0:T(8,128)(2,1)}, bf16[1,8,64,128]{3,2,1,0:T(8,128)(2,1)S(1)}, u32[]{:S(2)}) copy-start(bf16[1,8,64,128]{3,2,1,0:T(8,128)(2,1)S(1)} %collective-permute-done.above_ref) | copy-start | bytes 393220
  29.3 0.7 %copy-start.1 = (bf16[1,8,64,128]{3,2,1,0:T(8,128)(2,1)}, bf16[1,8,64,128]{3,2,1,0:T(8,128)(2,1)S(1)}, u32[]{:S(2)}) copy-start(bf16[1,8,64,128]{3,2,1,0:T(8,128)(2,1)S(1)} %collective-permute-done.1.below_ref) | copy-start | bytes 393220

commit v6 on v4

--- a/solution.py
+++ b/solution.py
@@ -56,9 +56,24 @@
         right_ref[x, 0] = (weight_of(mask_ref, x, columns - 1) * acc_ref[x, columns - 1]).astype(right_ref.dtype)
 
 
+def operator_kernel(stiffness_ref, load_ref, field_ref, operator_ref, pre_ref):
+    rows, columns, depth, loads = field_ref.shape
+    for x in range(rows):
+        wide = jnp.concatenate([field_ref[x, y] for y in range(columns)], axis=1)
+        local = jnp.dot(
+            operator_ref[...], wide,
+            precision=lax.Precision.HIGHEST,
+            preferred_element_type=jnp.float32,
+        )
+        for y in range(columns):
+            pre_ref[x, y] = load_ref[x, y] - stiffness_ref[x, y] * local[
+                :, y * loads : (y + 1) * loads
+            ]
+
+
 def later_sweep_kernel(
-    anchor_ref, count_ref, mask_ref, pre_ref, field_ref, above_ref, below_ref,
-    left_ref, right_ref, inv_ref, out_ref, packed_ref, acc_ref,
+    anchor_ref, count_ref, mask_ref, pre_ref, field_ref,
+    above_ref, below_ref, left_ref, right_ref, inv_ref, out_ref, packed_ref, acc_ref,
 ):
     rows, columns = field_ref.shape[:2]
 
@@ -99,6 +114,20 @@
     )(anchors, count.reshape(1), mask, src, inverse)
 
 
+def operator_part(load, field, operator, stiffness):
+    rows, columns, depth, loads = field.shape
+    flops = 2 * rows * columns * depth * depth * loads * 6
+    return pl.pallas_call(
+        operator_kernel,
+        out_shape=jax.ShapeDtypeStruct(field.shape, jnp.float32),
+        in_specs=[SMEM, VMEM, VMEM, VMEM],
+        out_specs=VMEM,
+        cost_estimate=pl.CostEstimate(
+            flops=flops, bytes_accessed=3 * field.size * 4, transcendentals=0
+        ),
+    )(stiffness, load, field, operator)
+
+
 def later_sweep(pre, field, halos, inverse, anchors, count, mask):
     return pl.pallas_call(
         later_sweep_kernel,
@@ -136,10 +165,7 @@
             shifted_in(right, "gy", True),
             shifted_in(left, "gy", False),
         )
-        local = jnp.einsum(
-            "kl,xylr->xykr", column_operator, field, precision=lax.Precision.HIGHEST
-        )
-        pre = load_field - stiffness[:, :, None, None] * local
+        pre = operator_part(load_field, field, column_operator, stiffness)
         field = later_sweep(pre, field, halos, inverse, anchors, count, fault_mask)
     return field
 

time: 34.8 us -> 34.4 us (0.989)
  the two profiles are of different devices: /device:TPU:467 before, /device:TPU:1 now
where the time goes in v6:
time: 34.4 us; the launch traced here: 34.2 us
  starting transfers between devices  20.3 us (59%)
  Pallas kernels  10.5 us (31%)
  waiting for transfers between devices  1.94 us (6%)
  between operations  0.71 us (2%)
  local copies, waits for them, and re-layouts  0.7 us (2%)
    ppermute x4, starting transfers between devices, shifted_in(): return lax.ppermute(edge, axis, pairs)  20.3 us
    pallas_call x1, Pallas kernels, later_sweep(): pl.pallas_call(later_sweep_kernel, out_shape=jax.ShapeDtypeStruct(field.s...  3.83 us
    pallas_call x1, Pallas kernels, operator_part(): pl.pallas_call(operator_kernel, out_shape=jax.ShapeDtypeStruct(field.shap...  3.56 us
    pallas_call x1, Pallas kernels, first_sweep(): pl.pallas_call(first_sweep_kernel, out_shape=(jax.ShapeDtypeStruct(src.sh...  3.14 us
    ppermute x4, waiting for transfers between devices, shifted_in(): return lax.ppermute(edge, axis, pairs)  1.94 us
    unnamed x8, local copies, waits for them, and re-layouts  0.7 us
  transfers between devices with their start and end apart: 4, of which 1 were waited for; matrix products, arithmetic and copies ran while one was open for 0% of the time, Pallas kernels for 10%

profile of v6, /device:TPU:1, one launch (start us, length us, event | category | flops | bytes accessed | tf_op | source)
XLA Modules:
  0.0 34.2 jit_solution(11221559813105740899)
XLA Ops:
  0.7 3.1 %shard_map.73 = (f32[4,8,64,128]{3,2,1,0:T(8,128)}, bf16[1,8,64,128]{3,2,1,0:T(8,128)(2,1)}, bf16[1,8,64,128]{3,2,1,0:T(8,128)(2,1)}, bf16[4,1,64,128]{3,2,1,0:T(8,128)(2,1)}, bf16[4,1,64,128]{3,2,1,0:T(8,128)(2,1)}) custom-call(s32[8]{0:T(128)} %bitcast.7, s32[1]{0:T(128)} %bitcast.3.count_ref, s32[4,8]{1,0:T(4,128)} %mask_ref.3, ...), custom_call_target="tpu_custom_call" | custom-call | tf_op jit(solution)/shard_map/pallas_call | solution.py:105
  3.8 4.9 %collective-permute-start = (bf16[1,8,64,128]{3,2,1,0:T(8,128)(2,1)}, bf16[1,8,64,128]{3,2,1,0:T(8,128)(2,1)S(1)}, u32[]{:S(2)}, u32[]{:S(2)}) collective-permute-start(bf16[1,8,64,128]{3,2,1,0:T(8,128)(2,1)} %get-tuple-element.11), channel_id=1, source_target_pairs={{0,32},{32,64},{64,96},{96,128},{128,160},{160,192},{192,224},{224... | collective-permute-start | bytes 393224 | tf_op jit(solution)/shard_map/ppermute | solution.py:150
  8.7 12.8 %collective-permute-start.1 = (bf16[1,8,64,128]{3,2,1,0:T(8,128)(2,1)}, bf16[1,8,64,128]{3,2,1,0:T(8,128)(2,1)S(1)}, u32[]{:S(2)}, u32[]{:S(2)}) collective-permute-start(bf16[1,8,64,128]{3,2,1,0:T(8,128)(2,1)} %get-tuple-element.12), channel_id=1, source_target_pairs={{32,0},{64,32},{96,64},{128,96},{160,128},{192,160},{224,192},{256... | collective-permute-start | bytes 393224 | tf_op jit(solution)/shard_map/ppermute | solution.py:150
  21.5 1.3 %collective-permute-start.2 = (bf16[4,1,64,128]{3,2,1,0:T(8,128)(2,1)}, bf16[4,1,64,128]{3,2,1,0:T(8,128)(2,1)S(1)}, u32[]{:S(2)}, u32[]{:S(2)}) collective-permute-start(bf16[4,1,64,128]{3,2,1,0:T(8,128)(2,1)} %get-tuple-element.13), channel_id=1, source_target_pairs={{0,1},{1,2},{2,3},{3,4},{4,5},{5,6},{6,7},{7,8},{8,9},{9,10},{10,1... | collective-permute-start | bytes 196616 | tf_op jit(solution)/shard_map/ppermute | solution.py:150
  22.8 1.3 %collective-permute-start.3 = (bf16[4,1,64,128]{3,2,1,0:T(8,128)(2,1)}, bf16[4,1,64,128]{3,2,1,0:T(8,128)(2,1)S(1)}, u32[]{:S(2)}, u32[]{:S(2)}) collective-permute-start(bf16[4,1,64,128]{3,2,1,0:T(8,128)(2,1)} %get-tuple-element.14), channel_id=1, source_target_pairs={{1,0},{2,1},{3,2},{4,3},{5,4},{6,5},{7,6},{8,7},{9,8},{10,9},{11,1... | collective-permute-start | bytes 196616 | tf_op jit(solution)/shard_map/ppermute | solution.py:150
  24.1 3.6 %shard_map.74.pre_ref = f32[4,8,64,128]{3,2,1,0:T(8,128)} custom-call(f32[4,8]{1,0:T(4,128)} %stiffness_ref.1, f32[4,8,64,128]{3,2,1,0:T(8,128)} %load_ref.1, f32[4,8,64,128]{3,2,1,0:T(8,128)} %get-tuple-element.10.field_ref, f32[64,64]{1,0:T(8,128)} %operator_ref.1), custom_call_target="tpu_custom_call" | custom-call | flops 201326592 | bytes 3145728 | tf_op jit(solution)/shard_map/pallas_call | solution.py:120
  27.7 0.0 collective-permute-done.2.left_ref
  27.7 0.0 copy-start.2
  27.7 1.9 %collective-permute-done.3.right_ref = bf16[4,1,64,128]{3,2,1,0:T(8,128)(2,1)S(1)} collective-permute-done((bf16[4,1,64,128]{3,2,1,0:T(8,128)(2,1)}, bf16[4,1,64,128]{3,2,1,0:T(8,128)(2,1)S(1)}, u32[]{:S(2)}, u32[]{:S(2)}) %collective-permute-start.3) | collective-permute-done | bytes 65568 | tf_op jit(solution)/shard_map/ppermute | solution.py:150
  29.6 0.0 copy-start.3
  29.6 0.0 collective-permute-done.above_ref
  29.6 0.0 copy-start
  29.6 0.0 collective-permute-done.1.below_ref
  29.6 0.0 copy-start.1
  29.6 0.0 copy-done.2
  29.7 0.6 %copy-done.3 = bf16[4,1,64,128]{3,2,1,0:T(8,128)(2,1)} copy-done((bf16[4,1,64,128]{3,2,1,0:T(8,128)(2,1)}, bf16[4,1,64,128]{3,2,1,0:T(8,128)(2,1)S(1)}, u32[]{:S(2)}) %copy-start.3) | copy-done | bytes 65560
  30.2 0.1 copy-done
  30.3 0.0 copy-done.1
  30.3 3.8 %shard_map.75 = f32[4,8,64,128]{3,2,1,0:T(8,128)} custom-call(s32[8]{0:T(128)} %bitcast.8, s32[1]{0:T(128)} %bitcast.4.count_ref, s32[4,8]{1,0:T(4,128)} %mask_ref.3, f32[4,8,64,128]{3,2,1,0:T(8,128)} %shard_map.74.pre_ref, f32[4,8,64,128]{3,2,1,0:T(8,128)} %get-tuple-element.10.field_ref, bf16[1,8,64,128]{3,2,1,0:T(8,128)(2,1)} %copy-done, ...), custom_call_target="tpu_custom_call" | custom-call | tf_op jit(solution)/shard_map/pallas_call | solution.py:132
Async XLA Ops:
  3.8 25.8 %collective-permute-start = (bf16[1,8,64,128]{3,2,1,0:T(8,128)(2,1)}, bf16[1,8,64,128]{3,2,1,0:T(8,128)(2,1)S(1)}, u32[]{:S(2)}, u32[]{:S(2)}) collective-permute-start(bf16[1,8,64,128]{3,2,1,0:T(8,128)(2,1)} %get-tuple-element.11), channel_id=1, source_target_pairs={{0,32},{32,64},{64,96},{96,128},{128,160},{160,192},{192,224},{224... | collective-permute-start | bytes 393224 | tf_op jit(solution)/shard_map/ppermute | solution.py:150
  8.7 21.0 %collective-permute-start.1 = (bf16[1,8,64,128]{3,2,1,0:T(8,128)(2,1)}, bf16[1,8,64,128]{3,2,1,0:T(8,128)(2,1)S(1)}, u32[]{:S(2)}, u32[]{:S(2)}) collective-permute-start(bf16[1,8,64,128]{3,2,1,0:T(8,128)(2,1)} %get-tuple-element.12), channel_id=1, source_target_pairs={{32,0},{64,32},{96,64},{128,96},{160,128},{192,160},{224,192},{256... | collective-permute-start | bytes 393224 | tf_op jit(solution)/shard_map/ppermute | solution.py:150
  21.5 6.2 %collective-permute-start.2 = (bf16[4,1,64,128]{3,2,1,0:T(8,128)(2,1)}, bf16[4,1,64,128]{3,2,1,0:T(8,128)(2,1)S(1)}, u32[]{:S(2)}, u32[]{:S(2)}) collective-permute-start(bf16[4,1,64,128]{3,2,1,0:T(8,128)(2,1)} %get-tuple-element.13), channel_id=1, source_target_pairs={{0,1},{1,2},{2,3},{3,4},{4,5},{5,6},{6,7},{7,8},{8,9},{9,10},{10,1... | collective-permute-start | bytes 196616 | tf_op jit(solution)/shard_map/ppermute | solution.py:150
  22.8 6.8 %collective-permute-start.3 = (bf16[4,1,64,128]{3,2,1,0:T(8,128)(2,1)}, bf16[4,1,64,128]{3,2,1,0:T(8,128)(2,1)S(1)}, u32[]{:S(2)}, u32[]{:S(2)}) collective-permute-start(bf16[4,1,64,128]{3,2,1,0:T(8,128)(2,1)} %get-tuple-element.14), channel_id=1, source_target_pairs={{1,0},{2,1},{3,2},{4,3},{5,4},{6,5},{7,6},{8,7},{9,8},{10,9},{11,1... | collective-permute-start | bytes 196616 | tf_op jit(solution)/shard_map/ppermute | solution.py:150
  27.7 2.0 %copy-start.2 = (bf16[4,1,64,128]{3,2,1,0:T(8,128)(2,1)}, bf16[4,1,64,128]{3,2,1,0:T(8,128)(2,1)S(1)}, u32[]{:S(2)}) copy-start(bf16[4,1,64,128]{3,2,1,0:T(8,128)(2,1)S(1)} %collective-permute-done.2.left_ref) | copy-start | bytes 196612
  29.6 0.6 %copy-start.3 = (bf16[4,1,64,128]{3,2,1,0:T(8,128)(2,1)}, bf16[4,1,64,128]{3,2,1,0:T(8,128)(2,1)S(1)}, u32[]{:S(2)}) copy-start(bf16[4,1,64,128]{3,2,1,0:T(8,128)(2,1)S(1)} %collective-permute-done.3.right_ref) | copy-start | bytes 196612
  29.6 0.7 %copy-start = (bf16[1,8,64,128]{3,2,1,0:T(8,128)(2,1)}, bf16[1,8,64,128]{3,2,1,0:T(8,128)(2,1)S(1)}, u32[]{:S(2)}) copy-start(bf16[1,8,64,128]{3,2,1,0:T(8,128)(2,1)S(1)} %collective-permute-done.above_ref) | copy-start | bytes 393220
  29.6 0.7 %copy-start.1 = (bf16[1,8,64,128]{3,2,1,0:T(8,128)(2,1)}, bf16[1,8,64,128]{3,2,1,0:T(8,128)(2,1)S(1)}, u32[]{:S(2)}) copy-start(bf16[1,8,64,128]{3,2,1,0:T(8,128)(2,1)S(1)} %collective-permute-done.1.below_ref) | copy-start | bytes 393220

commit v7 on v6

--- a/solution.py
+++ b/solution.py
@@ -19,7 +19,6 @@
     rows, columns, depth, loads = src_ref.shape
     slots = inv_ref.shape[0]
     count = count_ref[0]
-    acc_ref[...] = jnp.zeros(acc_ref.shape, jnp.float32)
     for number in range(slots):
 
         @pl.when(number < count)
@@ -43,11 +42,12 @@
 
 def first_sweep_kernel(
     anchor_ref, count_ref, mask_ref, src_ref, inv_ref,
-    out_ref, top_ref, bottom_ref, left_ref, right_ref, acc_ref,
+    out_ref, top_ref, bottom_ref, left_ref, right_ref,
 ):
     rows, columns = src_ref.shape[:2]
+    acc_ref = out_ref
+    acc_ref[...] = jnp.zeros(acc_ref.shape, jnp.float32)
     deposit_patches(anchor_ref, count_ref, src_ref, inv_ref, acc_ref)
-    out_ref[...] = acc_ref[...]
     for y in range(columns):
         top_ref[0, y] = (weight_of(mask_ref, 0, y) * acc_ref[0, y]).astype(top_ref.dtype)
         bottom_ref[0, y] = (weight_of(mask_ref, rows - 1, y) * acc_ref[rows - 1, y]).astype(bottom_ref.dtype)
@@ -73,7 +73,7 @@
 
 def later_sweep_kernel(
     anchor_ref, count_ref, mask_ref, pre_ref, field_ref,
-    above_ref, below_ref, left_ref, right_ref, inv_ref, out_ref, packed_ref, acc_ref,
+    above_ref, below_ref, left_ref, right_ref, inv_ref, out_ref, packed_ref,
 ):
     rows, columns = field_ref.shape[:2]
 
@@ -90,8 +90,8 @@
             packed_ref[x, y] = (pre_ref[x, y] + weight_of(mask_ref, x, y) * beside).astype(
                 jnp.bfloat16
             )
-    deposit_patches(anchor_ref, count_ref, packed_ref, inv_ref, acc_ref)
-    out_ref[...] = field_ref[...] + acc_ref[...]
+    out_ref[...] = field_ref[...]
+    deposit_patches(anchor_ref, count_ref, packed_ref, inv_ref, out_ref)
 
 
 SMEM = pl.BlockSpec(memory_space=pltpu.SMEM)
@@ -110,7 +110,6 @@
         ),
         in_specs=[SMEM, SMEM, SMEM, VMEM, VMEM],
         out_specs=(VMEM,) * 5,
-        scratch_shapes=[pltpu.VMEM(src.shape, jnp.float32)],
     )(anchors, count.reshape(1), mask, src, inverse)
 
 
@@ -134,10 +133,7 @@
         out_shape=jax.ShapeDtypeStruct(field.shape, jnp.float32),
         in_specs=[SMEM, SMEM, SMEM] + [VMEM] * 7,
         out_specs=VMEM,
-        scratch_shapes=[
-            pltpu.VMEM(field.shape, jnp.bfloat16),
-            pltpu.VMEM(field.shape, jnp.float32),
-        ],
+        scratch_shapes=[pltpu.VMEM(field.shape, jnp.bfloat16)],
     )(anchors, count.reshape(1), mask, pre, field, *halos, inverse)
 
 

time: 34.4 us -> 34.3 us (level)
  Pallas kernels: 10.5 us -> 11.1 us
  starting transfers between devices: 20.3 us -> 19.8 us
    ppermute x4, starting transfers between devices: 20.3 us -> 19.8 us  [shifted_in(): return lax.ppermute(edge, axis, pairs)]
where the time goes in v7:
time: 34.3 us; the launch traced here: 34.2 us
  starting transfers between devices  19.8 us (58%)
  Pallas kernels  11.1 us (32%)
  waiting for transfers between devices  1.94 us (6%)
  between operations  0.71 us (2%)
  local copies, waits for them, and re-layouts  0.7 us (2%)
    ppermute x4, starting transfers between devices, shifted_in(): return lax.ppermute(edge, axis, pairs)  19.8 us
    pallas_call x1, Pallas kernels, later_sweep(): pl.pallas_call(later_sweep_kernel, out_shape=jax.ShapeDtypeStruct(field.s...  4.06 us
    pallas_call x1, Pallas kernels, operator_part(): pl.pallas_call(operator_kernel, out_shape=jax.ShapeDtypeStruct(field.shap...  3.57 us
    pallas_call x1, Pallas kernels, first_sweep(): pl.pallas_call(first_sweep_kernel, out_shape=(jax.ShapeDtypeStruct(src.sh...  3.47 us
    ppermute x4, waiting for transfers between devices, shifted_in(): return lax.ppermute(edge, axis, pairs)  1.94 us
    unnamed x8, local copies, waits for them, and re-layouts  0.7 us
  transfers between devices with their start and end apart: 4, of which 1 were waited for; matrix products, arithmetic and copies ran while one was open for 0% of the time, Pallas kernels for 10%

profile of v7, /device:TPU:1, one launch (start us, length us, event | category | flops | bytes accessed | tf_op | source)
XLA Modules:
  0.0 34.2 jit_solution(11606469787662797867)
XLA Ops:
  0.7 3.5 %shard_map.73 = (f32[4,8,64,128]{3,2,1,0:T(8,128)}, bf16[1,8,64,128]{3,2,1,0:T(8,128)(2,1)}, bf16[1,8,64,128]{3,2,1,0:T(8,128)(2,1)}, bf16[4,1,64,128]{3,2,1,0:T(8,128)(2,1)}, bf16[4,1,64,128]{3,2,1,0:T(8,128)(2,1)}) custom-call(s32[8]{0:T(128)} %bitcast.7, s32[1]{0:T(128)} %bitcast.3.count_ref, s32[4,8]{1,0:T(4,128)} %mask_ref.3, ...), custom_call_target="tpu_custom_call" | custom-call | tf_op jit(solution)/shard_map/pallas_call | solution.py:105
  4.1 4.5 %collective-permute-start = (bf16[1,8,64,128]{3,2,1,0:T(8,128)(2,1)}, bf16[1,8,64,128]{3,2,1,0:T(8,128)(2,1)S(1)}, u32[]{:S(2)}, u32[]{:S(2)}) collective-permute-start(bf16[1,8,64,128]{3,2,1,0:T(8,128)(2,1)} %get-tuple-element.11), channel_id=1, source_target_pairs={{0,32},{32,64},{64,96},{96,128},{128,160},{160,192},{192,224},{224... | collective-permute-start | bytes 393224 | tf_op jit(solution)/shard_map/ppermute | solution.py:146
  8.6 12.7 %collective-permute-start.1 = (bf16[1,8,64,128]{3,2,1,0:T(8,128)(2,1)}, bf16[1,8,64,128]{3,2,1,0:T(8,128)(2,1)S(1)}, u32[]{:S(2)}, u32[]{:S(2)}) collective-permute-start(bf16[1,8,64,128]{3,2,1,0:T(8,128)(2,1)} %get-tuple-element.12), channel_id=1, source_target_pairs={{32,0},{64,32},{96,64},{128,96},{160,128},{192,160},{224,192},{256... | collective-permute-start | bytes 393224 | tf_op jit(solution)/shard_map/ppermute | solution.py:146
  21.3 1.3 %collective-permute-start.2 = (bf16[4,1,64,128]{3,2,1,0:T(8,128)(2,1)}, bf16[4,1,64,128]{3,2,1,0:T(8,128)(2,1)S(1)}, u32[]{:S(2)}, u32[]{:S(2)}) collective-permute-start(bf16[4,1,64,128]{3,2,1,0:T(8,128)(2,1)} %get-tuple-element.13), channel_id=1, source_target_pairs={{0,1},{1,2},{2,3},{3,4},{4,5},{5,6},{6,7},{7,8},{8,9},{9,10},{10,1... | collective-permute-start | bytes 196616 | tf_op jit(solution)/shard_map/ppermute | solution.py:146
  22.6 1.3 %collective-permute-start.3 = (bf16[4,1,64,128]{3,2,1,0:T(8,128)(2,1)}, bf16[4,1,64,128]{3,2,1,0:T(8,128)(2,1)S(1)}, u32[]{:S(2)}, u32[]{:S(2)}) collective-permute-start(bf16[4,1,64,128]{3,2,1,0:T(8,128)(2,1)} %get-tuple-element.14), channel_id=1, source_target_pairs={{1,0},{2,1},{3,2},{4,3},{5,4},{6,5},{7,6},{8,7},{9,8},{10,9},{11,1... | collective-permute-start | bytes 196616 | tf_op jit(solution)/shard_map/ppermute | solution.py:146
  23.9 3.6 %shard_map.74.pre_ref = f32[4,8,64,128]{3,2,1,0:T(8,128)} custom-call(f32[4,8]{1,0:T(4,128)} %stiffness_ref.1, f32[4,8,64,128]{3,2,1,0:T(8,128)} %load_ref.1, f32[4,8,64,128]{3,2,1,0:T(8,128)} %get-tuple-element.10.field_ref, f32[64,64]{1,0:T(8,128)} %operator_ref.1), custom_call_target="tpu_custom_call" | custom-call | flops 201326592 | bytes 3145728 | tf_op jit(solution)/shard_map/pallas_call | solution.py:119
  27.5 0.0 collective-permute-done.2.left_ref
  27.5 0.0 copy-start.2
  27.5 1.9 %collective-permute-done.3.right_ref = bf16[4,1,64,128]{3,2,1,0:T(8,128)(2,1)S(1)} collective-permute-done((bf16[4,1,64,128]{3,2,1,0:T(8,128)(2,1)}, bf16[4,1,64,128]{3,2,1,0:T(8,128)(2,1)S(1)}, u32[]{:S(2)}, u32[]{:S(2)}) %collective-permute-start.3) | collective-permute-done | bytes 65568 | tf_op jit(solution)/shard_map/ppermute | solution.py:146
  29.4 0.0 copy-start.3
  29.4 0.0 collective-permute-done.above_ref
  29.4 0.0 copy-start
  29.4 0.0 collective-permute-done.1.below_ref
  29.4 0.0 copy-start.1
  29.4 0.0 copy-done.2
  29.4 0.6 %copy-done.3 = bf16[4,1,64,128]{3,2,1,0:T(8,128)(2,1)} copy-done((bf16[4,1,64,128]{3,2,1,0:T(8,128)(2,1)}, bf16[4,1,64,128]{3,2,1,0:T(8,128)(2,1)S(1)}, u32[]{:S(2)}) %copy-start.3) | copy-done | bytes 65560
  30.0 0.1 copy-done
  30.1 0.0 copy-done.1
  30.1 4.1 %shard_map.75 = f32[4,8,64,128]{3,2,1,0:T(8,128)} custom-call(s32[8]{0:T(128)} %bitcast.8, s32[1]{0:T(128)} %bitcast.4.count_ref, s32[4,8]{1,0:T(4,128)} %mask_ref.3, f32[4,8,64,128]{3,2,1,0:T(8,128)} %shard_map.74.pre_ref, f32[4,8,64,128]{3,2,1,0:T(8,128)} %get-tuple-element.10.field_ref, bf16[1,8,64,128]{3,2,1,0:T(8,128)(2,1)} %copy-done, ...), custom_call_target="tpu_custom_call" | custom-call | tf_op jit(solution)/shard_map/pallas_call | solution.py:131
Async XLA Ops:
  4.1 25.3 %collective-permute-start = (bf16[1,8,64,128]{3,2,1,0:T(8,128)(2,1)}, bf16[1,8,64,128]{3,2,1,0:T(8,128)(2,1)S(1)}, u32[]{:S(2)}, u32[]{:S(2)}) collective-permute-start(bf16[1,8,64,128]{3,2,1,0:T(8,128)(2,1)} %get-tuple-element.11), channel_id=1, source_target_pairs={{0,32},{32,64},{64,96},{96,128},{128,160},{160,192},{192,224},{224... | collective-permute-start | bytes 393224 | tf_op jit(solution)/shard_map/ppermute | solution.py:146
  8.6 20.8 %collective-permute-start.1 = (bf16[1,8,64,128]{3,2,1,0:T(8,128)(2,1)}, bf16[1,8,64,128]{3,2,1,0:T(8,128)(2,1)S(1)}, u32[]{:S(2)}, u32[]{:S(2)}) collective-permute-start(bf16[1,8,64,128]{3,2,1,0:T(8,128)(2,1)} %get-tuple-element.12), channel_id=1, source_target_pairs={{32,0},{64,32},{96,64},{128,96},{160,128},{192,160},{224,192},{256... | collective-permute-start | bytes 393224 | tf_op jit(solution)/shard_map/ppermute | solution.py:146
  21.3 6.2 %collective-permute-start.2 = (bf16[4,1,64,128]{3,2,1,0:T(8,128)(2,1)}, bf16[4,1,64,128]{3,2,1,0:T(8,128)(2,1)S(1)}, u32[]{:S(2)}, u32[]{:S(2)}) collective-permute-start(bf16[4,1,64,128]{3,2,1,0:T(8,128)(2,1)} %get-tuple-element.13), channel_id=1, source_target_pairs={{0,1},{1,2},{2,3},{3,4},{4,5},{5,6},{6,7},{7,8},{8,9},{9,10},{10,1... | collective-permute-start | bytes 196616 | tf_op jit(solution)/shard_map/ppermute | solution.py:146
  22.6 6.8 %collective-permute-start.3 = (bf16[4,1,64,128]{3,2,1,0:T(8,128)(2,1)}, bf16[4,1,64,128]{3,2,1,0:T(8,128)(2,1)S(1)}, u32[]{:S(2)}, u32[]{:S(2)}) collective-permute-start(bf16[4,1,64,128]{3,2,1,0:T(8,128)(2,1)} %get-tuple-element.14), channel_id=1, source_target_pairs={{1,0},{2,1},{3,2},{4,3},{5,4},{6,5},{7,6},{8,7},{9,8},{10,9},{11,1... | collective-permute-start | bytes 196616 | tf_op jit(solution)/shard_map/ppermute | solution.py:146
  27.5 2.0 %copy-start.2 = (bf16[4,1,64,128]{3,2,1,0:T(8,128)(2,1)}, bf16[4,1,64,128]{3,2,1,0:T(8,128)(2,1)S(1)}, u32[]{:S(2)}) copy-start(bf16[4,1,64,128]{3,2,1,0:T(8,128)(2,1)S(1)} %collective-permute-done.2.left_ref) | copy-start | bytes 196612
  29.4 0.6 %copy-start.3 = (bf16[4,1,64,128]{3,2,1,0:T(8,128)(2,1)}, bf16[4,1,64,128]{3,2,1,0:T(8,128)(2,1)S(1)}, u32[]{:S(2)}) copy-start(bf16[4,1,64,128]{3,2,1,0:T(8,128)(2,1)S(1)} %collective-permute-done.3.right_ref) | copy-start | bytes 196612
  29.4 0.7 %copy-start = (bf16[1,8,64,128]{3,2,1,0:T(8,128)(2,1)}, bf16[1,8,64,128]{3,2,1,0:T(8,128)(2,1)S(1)}, u32[]{:S(2)}) copy-start(bf16[1,8,64,128]{3,2,1,0:T(8,128)(2,1)S(1)} %collective-permute-done.above_ref) | copy-start | bytes 393220
  29.4 0.7 %copy-start.1 = (bf16[1,8,64,128]{3,2,1,0:T(8,128)(2,1)}, bf16[1,8,64,128]{3,2,1,0:T(8,128)(2,1)S(1)}, u32[]{:S(2)}) copy-start(bf16[1,8,64,128]{3,2,1,0:T(8,128)(2,1)S(1)} %collective-permute-done.1.below_ref) | copy-start | bytes 393220

commit v8 on v7

--- a/solution.py
+++ b/solution.py
@@ -56,8 +56,12 @@
         right_ref[x, 0] = (weight_of(mask_ref, x, columns - 1) * acc_ref[x, columns - 1]).astype(right_ref.dtype)
 
 
-def operator_kernel(stiffness_ref, load_ref, field_ref, operator_ref, pre_ref):
+def operator_kernel(mask_ref, stiffness_ref, load_ref, field_ref, operator_ref, pre_ref):
     rows, columns, depth, loads = field_ref.shape
+
+    def weighted(x, y):
+        return weight_of(mask_ref, x, y) * field_ref[x, y]
+
     for x in range(rows):
         wide = jnp.concatenate([field_ref[x, y] for y in range(columns)], axis=1)
         local = jnp.dot(
@@ -66,9 +70,16 @@
             preferred_element_type=jnp.float32,
         )
         for y in range(columns):
-            pre_ref[x, y] = load_ref[x, y] - stiffness_ref[x, y] * local[
-                :, y * loads : (y + 1) * loads
+            near = [
+                weighted(x + dx, y + dy)
+                for dx, dy in ((1, 0), (-1, 0), (0, 1), (0, -1))
+                if 0 <= x + dx < rows and 0 <= y + dy < columns
             ]
+            beside = near[0]
+            for term in near[1:]:
+                beside = beside + term
+            operated = stiffness_ref[x, y] * local[:, y * loads : (y + 1) * loads]
+            pre_ref[x, y] = load_ref[x, y] - (operated - weight_of(mask_ref, x, y) * beside)
 
 
 def later_sweep_kernel(
@@ -76,20 +87,24 @@
     above_ref, below_ref, left_ref, right_ref, inv_ref, out_ref, packed_ref,
 ):
     rows, columns = field_ref.shape[:2]
-
-    def weighted(x, y):
-        return weight_of(mask_ref, x, y) * field_ref[x, y]
-
     for x in range(rows):
         for y in range(columns):
-            next_x = weighted(x + 1, y) if x + 1 < rows else below_ref[0, y].astype(jnp.float32)
-            prev_x = weighted(x - 1, y) if x > 0 else above_ref[0, y].astype(jnp.float32)
-            next_y = weighted(x, y + 1) if y + 1 < columns else right_ref[x, 0].astype(jnp.float32)
-            prev_y = weighted(x, y - 1) if y > 0 else left_ref[x, 0].astype(jnp.float32)
-            beside = next_x + prev_x + next_y + prev_y
-            packed_ref[x, y] = (pre_ref[x, y] + weight_of(mask_ref, x, y) * beside).astype(
-                jnp.bfloat16
-            )
+            outside = []
+            if x + 1 == rows:
+                outside.append(below_ref[0, y])
+            if x == 0:
+                outside.append(above_ref[0, y])
+            if y + 1 == columns:
+                outside.append(right_ref[x, 0])
+            if y == 0:
+                outside.append(left_ref[x, 0])
+            value = pre_ref[x, y]
+            if outside:
+                halo = outside[0].astype(jnp.float32)
+                for term in outside[1:]:
+                    halo = halo + term.astype(jnp.float32)
+                value = value + weight_of(mask_ref, x, y) * halo
+            packed_ref[x, y] = value.astype(jnp.bfloat16)
     out_ref[...] = field_ref[...]
     deposit_patches(anchor_ref, count_ref, packed_ref, inv_ref, out_ref)
 
@@ -113,18 +128,18 @@
     )(anchors, count.reshape(1), mask, src, inverse)
 
 
-def operator_part(load, field, operator, stiffness):
+def operator_part(load, field, operator, stiffness, mask):
     rows, columns, depth, loads = field.shape
     flops = 2 * rows * columns * depth * depth * loads * 6
     return pl.pallas_call(
         operator_kernel,
         out_shape=jax.ShapeDtypeStruct(field.shape, jnp.float32),
-        in_specs=[SMEM, VMEM, VMEM, VMEM],
+        in_specs=[SMEM, SMEM, VMEM, VMEM, VMEM],
         out_specs=VMEM,
         cost_estimate=pl.CostEstimate(
             flops=flops, bytes_accessed=3 * field.size * 4, transcendentals=0
         ),
-    )(stiffness, load, field, operator)
+    )(mask, stiffness, load, field, operator)
 
 
 def later_sweep(pre, field, halos, inverse, anchors, count, mask):
@@ -161,7 +176,7 @@
             shifted_in(right, "gy", True),
             shifted_in(left, "gy", False),
         )
-        pre = operator_part(load_field, field, column_operator, stiffness)
+        pre = operator_part(load_field, field, column_operator, stiffness, fault_mask)
         field = later_sweep(pre, field, halos, inverse, anchors, count, fault_mask)
     return field
 

time: 34.3 us -> 33.5 us (0.977)
  Pallas kernels: 11.1 us -> 9.85 us
    pallas_call x1, Pallas kernels: 4.06 us -> 3.31 us  [later_sweep(): pl.pallas_call(later_sweep_kernel, out_shape=jax.ShapeDtypeStruct(field.s...]
    pallas_call x1, Pallas kernels: 3.47 us -> 2.93 us  [first_sweep(): pl.pallas_call(first_sweep_kernel, out_shape=(jax.ShapeDtypeStruct(src.sh...]
  transfers between devices with their start and end apart: 4 -> 4, of which waited for: 1 -> 1; matrix products, arithmetic and copies ran while one was open for 0% -> 0% of each run, Pallas kernels for 10% -> 11%
where the time goes in v8:
time: 33.5 us; the launch traced here: 33.1 us
  starting transfers between devices  19.9 us (59%)
  Pallas kernels  9.85 us (29%)
  waiting for transfers between devices  1.9 us (6%)
  between operations  0.71 us (2%)
  local copies, waits for them, and re-layouts  0.7 us (2%)
    ppermute x4, starting transfers between devices, shifted_in(): return lax.ppermute(edge, axis, pairs)  19.9 us
    pallas_call x1, Pallas kernels, operator_part(): pl.pallas_call(operator_kernel, out_shape=jax.ShapeDtypeStruct(field.shap...  3.61 us
    pallas_call x1, Pallas kernels, later_sweep(): pl.pallas_call(later_sweep_kernel, out_shape=jax.ShapeDtypeStruct(field.s...  3.31 us
    pallas_call x1, Pallas kernels, first_sweep(): pl.pallas_call(first_sweep_kernel, out_shape=(jax.ShapeDtypeStruct(src.sh...  2.93 us
    ppermute x4, waiting for transfers between devices, shifted_in(): return lax.ppermute(edge, axis, pairs)  1.9 us
    unnamed x8, local copies, waits for them, and re-layouts  0.7 us
  transfers between devices with their start and end apart: 4, of which 1 were waited for; matrix products, arithmetic and copies ran while one was open for 0% of the time, Pallas kernels for 11%

profile of v8, /device:TPU:1, one launch (start us, length us, event | category | flops | bytes accessed | tf_op | source)
XLA Modules:
  0.0 33.1 jit_solution(9837701481394841356)
XLA Ops:
  0.7 2.9 %shard_map.73 = (f32[4,8,64,128]{3,2,1,0:T(8,128)}, bf16[1,8,64,128]{3,2,1,0:T(8,128)(2,1)}, bf16[1,8,64,128]{3,2,1,0:T(8,128)(2,1)}, bf16[4,1,64,128]{3,2,1,0:T(8,128)(2,1)}, bf16[4,1,64,128]{3,2,1,0:T(8,128)(2,1)}) custom-call(s32[8]{0:T(128)} %bitcast.7, s32[1]{0:T(128)} %bitcast.3.count_ref, s32[4,8]{1,0:T(4,128)} %mask_ref.5, ...), custom_call_target="tpu_custom_call" | custom-call | tf_op jit(solution)/shard_map/pallas_call | solution.py:120
  3.6 4.7 %collective-permute-start = (bf16[1,8,64,128]{3,2,1,0:T(8,128)(2,1)}, bf16[1,8,64,128]{3,2,1,0:T(8,128)(2,1)S(1)}, u32[]{:S(2)}, u32[]{:S(2)}) collective-permute-start(bf16[1,8,64,128]{3,2,1,0:T(8,128)(2,1)} %get-tuple-element.11), channel_id=1, source_target_pairs={{0,32},{32,64},{64,96},{96,128},{128,160},{160,192},{192,224},{224... | collective-permute-start | bytes 393224 | tf_op jit(solution)/shard_map/ppermute | solution.py:161
  8.3 12.6 %collective-permute-start.1 = (bf16[1,8,64,128]{3,2,1,0:T(8,128)(2,1)}, bf16[1,8,64,128]{3,2,1,0:T(8,128)(2,1)S(1)}, u32[]{:S(2)}, u32[]{:S(2)}) collective-permute-start(bf16[1,8,64,128]{3,2,1,0:T(8,128)(2,1)} %get-tuple-element.12), channel_id=1, source_target_pairs={{32,0},{64,32},{96,64},{128,96},{160,128},{192,160},{224,192},{256... | collective-permute-start | bytes 393224 | tf_op jit(solution)/shard_map/ppermute | solution.py:161
  20.9 1.3 %collective-permute-start.2 = (bf16[4,1,64,128]{3,2,1,0:T(8,128)(2,1)}, bf16[4,1,64,128]{3,2,1,0:T(8,128)(2,1)S(1)}, u32[]{:S(2)}, u32[]{:S(2)}) collective-permute-start(bf16[4,1,64,128]{3,2,1,0:T(8,128)(2,1)} %get-tuple-element.13), channel_id=1, source_target_pairs={{0,1},{1,2},{2,3},{3,4},{4,5},{5,6},{6,7},{7,8},{8,9},{9,10},{10,1... | collective-permute-start | bytes 196616 | tf_op jit(solution)/shard_map/ppermute | solution.py:161
  22.2 1.3 %collective-permute-start.3 = (bf16[4,1,64,128]{3,2,1,0:T(8,128)(2,1)}, bf16[4,1,64,128]{3,2,1,0:T(8,128)(2,1)S(1)}, u32[]{:S(2)}, u32[]{:S(2)}) collective-permute-start(bf16[4,1,64,128]{3,2,1,0:T(8,128)(2,1)} %get-tuple-element.14), channel_id=1, source_target_pairs={{1,0},{2,1},{3,2},{4,3},{5,4},{6,5},{7,6},{8,7},{9,8},{10,9},{11,1... | collective-permute-start | bytes 196616 | tf_op jit(solution)/shard_map/ppermute | solution.py:161
  23.5 3.6 %shard_map.74.pre_ref = f32[4,8,64,128]{3,2,1,0:T(8,128)} custom-call(s32[4,8]{1,0:T(4,128)} %mask_ref.5, f32[4,8]{1,0:T(4,128)} %stiffness_ref.1, f32[4,8,64,128]{3,2,1,0:T(8,128)} %load_ref.1, f32[4,8,64,128]{3,2,1,0:T(8,128)} %get-tuple-element.10.field_ref, f32[64,64]{1,0:T(8,128)} %operator_ref.1), custom_call_target="tpu_custom_call" | custom-call | flops 201326592 | bytes 3145728 | tf_op jit(solution)/shard_map/pallas_call | solution.py:134
  27.2 0.0 collective-permute-done.2.left_ref
  27.2 0.0 copy-start.2
  27.2 1.9 %collective-permute-done.3.right_ref = bf16[4,1,64,128]{3,2,1,0:T(8,128)(2,1)S(1)} collective-permute-done((bf16[4,1,64,128]{3,2,1,0:T(8,128)(2,1)}, bf16[4,1,64,128]{3,2,1,0:T(8,128)(2,1)S(1)}, u32[]{:S(2)}, u32[]{:S(2)}) %collective-permute-start.3) | collective-permute-done | bytes 65568 | tf_op jit(solution)/shard_map/ppermute | solution.py:161
  29.1 0.0 copy-start.3
  29.1 0.0 collective-permute-done.above_ref
  29.1 0.0 copy-start
  29.1 0.0 collective-permute-done.1.below_ref
  29.1 0.0 copy-start.1
  29.1 0.0 copy-done.2
  29.1 0.6 %copy-done.3 = bf16[4,1,64,128]{3,2,1,0:T(8,128)(2,1)} copy-done((bf16[4,1,64,128]{3,2,1,0:T(8,128)(2,1)}, bf16[4,1,64,128]{3,2,1,0:T(8,128)(2,1)S(1)}, u32[]{:S(2)}) %copy-start.3) | copy-done | bytes 65560
  29.7 0.1 copy-done
  29.7 0.0 copy-done.1
  29.8 3.3 %shard_map.75 = f32[4,8,64,128]{3,2,1,0:T(8,128)} custom-call(s32[8]{0:T(128)} %bitcast.8, s32[1]{0:T(128)} %bitcast.4.count_ref, s32[4,8]{1,0:T(4,128)} %mask_ref.5, f32[4,8,64,128]{3,2,1,0:T(8,128)} %shard_map.74.pre_ref, f32[4,8,64,128]{3,2,1,0:T(8,128)} %get-tuple-element.10.field_ref, bf16[1,8,64,128]{3,2,1,0:T(8,128)(2,1)} %copy-done, ...), custom_call_target="tpu_custom_call" | custom-call | tf_op jit(solution)/shard_map/pallas_call | solution.py:146
Async XLA Ops:
  3.6 25.5 %collective-permute-start = (bf16[1,8,64,128]{3,2,1,0:T(8,128)(2,1)}, bf16[1,8,64,128]{3,2,1,0:T(8,128)(2,1)S(1)}, u32[]{:S(2)}, u32[]{:S(2)}) collective-permute-start(bf16[1,8,64,128]{3,2,1,0:T(8,128)(2,1)} %get-tuple-element.11), channel_id=1, source_target_pairs={{0,32},{32,64},{64,96},{96,128},{128,160},{160,192},{192,224},{224... | collective-permute-start | bytes 393224 | tf_op jit(solution)/shard_map/ppermute | solution.py:161
  8.3 20.8 %collective-permute-start.1 = (bf16[1,8,64,128]{3,2,1,0:T(8,128)(2,1)}, bf16[1,8,64,128]{3,2,1,0:T(8,128)(2,1)S(1)}, u32[]{:S(2)}, u32[]{:S(2)}) collective-permute-start(bf16[1,8,64,128]{3,2,1,0:T(8,128)(2,1)} %get-tuple-element.12), channel_id=1, source_target_pairs={{32,0},{64,32},{96,64},{128,96},{160,128},{192,160},{224,192},{256... | collective-permute-start | bytes 393224 | tf_op jit(solution)/shard_map/ppermute | solution.py:161
  20.9 6.2 %collective-permute-start.2 = (bf16[4,1,64,128]{3,2,1,0:T(8,128)(2,1)}, bf16[4,1,64,128]{3,2,1,0:T(8,128)(2,1)S(1)}, u32[]{:S(2)}, u32[]{:S(2)}) collective-permute-start(bf16[4,1,64,128]{3,2,1,0:T(8,128)(2,1)} %get-tuple-element.13), channel_id=1, source_target_pairs={{0,1},{1,2},{2,3},{3,4},{4,5},{5,6},{6,7},{7,8},{8,9},{9,10},{10,1... | collective-permute-start | bytes 196616 | tf_op jit(solution)/shard_map/ppermute | solution.py:161
  22.2 6.8 %collective-permute-start.3 = (bf16[4,1,64,128]{3,2,1,0:T(8,128)(2,1)}, bf16[4,1,64,128]{3,2,1,0:T(8,128)(2,1)S(1)}, u32[]{:S(2)}, u32[]{:S(2)}) collective-permute-start(bf16[4,1,64,128]{3,2,1,0:T(8,128)(2,1)} %get-tuple-element.14), channel_id=1, source_target_pairs={{1,0},{2,1},{3,2},{4,3},{5,4},{6,5},{7,6},{8,7},{9,8},{10,9},{11,1... | collective-permute-start | bytes 196616 | tf_op jit(solution)/shard_map/ppermute | solution.py:161
  27.2 1.9 %copy-start.2 = (bf16[4,1,64,128]{3,2,1,0:T(8,128)(2,1)}, bf16[4,1,64,128]{3,2,1,0:T(8,128)(2,1)S(1)}, u32[]{:S(2)}) copy-start(bf16[4,1,64,128]{3,2,1,0:T(8,128)(2,1)S(1)} %collective-permute-done.2.left_ref) | copy-start | bytes 196612
  29.1 0.6 %copy-start.3 = (bf16[4,1,64,128]{3,2,1,0:T(8,128)(2,1)}, bf16[4,1,64,128]{3,2,1,0:T(8,128)(2,1)S(1)}, u32[]{:S(2)}) copy-start(bf16[4,1,64,128]{3,2,1,0:T(8,128)(2,1)S(1)} %collective-permute-done.3.right_ref) | copy-start | bytes 196612
  29.1 0.7 %copy-start = (bf16[1,8,64,128]{3,2,1,0:T(8,128)(2,1)}, bf16[1,8,64,128]{3,2,1,0:T(8,128)(2,1)S(1)}, u32[]{:S(2)}) copy-start(bf16[1,8,64,128]{3,2,1,0:T(8,128)(2,1)S(1)} %collective-permute-done.above_ref) | copy-start | bytes 393220
  29.1 0.7 %copy-start.1 = (bf16[1,8,64,128]{3,2,1,0:T(8,128)(2,1)}, bf16[1,8,64,128]{3,2,1,0:T(8,128)(2,1)S(1)}, u32[]{:S(2)}) copy-start(bf16[1,8,64,128]{3,2,1,0:T(8,128)(2,1)S(1)} %collective-permute-done.1.below_ref) | copy-start | bytes 393220

commit v9 on v8

--- a/solution.py
+++ b/solution.py
@@ -82,29 +82,7 @@
             pre_ref[x, y] = load_ref[x, y] - (operated - weight_of(mask_ref, x, y) * beside)
 
 
-def later_sweep_kernel(
-    anchor_ref, count_ref, mask_ref, pre_ref, field_ref,
-    above_ref, below_ref, left_ref, right_ref, inv_ref, out_ref, packed_ref,
-):
-    rows, columns = field_ref.shape[:2]
-    for x in range(rows):
-        for y in range(columns):
-            outside = []
-            if x + 1 == rows:
-                outside.append(below_ref[0, y])
-            if x == 0:
-                outside.append(above_ref[0, y])
-            if y + 1 == columns:
-                outside.append(right_ref[x, 0])
-            if y == 0:
-                outside.append(left_ref[x, 0])
-            value = pre_ref[x, y]
-            if outside:
-                halo = outside[0].astype(jnp.float32)
-                for term in outside[1:]:
-                    halo = halo + term.astype(jnp.float32)
-                value = value + weight_of(mask_ref, x, y) * halo
-            packed_ref[x, y] = value.astype(jnp.bfloat16)
+def later_sweep_kernel(anchor_ref, count_ref, packed_ref, field_ref, inv_ref, out_ref):
     out_ref[...] = field_ref[...]
     deposit_patches(anchor_ref, count_ref, packed_ref, inv_ref, out_ref)
 
@@ -142,14 +120,26 @@
     )(mask, stiffness, load, field, operator)
 
 
-def later_sweep(pre, field, halos, inverse, anchors, count, mask):
+def later_sweep(packed, field, inverse, anchors, count):
     return pl.pallas_call(
         later_sweep_kernel,
         out_shape=jax.ShapeDtypeStruct(field.shape, jnp.float32),
-        in_specs=[SMEM, SMEM, SMEM] + [VMEM] * 7,
+        in_specs=[SMEM, SMEM, VMEM, VMEM, VMEM],
         out_specs=VMEM,
-        scratch_shapes=[pltpu.VMEM(field.shape, jnp.bfloat16)],
-    )(anchors, count.reshape(1), mask, pre, field, *halos, inverse)
+    )(anchors, count.reshape(1), packed, field, inverse)
+
+
+def with_halos(pre, halos, mask):
+    rows, columns = pre.shape[:2]
+    above, below, left, right = (halo.astype(jnp.float32) for halo in halos)
+    outside = (
+        jnp.pad(below, ((rows - 1, 0), (0, 0), (0, 0), (0, 0)))
+        + jnp.pad(above, ((0, rows - 1), (0, 0), (0, 0), (0, 0)))
+        + jnp.pad(right, ((0, 0), (columns - 1, 0), (0, 0), (0, 0)))
+        + jnp.pad(left, ((0, 0), (0, columns - 1), (0, 0), (0, 0)))
+    )
+    weight = 1.0 - 0.6 * mask.astype(jnp.float32)
+    return (pre + weight[:, :, None, None] * outside).astype(jnp.bfloat16)
 
 
 def shifted_in(edge, axis, forward):
@@ -177,7 +167,8 @@
             shifted_in(left, "gy", False),
         )
         pre = operator_part(load_field, field, column_operator, stiffness, fault_mask)
-        field = later_sweep(pre, field, halos, inverse, anchors, count, fault_mask)
+        packed = with_halos(pre, halos, fault_mask)
+        field = later_sweep(packed, field, inverse, anchors, count)
     return field
 
 

time: 33.5 us -> 38 us (1.13)
  starting transfers between devices: 19.9 us -> 24.9 us
  other arithmetic: 0 us -> 2.22 us
  waiting for transfers between devices: 1.9 us -> 0.01 us
  local copies, waits for them, and re-layouts: 0.7 us -> 0.01 us
    ppermute x4, starting transfers between devices: 19.9 us -> 24.9 us  [shifted_in(): return lax.ppermute(edge, axis, pairs)]
    convert_element_type x0 -> x1, other arithmetic: none -> 2.22 us  [with_halos(): return (pre + weight[:, :, None, None] * outside).astype(jnp.bfloat16)]
    ppermute x4, waiting for transfers between devices: 1.9 us -> 0.01 us  [shifted_in(): return lax.ppermute(edge, axis, pairs)]
    unnamed x8 -> x2, local copies, waits for them, and re-layouts: 0.7 us -> 0.01 us
  transfers between devices with their start and end apart: 4 -> 4, of which waited for: 1 -> 0; matrix products, arithmetic and copies ran while one was open for 0% -> 0% of each run, Pallas kernels for 11% -> 9%
where the time goes in v9:
time: 38 us; the launch traced here: 37.7 us
  starting transfers between devices  24.9 us (66%)
  Pallas kernels  9.83 us (26%)
  other arithmetic  2.22 us (6%)
  between operations  0.73 us (2%)
    ppermute x4, starting transfers between devices, shifted_in(): return lax.ppermute(edge, axis, pairs)  24.9 us
    pallas_call x1, Pallas kernels, operator_part(): pl.pallas_call(operator_kernel, out_shape=jax.ShapeDtypeStruct(field.shap...  3.54 us
    pallas_call x1, Pallas kernels, first_sweep(): pl.pallas_call(first_sweep_kernel, out_shape=(jax.ShapeDtypeStruct(src.sh...  3.15 us
    pallas_call x1, Pallas kernels, later_sweep(): pl.pallas_call(later_sweep_kernel, out_shape=jax.ShapeDtypeStruct(field.s...  3.14 us
    convert_element_type x1, other arithmetic, with_halos(): return (pre + weight[:, :, None, None] * outside).astype(jnp.bfloat16)  2.22 us
  transfers between devices with their start and end apart: 4, of which 0 were waited for; matrix products, arithmetic and copies ran while one was open for 0% of the time, Pallas kernels for 9%

profile of v9, /device:TPU:1, one launch (start us, length us, event | category | flops | bytes accessed | tf_op | source)
XLA Modules:
  0.0 37.7 jit_solution(13683494563623132978)
XLA Ops:
  0.7 3.2 %shard_map.73 = (f32[4,8,64,128]{3,2,1,0:T(8,128)}, bf16[1,8,64,128]{3,2,1,0:T(8,128)(2,1)}, bf16[1,8,64,128]{3,2,1,0:T(8,128)(2,1)}, bf16[4,1,64,128]{3,2,1,0:T(8,128)(2,1)}, bf16[4,1,64,128]{3,2,1,0:T(8,128)(2,1)}) custom-call(s32[8]{0:T(128)} %bitcast.7, s32[1]{0:T(128)} %bitcast.3.count_ref, s32[4,8]{1,0:T(4,128)} %mask_ref.3, ...), custom_call_target="tpu_custom_call" | custom-call | tf_op jit(solution)/shard_map/pallas_call | solution.py:98
  3.8 1.3 %collective-permute-start.2 = (bf16[4,1,64,128]{3,2,1,0:T(8,128)(2,1)}, bf16[4,1,64,128]{3,2,1,0:T(8,128)(2,1)S(1)}, u32[]{:S(2)}, u32[]{:S(2)}) collective-permute-start(bf16[4,1,64,128]{3,2,1,0:T(8,128)(2,1)} %get-tuple-element.13), channel_id=1, source_target_pairs={{1,0},{2,1},{3,2},{4,3},{5,4},{6,5},{7,6},{8,7},{9,8},{10,9},{11,1... | collective-permute-start | bytes 196616 | tf_op jit(solution)/shard_map/ppermute | solution.py:151
  5.1 0.0 copy-start
  5.1 6.1 %collective-permute-start.3 = (bf16[4,1,64,128]{3,2,1,0:T(8,128)(2,1)}, bf16[4,1,64,128]{3,2,1,0:T(8,128)(2,1)S(1)}, u32[]{:S(2)}, u32[]{:S(2)}) collective-permute-start(bf16[4,1,64,128]{3,2,1,0:T(8,128)(2,1)} %get-tuple-element.14), channel_id=1, source_target_pairs={{0,1},{1,2},{2,3},{3,4},{4,5},{5,6},{6,7},{7,8},{8,9},{9,10},{10,1... | collective-permute-start | bytes 196616 | tf_op jit(solution)/shard_map/ppermute | solution.py:151
  11.2 15.6 %collective-permute-start = (bf16[1,8,64,128]{3,2,1,0:T(8,128)(2,1)}, bf16[1,8,64,128]{3,2,1,0:T(8,128)(2,1)S(1)}, u32[]{:S(2)}, u32[]{:S(2)}) collective-permute-start(bf16[1,8,64,128]{3,2,1,0:T(8,128)(2,1)} %get-tuple-element.11), channel_id=1, source_target_pairs={{32,0},{64,32},{96,64},{128,96},{160,128},{192,160},{224,192},{256... | collective-permute-start | bytes 393224 | tf_op jit(solution)/shard_map/ppermute | solution.py:151
  26.8 1.9 %collective-permute-start.1 = (bf16[1,8,64,128]{3,2,1,0:T(8,128)(2,1)}, bf16[1,8,64,128]{3,2,1,0:T(8,128)(2,1)S(1)}, u32[]{:S(2)}, u32[]{:S(2)}) collective-permute-start(bf16[1,8,64,128]{3,2,1,0:T(8,128)(2,1)} %get-tuple-element.12), channel_id=1, source_target_pairs={{0,32},{32,64},{64,96},{96,128},{128,160},{160,192},{192,224},{224... | collective-permute-start | bytes 393224 | tf_op jit(solution)/shard_map/ppermute | solution.py:151
  28.7 0.0 copy-done
  28.8 3.5 %shard_map.74 = f32[4,8,64,128]{3,2,1,0:T(8,128)} custom-call(s32[4,8]{1,0:T(4,128)} %mask_ref.3, f32[4,8]{1,0:T(4,128)} %stiffness_ref.1, f32[4,8,64,128]{3,2,1,0:T(8,128)} %load_ref.1, f32[4,8,64,128]{3,2,1,0:T(8,128)} %get-tuple-element.10.field_ref, f32[64,64]{1,0:T(8,128)} %operator_ref.1), custom_call_target="tpu_custom_call" | custom-call | flops 201326592 | bytes 3145728 | tf_op jit(solution)/shard_map/pallas_call | solution.py:112
  32.3 0.0 collective-permute-done.2
  32.3 0.0 collective-permute-done.3
  32.3 0.0 collective-permute-done
  32.3 0.0 collective-permute-done.1
  32.3 2.2 %add_convert_fusion.packed_ref = bf16[4,8,64,128]{3,2,1,0:T(8,128)(2,1)} fusion(f32[4,8,64,128]{3,2,1,0:T(8,128)} %shard_map.74, bf16[4,1,64,128]{3,2,1,0:T(8,128)(2,1)S(1)} %collective-permute-done.3, bf16[4,1,64,128]{3,2,1,0:T(8,128)(2,1)S(1)} %collective-permute-done.2, bf16[1,8,64,128]{3,2,1,0:T(8,128)(2,1)S(1)} %collective-permute-done.1, ...), kind=kLoop, calls=%fused_computation | loop fusion | flops 2621440 | bytes 1966208 | tf_op jit(solution)/shard_map/convert_element_type | solution.py:142
  34.6 3.1 %shard_map.75 = f32[4,8,64,128]{3,2,1,0:T(8,128)} custom-call(s32[8]{0:T(128)} %bitcast.8, s32[1]{0:T(128)} %bitcast.4.count_ref, bf16[4,8,64,128]{3,2,1,0:T(8,128)(2,1)} %add_convert_fusion.packed_ref, f32[4,8,64,128]{3,2,1,0:T(8,128)} %get-tuple-element.10.field_ref, bf16[8,256,256]{2,1,0:T(8,128)(2,1)} %bitcast.6), custom_call_target="tpu_custom_call" | custom-call | tf_op jit(solution)/shard_map/pallas_call | solution.py:124
  (1 shorter events, 0.0 us)
Async XLA Ops:
  3.8 28.5 %collective-permute-start.2 = (bf16[4,1,64,128]{3,2,1,0:T(8,128)(2,1)}, bf16[4,1,64,128]{3,2,1,0:T(8,128)(2,1)S(1)}, u32[]{:S(2)}, u32[]{:S(2)}) collective-permute-start(bf16[4,1,64,128]{3,2,1,0:T(8,128)(2,1)} %get-tuple-element.13), channel_id=1, source_target_pairs={{1,0},{2,1},{3,2},{4,3},{5,4},{6,5},{7,6},{8,7},{9,8},{10,9},{11,1... | collective-permute-start | bytes 196616 | tf_op jit(solution)/shard_map/ppermute | solution.py:151
  5.1 23.7 %copy-start = (s32[4,8]{1,0:T(4,128)S(1)}, s32[4,8]{1,0:T(4,128)}, u32[]{:S(2)}) copy-start(s32[4,8]{1,0:T(4,128)} %mask_ref.3) | copy-start | bytes 388
  5.1 27.2 %collective-permute-start.3 = (bf16[4,1,64,128]{3,2,1,0:T(8,128)(2,1)}, bf16[4,1,64,128]{3,2,1,0:T(8,128)(2,1)S(1)}, u32[]{:S(2)}, u32[]{:S(2)}) collective-permute-start(bf16[4,1,64,128]{3,2,1,0:T(8,128)(2,1)} %get-tuple-element.14), channel_id=1, source_target_pairs={{0,1},{1,2},{2,3},{3,4},{4,5},{5,6},{6,7},{7,8},{8,9},{9,10},{10,1... | collective-permute-start | bytes 196616 | tf_op jit(solution)/shard_map/ppermute | solution.py:151
  11.2 21.1 %collective-permute-start = (bf16[1,8,64,128]{3,2,1,0:T(8,128)(2,1)}, bf16[1,8,64,128]{3,2,1,0:T(8,128)(2,1)S(1)}, u32[]{:S(2)}, u32[]{:S(2)}) collective-permute-start(bf16[1,8,64,128]{3,2,1,0:T(8,128)(2,1)} %get-tuple-element.11), channel_id=1, source_target_pairs={{32,0},{64,32},{96,64},{128,96},{160,128},{192,160},{224,192},{256... | collective-permute-start | bytes 393224 | tf_op jit(solution)/shard_map/ppermute | solution.py:151
  26.8 5.5 %collective-permute-start.1 = (bf16[1,8,64,128]{3,2,1,0:T(8,128)(2,1)}, bf16[1,8,64,128]{3,2,1,0:T(8,128)(2,1)S(1)}, u32[]{:S(2)}, u32[]{:S(2)}) collective-permute-start(bf16[1,8,64,128]{3,2,1,0:T(8,128)(2,1)} %get-tuple-element.12), channel_id=1, source_target_pairs={{0,32},{32,64},{64,96},{96,128},{128,160},{160,192},{192,224},{224... | collective-permute-start | bytes 393224 | tf_op jit(solution)/shard_map/ppermute | solution.py:151

commit v10 on v8

--- a/solution.py
+++ b/solution.py
@@ -13,6 +13,26 @@
 
 def weight_of(mask_ref, x, y):
     return 1.0 - 0.6 * mask_ref[x, y].astype(jnp.float32)
+
+
+def fetch_inverse(count_ref, inv_hbm, inv_ref, sem):
+    slots = inv_ref.shape[0]
+    half = slots // 2
+    count = count_ref[0]
+
+    @pl.when(count > half)
+    def _():
+        copy = pltpu.make_async_copy(inv_hbm, inv_ref, sem)
+        copy.start()
+        copy.wait()
+
+    @pl.when(count <= half)
+    def _():
+        copy = pltpu.make_async_copy(
+            inv_hbm.at[pl.ds(0, half)], inv_ref.at[pl.ds(0, half)], sem
+        )
+        copy.start()
+        copy.wait()
 
 
 def deposit_patches(anchor_ref, count_ref, src_ref, inv_ref, acc_ref):
@@ -41,12 +61,13 @@
 
 
 def first_sweep_kernel(
-    anchor_ref, count_ref, mask_ref, src_ref, inv_ref,
-    out_ref, top_ref, bottom_ref, left_ref, right_ref,
+    anchor_ref, count_ref, mask_ref, src_ref, inv_hbm,
+    out_ref, top_ref, bottom_ref, left_ref, right_ref, inv_ref, sem,
 ):
     rows, columns = src_ref.shape[:2]
     acc_ref = out_ref
     acc_ref[...] = jnp.zeros(acc_ref.shape, jnp.float32)
+    fetch_inverse(count_ref, inv_hbm, inv_ref, sem)
     deposit_patches(anchor_ref, count_ref, src_ref, inv_ref, acc_ref)
     for y in range(columns):
         top_ref[0, y] = (weight_of(mask_ref, 0, y) * acc_ref[0, y]).astype(top_ref.dtype)
@@ -84,9 +105,10 @@
 
 def later_sweep_kernel(
     anchor_ref, count_ref, mask_ref, pre_ref, field_ref,
-    above_ref, below_ref, left_ref, right_ref, inv_ref, out_ref, packed_ref,
+    above_ref, below_ref, left_ref, right_ref, inv_hbm, out_ref, inv_ref, sem, packed_ref,
 ):
     rows, columns = field_ref.shape[:2]
+    fetch_inverse(count_ref, inv_hbm, inv_ref, sem)
     for x in range(rows):
         for y in range(columns):
             outside = []
@@ -111,6 +133,7 @@
 
 SMEM = pl.BlockSpec(memory_space=pltpu.SMEM)
 VMEM = pl.BlockSpec(memory_space=pltpu.VMEM)
+ANY = pl.BlockSpec(memory_space=pl.ANY)
 
 
 def first_sweep(src, inverse, anchors, count, mask):
@@ -123,8 +146,12 @@
             jax.ShapeDtypeStruct(src.shape, jnp.float32),
             row_edge, row_edge, column_edge, column_edge,
         ),
-        in_specs=[SMEM, SMEM, SMEM, VMEM, VMEM],
+        in_specs=[SMEM, SMEM, SMEM, VMEM, ANY],
         out_specs=(VMEM,) * 5,
+        scratch_shapes=[
+            pltpu.VMEM(inverse.shape, inverse.dtype),
+            pltpu.SemaphoreType.DMA(()),
+        ],
     )(anchors, count.reshape(1), mask, src, inverse)
 
 
@@ -146,9 +173,13 @@
     return pl.pallas_call(
         later_sweep_kernel,
         out_shape=jax.ShapeDtypeStruct(field.shape, jnp.float32),
-        in_specs=[SMEM, SMEM, SMEM] + [VMEM] * 7,
+        in_specs=[SMEM, SMEM, SMEM] + [VMEM] * 6 + [ANY],
         out_specs=VMEM,
-        scratch_shapes=[pltpu.VMEM(field.shape, jnp.bfloat16)],
+        scratch_shapes=[
+            pltpu.VMEM(inverse.shape, inverse.dtype),
+            pltpu.SemaphoreType.DMA(()),
+            pltpu.VMEM(field.shape, jnp.bfloat16),
+        ],
     )(anchors, count.reshape(1), mask, pre, field, *halos, inverse)
 
 

time: 33.5 us -> 35.9 us (1.072)
  Pallas kernels: 9.85 us -> 12.3 us
    pallas_call x1, Pallas kernels: 2.93 us -> 4.21 us  [first_sweep(): pl.pallas_call(first_sweep_kernel, out_shape=(jax.ShapeDtypeStruct(src.sh...]
    pallas_call x1, Pallas kernels: 3.31 us -> 4.52 us  [later_sweep(): pl.pallas_call(later_sweep_kernel, out_shape=jax.ShapeDtypeStruct(field.s...]
  transfers between devices with their start and end apart: 4 -> 4, of which waited for: 1 -> 1; matrix products, arithmetic and copies ran while one was open for 0% -> 0% of each run, Pallas kernels for 11% -> 10%
where the time goes in v10:
time: 35.9 us; the launch traced here: 35.6 us
  starting transfers between devices  19.9 us (55%)
  Pallas kernels  12.3 us (34%)
  waiting for transfers between devices  1.9 us (5%)
  between operations  0.72 us (2%)
  local copies, waits for them, and re-layouts  0.7 us (2%)
    ppermute x4, starting transfers between devices, shifted_in(): return lax.ppermute(edge, axis, pairs)  19.9 us
    pallas_call x1, Pallas kernels, later_sweep(): pl.pallas_call(later_sweep_kernel, out_shape=jax.ShapeDtypeStruct(field.s...  4.52 us
    pallas_call x1, Pallas kernels, first_sweep(): pl.pallas_call(first_sweep_kernel, out_shape=(jax.ShapeDtypeStruct(src.sh...  4.21 us
    pallas_call x1, Pallas kernels, operator_part(): pl.pallas_call(operator_kernel, out_shape=jax.ShapeDtypeStruct(field.shap...  3.61 us
    ppermute x4, waiting for transfers between devices, shifted_in(): return lax.ppermute(edge, axis, pairs)  1.9 us
  transfers between devices with their start and end apart: 4, of which 1 were waited for; matrix products, arithmetic and copies ran while one was open for 0% of the time, Pallas kernels for 10%

profile of v10, /device:TPU:1, one launch (start us, length us, event | category | flops | bytes accessed | tf_op | source)
XLA Modules:
  0.0 35.6 jit_solution(16490885649139931869)
XLA Ops:
  0.7 4.2 %shard_map.73 = (f32[4,8,64,128]{3,2,1,0:T(8,128)}, bf16[1,8,64,128]{3,2,1,0:T(8,128)(2,1)}, bf16[1,8,64,128]{3,2,1,0:T(8,128)(2,1)}, bf16[4,1,64,128]{3,2,1,0:T(8,128)(2,1)}, bf16[4,1,64,128]{3,2,1,0:T(8,128)(2,1)}) custom-call(s32[8]{0:T(128)} %bitcast.7, s32[1]{0:T(128)} %bitcast.3.count_ref, s32[4,8]{1,0:T(4,128)} %mask_ref.5, ...), custom_call_target="tpu_custom_call" | custom-call | tf_op jit(solution)/shard_map/pallas_call | solution.py:143
  4.9 4.5 %collective-permute-start = (bf16[1,8,64,128]{3,2,1,0:T(8,128)(2,1)}, bf16[1,8,64,128]{3,2,1,0:T(8,128)(2,1)S(1)}, u32[]{:S(2)}, u32[]{:S(2)}) collective-permute-start(bf16[1,8,64,128]{3,2,1,0:T(8,128)(2,1)} %get-tuple-element.11), channel_id=1, source_target_pairs={{0,32},{32,64},{64,96},{96,128},{128,160},{160,192},{192,224},{224... | collective-permute-start | bytes 393224 | tf_op jit(solution)/shard_map/ppermute | solution.py:192
  9.4 12.8 %collective-permute-start.1 = (bf16[1,8,64,128]{3,2,1,0:T(8,128)(2,1)}, bf16[1,8,64,128]{3,2,1,0:T(8,128)(2,1)S(1)}, u32[]{:S(2)}, u32[]{:S(2)}) collective-permute-start(bf16[1,8,64,128]{3,2,1,0:T(8,128)(2,1)} %get-tuple-element.12), channel_id=1, source_target_pairs={{32,0},{64,32},{96,64},{128,96},{160,128},{192,160},{224,192},{256... | collective-permute-start | bytes 393224 | tf_op jit(solution)/shard_map/ppermute | solution.py:192
  22.2 1.3 %collective-permute-start.2 = (bf16[4,1,64,128]{3,2,1,0:T(8,128)(2,1)}, bf16[4,1,64,128]{3,2,1,0:T(8,128)(2,1)S(1)}, u32[]{:S(2)}, u32[]{:S(2)}) collective-permute-start(bf16[4,1,64,128]{3,2,1,0:T(8,128)(2,1)} %get-tuple-element.13), channel_id=1, source_target_pairs={{0,1},{1,2},{2,3},{3,4},{4,5},{5,6},{6,7},{7,8},{8,9},{9,10},{10,1... | collective-permute-start | bytes 196616 | tf_op jit(solution)/shard_map/ppermute | solution.py:192
  23.5 1.3 %collective-permute-start.3 = (bf16[4,1,64,128]{3,2,1,0:T(8,128)(2,1)}, bf16[4,1,64,128]{3,2,1,0:T(8,128)(2,1)S(1)}, u32[]{:S(2)}, u32[]{:S(2)}) collective-permute-start(bf16[4,1,64,128]{3,2,1,0:T(8,128)(2,1)} %get-tuple-element.14), channel_id=1, source_target_pairs={{1,0},{2,1},{3,2},{4,3},{5,4},{6,5},{7,6},{8,7},{9,8},{10,9},{11,1... | collective-permute-start | bytes 196616 | tf_op jit(solution)/shard_map/ppermute | solution.py:192
  24.8 3.6 %shard_map.74.pre_ref = f32[4,8,64,128]{3,2,1,0:T(8,128)} custom-call(s32[4,8]{1,0:T(4,128)} %mask_ref.5, f32[4,8]{1,0:T(4,128)} %stiffness_ref.1, f32[4,8,64,128]{3,2,1,0:T(8,128)} %load_ref.1, f32[4,8,64,128]{3,2,1,0:T(8,128)} %get-tuple-element.10.field_ref, f32[64,64]{1,0:T(8,128)} %operator_ref.1), custom_call_target="tpu_custom_call" | custom-call | flops 201326592 | bytes 3145728 | tf_op jit(solution)/shard_map/pallas_call | solution.py:161
  28.4 0.0 collective-permute-done.2.left_ref
  28.5 0.0 copy-start.2
  28.5 1.9 %collective-permute-done.3.right_ref = bf16[4,1,64,128]{3,2,1,0:T(8,128)(2,1)S(1)} collective-permute-done((bf16[4,1,64,128]{3,2,1,0:T(8,128)(2,1)}, bf16[4,1,64,128]{3,2,1,0:T(8,128)(2,1)S(1)}, u32[]{:S(2)}, u32[]{:S(2)}) %collective-permute-start.3) | collective-permute-done | bytes 65568 | tf_op jit(solution)/shard_map/ppermute | solution.py:192
  30.3 0.0 copy-start.3
  30.3 0.0 collective-permute-done.above_ref
  30.3 0.0 copy-start
  30.4 0.0 collective-permute-done.1.below_ref
  30.4 0.0 copy-start.1
  30.4 0.0 copy-done.2
  30.4 0.6 %copy-done.3 = bf16[4,1,64,128]{3,2,1,0:T(8,128)(2,1)} copy-done((bf16[4,1,64,128]{3,2,1,0:T(8,128)(2,1)}, bf16[4,1,64,128]{3,2,1,0:T(8,128)(2,1)S(1)}, u32[]{:S(2)}) %copy-start.3) | copy-done | bytes 65560
  31.0 0.1 copy-done
  31.0 0.0 copy-done.1
  31.1 4.5 %shard_map.75 = f32[4,8,64,128]{3,2,1,0:T(8,128)} custom-call(s32[8]{0:T(128)} %bitcast.8, s32[1]{0:T(128)} %bitcast.4.count_ref, s32[4,8]{1,0:T(4,128)} %mask_ref.5, f32[4,8,64,128]{3,2,1,0:T(8,128)} %shard_map.74.pre_ref, f32[4,8,64,128]{3,2,1,0:T(8,128)} %get-tuple-element.10.field_ref, bf16[1,8,64,128]{3,2,1,0:T(8,128)(2,1)} %copy-done, ...), custom_call_target="tpu_custom_call" | custom-call | tf_op jit(solution)/shard_map/pallas_call | solution.py:173
Async XLA Ops:
  4.9 25.5 %collective-permute-start = (bf16[1,8,64,128]{3,2,1,0:T(8,128)(2,1)}, bf16[1,8,64,128]{3,2,1,0:T(8,128)(2,1)S(1)}, u32[]{:S(2)}, u32[]{:S(2)}) collective-permute-start(bf16[1,8,64,128]{3,2,1,0:T(8,128)(2,1)} %get-tuple-element.11), channel_id=1, source_target_pairs={{0,32},{32,64},{64,96},{96,128},{128,160},{160,192},{192,224},{224... | collective-permute-start | bytes 393224 | tf_op jit(solution)/shard_map/ppermute | solution.py:192
  9.4 20.9 %collective-permute-start.1 = (bf16[1,8,64,128]{3,2,1,0:T(8,128)(2,1)}, bf16[1,8,64,128]{3,2,1,0:T(8,128)(2,1)S(1)}, u32[]{:S(2)}, u32[]{:S(2)}) collective-permute-start(bf16[1,8,64,128]{3,2,1,0:T(8,128)(2,1)} %get-tuple-element.12), channel_id=1, source_target_pairs={{32,0},{64,32},{96,64},{128,96},{160,128},{192,160},{224,192},{256... | collective-permute-start | bytes 393224 | tf_op jit(solution)/shard_map/ppermute | solution.py:192
  22.2 6.2 %collective-permute-start.2 = (bf16[4,1,64,128]{3,2,1,0:T(8,128)(2,1)}, bf16[4,1,64,128]{3,2,1,0:T(8,128)(2,1)S(1)}, u32[]{:S(2)}, u32[]{:S(2)}) collective-permute-start(bf16[4,1,64,128]{3,2,1,0:T(8,128)(2,1)} %get-tuple-element.13), channel_id=1, source_target_pairs={{0,1},{1,2},{2,3},{3,4},{4,5},{5,6},{6,7},{7,8},{8,9},{9,10},{10,1... | collective-permute-start | bytes 196616 | tf_op jit(solution)/shard_map/ppermute | solution.py:192
  23.5 6.8 %collective-permute-start.3 = (bf16[4,1,64,128]{3,2,1,0:T(8,128)(2,1)}, bf16[4,1,64,128]{3,2,1,0:T(8,128)(2,1)S(1)}, u32[]{:S(2)}, u32[]{:S(2)}) collective-permute-start(bf16[4,1,64,128]{3,2,1,0:T(8,128)(2,1)} %get-tuple-element.14), channel_id=1, source_target_pairs={{1,0},{2,1},{3,2},{4,3},{5,4},{6,5},{7,6},{8,7},{9,8},{10,9},{11,1... | collective-permute-start | bytes 196616 | tf_op jit(solution)/shard_map/ppermute | solution.py:192
  28.5 1.9 %copy-start.2 = (bf16[4,1,64,128]{3,2,1,0:T(8,128)(2,1)}, bf16[4,1,64,128]{3,2,1,0:T(8,128)(2,1)S(1)}, u32[]{:S(2)}) copy-start(bf16[4,1,64,128]{3,2,1,0:T(8,128)(2,1)S(1)} %collective-permute-done.2.left_ref) | copy-start | bytes 196612
  30.3 0.6 %copy-start.3 = (bf16[4,1,64,128]{3,2,1,0:T(8,128)(2,1)}, bf16[4,1,64,128]{3,2,1,0:T(8,128)(2,1)S(1)}, u32[]{:S(2)}) copy-start(bf16[4,1,64,128]{3,2,1,0:T(8,128)(2,1)S(1)} %collective-permute-done.3.right_ref) | copy-start | bytes 196612
  30.3 0.7 %copy-start = (bf16[1,8,64,128]{3,2,1,0:T(8,128)(2,1)}, bf16[1,8,64,128]{3,2,1,0:T(8,128)(2,1)S(1)}, u32[]{:S(2)}) copy-start(bf16[1,8,64,128]{3,2,1,0:T(8,128)(2,1)S(1)} %collective-permute-done.above_ref) | copy-start | bytes 393220
  30.4 0.7 %copy-start.1 = (bf16[1,8,64,128]{3,2,1,0:T(8,128)(2,1)}, bf16[1,8,64,128]{3,2,1,0:T(8,128)(2,1)S(1)}, u32[]{:S(2)}) copy-start(bf16[1,8,64,128]{3,2,1,0:T(8,128)(2,1)S(1)} %collective-permute-done.1.below_ref) | copy-start | bytes 393220

commit v11 on v8

--- a/solution.py
+++ b/solution.py
@@ -83,21 +83,22 @@
 
 
 def later_sweep_kernel(
-    anchor_ref, count_ref, mask_ref, pre_ref, field_ref,
-    above_ref, below_ref, left_ref, right_ref, inv_ref, out_ref, packed_ref,
+    anchor_ref, count_ref, mask_ref, pre_ref, field_ref, halo_ref, inv_ref, out_ref, packed_ref,
 ):
     rows, columns = field_ref.shape[:2]
+    above_at, below_at = 0, columns
+    left_at, right_at = 2 * columns, 2 * columns + rows
     for x in range(rows):
         for y in range(columns):
             outside = []
             if x + 1 == rows:
-                outside.append(below_ref[0, y])
+                outside.append(halo_ref[below_at + y])
             if x == 0:
-                outside.append(above_ref[0, y])
+                outside.append(halo_ref[above_at + y])
             if y + 1 == columns:
-                outside.append(right_ref[x, 0])
+                outside.append(halo_ref[right_at + x])
             if y == 0:
-                outside.append(left_ref[x, 0])
+                outside.append(halo_ref[left_at + x])
             value = pre_ref[x, y]
             if outside:
                 halo = outside[0].astype(jnp.float32)
@@ -143,13 +144,15 @@
 
 
 def later_sweep(pre, field, halos, inverse, anchors, count, mask):
+    depth, loads = field.shape[2:]
+    halo = jnp.concatenate([h.reshape(-1, depth, loads) for h in halos], axis=0)
     return pl.pallas_call(
         later_sweep_kernel,
         out_shape=jax.ShapeDtypeStruct(field.shape, jnp.float32),
-        in_specs=[SMEM, SMEM, SMEM] + [VMEM] * 7,
+        in_specs=[SMEM, SMEM, SMEM] + [VMEM] * 4,
         out_specs=VMEM,
         scratch_shapes=[pltpu.VMEM(field.shape, jnp.bfloat16)],
-    )(anchors, count.reshape(1), mask, pre, field, *halos, inverse)
+    )(anchors, count.reshape(1), mask, pre, field, halo, inverse)
 
 
 def shifted_in(edge, axis, forward):

time: 33.5 us -> 33.8 us (level)
  other arithmetic: 0 us -> 0.8 us
  local copies, waits for them, and re-layouts: 0.7 us -> 0 us
  Pallas kernels: 9.85 us -> 10.5 us
    concatenate x0 -> x1, other arithmetic: none -> 0.8 us  [later_sweep(): halo = jnp.concatenate([h.reshape(-1, depth, loads) for h in halos], axis=0)]
    unnamed x8 -> x0, local copies, waits for them, and re-layouts: 0.7 us -> none
    ppermute x4, starting transfers between devices: 19.9 us -> 19.6 us  [shifted_in(): return lax.ppermute(edge, axis, pairs)]
    pallas_call x1, Pallas kernels: 3.31 us -> 3.67 us  [later_sweep(): pl.pallas_call(later_sweep_kernel, out_shape=jax.ShapeDtypeStruct(field.s...]
    pallas_call x1, Pallas kernels: 2.93 us -> 3.27 us  [first_sweep(): pl.pallas_call(first_sweep_kernel, out_shape=(jax.ShapeDtypeStruct(src.sh...]
where the time goes in v11:
time: 33.8 us; the launch traced here: 33.5 us
  starting transfers between devices  19.6 us (58%)
  Pallas kernels  10.5 us (31%)
  waiting for transfers between devices  1.92 us (6%)
  other arithmetic  0.8 us (2%)
  between operations  0.69 us (2%)
    ppermute x4, starting transfers between devices, shifted_in(): return lax.ppermute(edge, axis, pairs)  19.6 us
    pallas_call x1, Pallas kernels, later_sweep(): pl.pallas_call(later_sweep_kernel, out_shape=jax.ShapeDtypeStruct(field.s...  3.67 us
    pallas_call x1, Pallas kernels, operator_part(): pl.pallas_call(operator_kernel, out_shape=jax.ShapeDtypeStruct(field.shap...  3.59 us
    pallas_call x1, Pallas kernels, first_sweep(): pl.pallas_call(first_sweep_kernel, out_shape=(jax.ShapeDtypeStruct(src.sh...  3.27 us
    ppermute x4, waiting for transfers between devices, shifted_in(): return lax.ppermute(edge, axis, pairs)  1.92 us
    concatenate x1, other arithmetic, later_sweep(): halo = jnp.concatenate([h.reshape(-1, depth, loads) for h in halos], axis=0)  0.8 us
  transfers between devices with their start and end apart: 4, of which 1 were waited for; matrix products, arithmetic and copies ran while one was open for 0% of the time, Pallas kernels for 11%

profile of v11, /device:TPU:1, one launch (start us, length us, event | category | flops | bytes accessed | tf_op | source)
XLA Modules:
  0.0 33.5 jit_solution(5251575448512753979)
XLA Ops:
  0.7 3.3 %shard_map.73 = (f32[4,8,64,128]{3,2,1,0:T(8,128)}, bf16[1,8,64,128]{3,2,1,0:T(8,128)(2,1)}, bf16[1,8,64,128]{3,2,1,0:T(8,128)(2,1)}, bf16[4,1,64,128]{3,2,1,0:T(8,128)(2,1)}, bf16[4,1,64,128]{3,2,1,0:T(8,128)(2,1)}) custom-call(s32[8]{0:T(128)} %bitcast.17, s32[1]{0:T(128)} %bitcast.9.count_ref, s32[4,8]{1,0:T(4,128)} %mask_ref.5, ...), custom_call_target="tpu_custom_call" | custom-call | tf_op jit(solution)/shard_map/pallas_call | solution.py:121
  3.9 4.9 %collective-permute-start = (bf16[1,8,64,128]{3,2,1,0:T(8,128)(2,1)}, bf16[1,8,64,128]{3,2,1,0:T(8,128)(2,1)S(1)}, u32[]{:S(2)}, u32[]{:S(2)}) collective-permute-start(bf16[1,8,64,128]{3,2,1,0:T(8,128)(2,1)} %get-tuple-element.11), channel_id=1, source_target_pairs={{0,32},{32,64},{64,96},{96,128},{128,160},{160,192},{192,224},{224... | collective-permute-start | bytes 393224 | tf_op jit(solution)/shard_map/ppermute | solution.py:164
  8.8 12.1 %collective-permute-start.1 = (bf16[1,8,64,128]{3,2,1,0:T(8,128)(2,1)}, bf16[1,8,64,128]{3,2,1,0:T(8,128)(2,1)S(1)}, u32[]{:S(2)}, u32[]{:S(2)}) collective-permute-start(bf16[1,8,64,128]{3,2,1,0:T(8,128)(2,1)} %get-tuple-element.12), channel_id=1, source_target_pairs={{32,0},{64,32},{96,64},{128,96},{160,128},{192,160},{224,192},{256... | collective-permute-start | bytes 393224 | tf_op jit(solution)/shard_map/ppermute | solution.py:164
  20.9 1.3 %collective-permute-start.2 = (bf16[4,1,64,128]{3,2,0,1:T(8,128)(2,1)}, bf16[4,1,64,128]{3,2,0,1:T(8,128)(2,1)S(1)}, u32[]{:S(2)}, u32[]{:S(2)}) collective-permute-start(bf16[4,1,64,128]{3,2,0,1:T(8,128)(2,1)} %bitcast.20), channel_id=1, source_target_pairs={{0,1},{1,2},{2,3},{3,4},{4,5},{5,6},{6,7},{7,8},{8,9},{9,10},{10,1... | collective-permute-start | bytes 196616 | tf_op jit(solution)/shard_map/ppermute | solution.py:164
  22.2 1.3 %collective-permute-start.3 = (bf16[4,1,64,128]{3,2,0,1:T(8,128)(2,1)}, bf16[4,1,64,128]{3,2,0,1:T(8,128)(2,1)S(1)}, u32[]{:S(2)}, u32[]{:S(2)}) collective-permute-start(bf16[4,1,64,128]{3,2,0,1:T(8,128)(2,1)} %bitcast.19), channel_id=1, source_target_pairs={{1,0},{2,1},{3,2},{4,3},{5,4},{6,5},{7,6},{8,7},{9,8},{10,9},{11,1... | collective-permute-start | bytes 196616 | tf_op jit(solution)/shard_map/ppermute | solution.py:164
  23.5 3.6 %shard_map.74.pre_ref = f32[4,8,64,128]{3,2,1,0:T(8,128)} custom-call(s32[4,8]{1,0:T(4,128)} %mask_ref.5, f32[4,8]{1,0:T(4,128)} %stiffness_ref.1, f32[4,8,64,128]{3,2,1,0:T(8,128)} %load_ref.1, f32[4,8,64,128]{3,2,1,0:T(8,128)} %get-tuple-element.10.field_ref, f32[64,64]{1,0:T(8,128)} %operator_ref.1), custom_call_target="tpu_custom_call" | custom-call | flops 201326592 | bytes 3145728 | tf_op jit(solution)/shard_map/pallas_call | solution.py:135
  27.1 0.0 collective-permute-done.2
  27.1 1.9 %collective-permute-done.3 = bf16[4,1,64,128]{3,2,0,1:T(8,128)(2,1)S(1)} collective-permute-done((bf16[4,1,64,128]{3,2,0,1:T(8,128)(2,1)}, bf16[4,1,64,128]{3,2,0,1:T(8,128)(2,1)S(1)}, u32[]{:S(2)}, u32[]{:S(2)}) %collective-permute-start.3) | collective-permute-done | bytes 65568 | tf_op jit(solution)/shard_map/ppermute | solution.py:164
  29.0 0.0 collective-permute-done
  29.0 0.0 collective-permute-done.1
  29.0 0.8 %pad_maximum_fusion.halo_ref = bf16[24,64,128]{2,1,0:T(8,128)(2,1)} fusion(bf16[4,64,128]{2,1,0:T(8,128)(2,1)S(1)} %bitcast.16, bf16[4,64,128]{2,1,0:T(8,128)(2,1)S(1)} %bitcast.15, bf16[8,64,128]{2,1,0:T(8,128)(2,1)S(1)} %bitcast.14, bf16[8,64,128]{2,1,0:T(8,128)(2,1)S(1)} %bitcast.13), kind=kLoop, calls=%fused_computation | loop fusion | flops 589824 | bytes 786432 | tf_op jit(solution)/shard_map/concatenate | solution.py:148
  29.8 3.7 %shard_map.75 = f32[4,8,64,128]{3,2,1,0:T(8,128)} custom-call(s32[8]{0:T(128)} %bitcast.18, s32[1]{0:T(128)} %bitcast.10.count_ref, s32[4,8]{1,0:T(4,128)} %mask_ref.5, f32[4,8,64,128]{3,2,1,0:T(8,128)} %shard_map.74.pre_ref, f32[4,8,64,128]{3,2,1,0:T(8,128)} %get-tuple-element.10.field_ref, bf16[24,64,128]{2,1,0:T(8,128)(2,1)} %pad_maximum_fusion.halo_ref, ...), custom_call_target="tpu_custom_call" | custom-call | tf_op jit(solution)/shard_map/pallas_call | solution.py:149
Async XLA Ops:
  3.9 25.1 %collective-permute-start = (bf16[1,8,64,128]{3,2,1,0:T(8,128)(2,1)}, bf16[1,8,64,128]{3,2,1,0:T(8,128)(2,1)S(1)}, u32[]{:S(2)}, u32[]{:S(2)}) collective-permute-start(bf16[1,8,64,128]{3,2,1,0:T(8,128)(2,1)} %get-tuple-element.11), channel_id=1, source_target_pairs={{0,32},{32,64},{64,96},{96,128},{128,160},{160,192},{192,224},{224... | collective-permute-start | bytes 393224 | tf_op jit(solution)/shard_map/ppermute | solution.py:164
  8.8 20.2 %collective-permute-start.1 = (bf16[1,8,64,128]{3,2,1,0:T(8,128)(2,1)}, bf16[1,8,64,128]{3,2,1,0:T(8,128)(2,1)S(1)}, u32[]{:S(2)}, u32[]{:S(2)}) collective-permute-start(bf16[1,8,64,128]{3,2,1,0:T(8,128)(2,1)} %get-tuple-element.12), channel_id=1, source_target_pairs={{32,0},{64,32},{96,64},{128,96},{160,128},{192,160},{224,192},{256... | collective-permute-start | bytes 393224 | tf_op jit(solution)/shard_map/ppermute | solution.py:164
  20.9 6.2 %collective-permute-start.2 = (bf16[4,1,64,128]{3,2,0,1:T(8,128)(2,1)}, bf16[4,1,64,128]{3,2,0,1:T(8,128)(2,1)S(1)}, u32[]{:S(2)}, u32[]{:S(2)}) collective-permute-start(bf16[4,1,64,128]{3,2,0,1:T(8,128)(2,1)} %bitcast.20), channel_id=1, source_target_pairs={{0,1},{1,2},{2,3},{3,4},{4,5},{5,6},{6,7},{7,8},{8,9},{9,10},{10,1... | collective-permute-start | bytes 196616 | tf_op jit(solution)/shard_map/ppermute | solution.py:164
  22.2 6.8 %collective-permute-start.3 = (bf16[4,1,64,128]{3,2,0,1:T(8,128)(2,1)}, bf16[4,1,64,128]{3,2,0,1:T(8,128)(2,1)S(1)}, u32[]{:S(2)}, u32[]{:S(2)}) collective-permute-start(bf16[4,1,64,128]{3,2,0,1:T(8,128)(2,1)} %bitcast.19), channel_id=1, source_target_pairs={{1,0},{2,1},{3,2},{4,3},{5,4},{6,5},{7,6},{8,7},{9,8},{10,9},{11,1... | collective-permute-start | bytes 196616 | tf_op jit(solution)/shard_map/ppermute | solution.py:164

commit v12 on v8

--- a/solution.py
+++ b/solution.py
@@ -84,11 +84,35 @@
 
 def later_sweep_kernel(
     anchor_ref, count_ref, mask_ref, pre_ref, field_ref,
-    above_ref, below_ref, left_ref, right_ref, inv_ref, out_ref, packed_ref,
+    above_ref, below_ref, left_ref, right_ref, inv_ref, out_ref, packed_ref, cover_ref,
 ):
     rows, columns = field_ref.shape[:2]
+    count = count_ref[0]
+    for vertex in range(rows * columns):
+        cover_ref[vertex] = 0
+    for number in range(inv_ref.shape[0]):
+
+        @pl.when(number < count)
+        def _():
+            anchor = anchor_ref[number]
+            corner = (anchor // (columns - 1)) * columns + anchor % (columns - 1)
+            for offset in (0, 1, columns, columns + 1):
+                cover_ref[corner + offset] = 1
+
     for x in range(rows):
         for y in range(columns):
+            pack_vertex(x, y, cover_ref, mask_ref, pre_ref, above_ref, below_ref,
+                        left_ref, right_ref, packed_ref)
+    out_ref[...] = field_ref[...]
+    deposit_patches(anchor_ref, count_ref, packed_ref, inv_ref, out_ref)
+
+
+def pack_vertex(x, y, cover_ref, mask_ref, pre_ref, above_ref, below_ref, left_ref,
+                right_ref, packed_ref):
+    rows, columns = pre_ref.shape[:2]
+
+    @pl.when(cover_ref[x * columns + y] > 0)
+    def _():
             outside = []
             if x + 1 == rows:
                 outside.append(below_ref[0, y])
@@ -105,8 +129,6 @@
                     halo = halo + term.astype(jnp.float32)
                 value = value + weight_of(mask_ref, x, y) * halo
             packed_ref[x, y] = value.astype(jnp.bfloat16)
-    out_ref[...] = field_ref[...]
-    deposit_patches(anchor_ref, count_ref, packed_ref, inv_ref, out_ref)
 
 
 SMEM = pl.BlockSpec(memory_space=pltpu.SMEM)
@@ -148,7 +170,10 @@
         out_shape=jax.ShapeDtypeStruct(field.shape, jnp.float32),
         in_specs=[SMEM, SMEM, SMEM] + [VMEM] * 7,
         out_specs=VMEM,
-        scratch_shapes=[pltpu.VMEM(field.shape, jnp.bfloat16)],
+        scratch_shapes=[
+            pltpu.VMEM(field.shape, jnp.bfloat16),
+            pltpu.SMEM((field.shape[0] * field.shape[1],), jnp.int32),
+        ],
     )(anchors, count.reshape(1), mask, pre, field, *halos, inverse)
 
 

time: 33.5 us -> 34.2 us (1.021)
  Pallas kernels: 9.85 us -> 11.2 us
  starting transfers between devices: 19.9 us -> 19.4 us
    pallas_call x1, Pallas kernels: 3.31 us -> 4.17 us  [later_sweep(): pl.pallas_call(later_sweep_kernel, out_shape=jax.ShapeDtypeStruct(field.s...]
    pallas_call x1, Pallas kernels: 2.93 us -> 3.47 us  [first_sweep(): pl.pallas_call(first_sweep_kernel, out_shape=(jax.ShapeDtypeStruct(src.sh...]
    ppermute x4, starting transfers between devices: 19.9 us -> 19.4 us  [shifted_in(): return lax.ppermute(edge, axis, pairs)]
where the time goes in v12:
time: 34.2 us; the launch traced here: 33.9 us
  starting transfers between devices  19.4 us (57%)
  Pallas kernels  11.2 us (33%)
  waiting for transfers between devices  1.9 us (6%)
  between operations  0.71 us (2%)
  local copies, waits for them, and re-layouts  0.7 us (2%)
    ppermute x4, starting transfers between devices, shifted_in(): return lax.ppermute(edge, axis, pairs)  19.4 us
    pallas_call x1, Pallas kernels, later_sweep(): pl.pallas_call(later_sweep_kernel, out_shape=jax.ShapeDtypeStruct(field.s...  4.17 us
    pallas_call x1, Pallas kernels, operator_part(): pl.pallas_call(operator_kernel, out_shape=jax.ShapeDtypeStruct(field.shap...  3.61 us
    pallas_call x1, Pallas kernels, first_sweep(): pl.pallas_call(first_sweep_kernel, out_shape=(jax.ShapeDtypeStruct(src.sh...  3.47 us
    ppermute x4, waiting for transfers between devices, shifted_in(): return lax.ppermute(edge, axis, pairs)  1.9 us
    unnamed x8, local copies, waits for them, and re-layouts  0.7 us
  transfers between devices with their start and end apart: 4, of which 1 were waited for; matrix products, arithmetic and copies ran while one was open for 0% of the time, Pallas kernels for 11%

profile of v12, /device:TPU:1, one launch (start us, length us, event | category | flops | bytes accessed | tf_op | source)
XLA Modules:
  0.0 33.9 jit_solution(1310664437105395490)
XLA Ops:
  0.7 3.5 %shard_map.73 = (f32[4,8,64,128]{3,2,1,0:T(8,128)}, bf16[1,8,64,128]{3,2,1,0:T(8,128)(2,1)}, bf16[1,8,64,128]{3,2,1,0:T(8,128)(2,1)}, bf16[4,1,64,128]{3,2,1,0:T(8,128)(2,1)}, bf16[4,1,64,128]{3,2,1,0:T(8,128)(2,1)}) custom-call(s32[8]{0:T(128)} %bitcast.7, s32[1]{0:T(128)} %bitcast.3.count_ref, s32[4,8]{1,0:T(4,128)} %mask_ref.5, ...), custom_call_target="tpu_custom_call" | custom-call | tf_op jit(solution)/shard_map/pallas_call | solution.py:142
  4.1 4.2 %collective-permute-start = (bf16[1,8,64,128]{3,2,1,0:T(8,128)(2,1)}, bf16[1,8,64,128]{3,2,1,0:T(8,128)(2,1)S(1)}, u32[]{:S(2)}, u32[]{:S(2)}) collective-permute-start(bf16[1,8,64,128]{3,2,1,0:T(8,128)(2,1)} %get-tuple-element.11), channel_id=1, source_target_pairs={{0,32},{32,64},{64,96},{96,128},{128,160},{160,192},{192,224},{224... | collective-permute-start | bytes 393224 | tf_op jit(solution)/shard_map/ppermute | solution.py:186
  8.3 12.6 %collective-permute-start.1 = (bf16[1,8,64,128]{3,2,1,0:T(8,128)(2,1)}, bf16[1,8,64,128]{3,2,1,0:T(8,128)(2,1)S(1)}, u32[]{:S(2)}, u32[]{:S(2)}) collective-permute-start(bf16[1,8,64,128]{3,2,1,0:T(8,128)(2,1)} %get-tuple-element.12), channel_id=1, source_target_pairs={{32,0},{64,32},{96,64},{128,96},{160,128},{192,160},{224,192},{256... | collective-permute-start | bytes 393224 | tf_op jit(solution)/shard_map/ppermute | solution.py:186
  20.9 1.3 %collective-permute-start.2 = (bf16[4,1,64,128]{3,2,1,0:T(8,128)(2,1)}, bf16[4,1,64,128]{3,2,1,0:T(8,128)(2,1)S(1)}, u32[]{:S(2)}, u32[]{:S(2)}) collective-permute-start(bf16[4,1,64,128]{3,2,1,0:T(8,128)(2,1)} %get-tuple-element.13), channel_id=1, source_target_pairs={{0,1},{1,2},{2,3},{3,4},{4,5},{5,6},{6,7},{7,8},{8,9},{9,10},{10,1... | collective-permute-start | bytes 196616 | tf_op jit(solution)/shard_map/ppermute | solution.py:186
  22.2 1.3 %collective-permute-start.3 = (bf16[4,1,64,128]{3,2,1,0:T(8,128)(2,1)}, bf16[4,1,64,128]{3,2,1,0:T(8,128)(2,1)S(1)}, u32[]{:S(2)}, u32[]{:S(2)}) collective-permute-start(bf16[4,1,64,128]{3,2,1,0:T(8,128)(2,1)} %get-tuple-element.14), channel_id=1, source_target_pairs={{1,0},{2,1},{3,2},{4,3},{5,4},{6,5},{7,6},{8,7},{9,8},{10,9},{11,1... | collective-permute-start | bytes 196616 | tf_op jit(solution)/shard_map/ppermute | solution.py:186
  23.5 3.6 %shard_map.74.pre_ref = f32[4,8,64,128]{3,2,1,0:T(8,128)} custom-call(s32[4,8]{1,0:T(4,128)} %mask_ref.5, f32[4,8]{1,0:T(4,128)} %stiffness_ref.1, f32[4,8,64,128]{3,2,1,0:T(8,128)} %load_ref.1, f32[4,8,64,128]{3,2,1,0:T(8,128)} %get-tuple-element.10.field_ref, f32[64,64]{1,0:T(8,128)} %operator_ref.1), custom_call_target="tpu_custom_call" | custom-call | flops 201326592 | bytes 3145728 | tf_op jit(solution)/shard_map/pallas_call | solution.py:156
  27.2 0.0 collective-permute-done.2.left_ref
  27.2 0.0 copy-start.2
  27.2 1.9 %collective-permute-done.3.right_ref = bf16[4,1,64,128]{3,2,1,0:T(8,128)(2,1)S(1)} collective-permute-done((bf16[4,1,64,128]{3,2,1,0:T(8,128)(2,1)}, bf16[4,1,64,128]{3,2,1,0:T(8,128)(2,1)S(1)}, u32[]{:S(2)}, u32[]{:S(2)}) %collective-permute-start.3) | collective-permute-done | bytes 65568 | tf_op jit(solution)/shard_map/ppermute | solution.py:186
  29.1 0.0 copy-start.3
  29.1 0.0 collective-permute-done.above_ref
  29.1 0.0 copy-start
  29.1 0.0 collective-permute-done.1.below_ref
  29.1 0.0 copy-start.1
  29.1 0.0 copy-done.2
  29.1 0.6 %copy-done.3 = bf16[4,1,64,128]{3,2,1,0:T(8,128)(2,1)} copy-done((bf16[4,1,64,128]{3,2,1,0:T(8,128)(2,1)}, bf16[4,1,64,128]{3,2,1,0:T(8,128)(2,1)S(1)}, u32[]{:S(2)}) %copy-start.3) | copy-done | bytes 65560
  29.7 0.1 copy-done
  29.7 0.0 copy-done.1
  29.8 4.2 %shard_map.75 = f32[4,8,64,128]{3,2,1,0:T(8,128)} custom-call(s32[8]{0:T(128)} %bitcast.8, s32[1]{0:T(128)} %bitcast.4.count_ref, s32[4,8]{1,0:T(4,128)} %mask_ref.5, f32[4,8,64,128]{3,2,1,0:T(8,128)} %shard_map.74.pre_ref, f32[4,8,64,128]{3,2,1,0:T(8,128)} %get-tuple-element.10.field_ref, bf16[1,8,64,128]{3,2,1,0:T(8,128)(2,1)} %copy-done, ...), custom_call_target="tpu_custom_call" | custom-call | tf_op jit(solution)/shard_map/pallas_call | solution.py:168
Async XLA Ops:
  4.1 24.9 %collective-permute-start = (bf16[1,8,64,128]{3,2,1,0:T(8,128)(2,1)}, bf16[1,8,64,128]{3,2,1,0:T(8,128)(2,1)S(1)}, u32[]{:S(2)}, u32[]{:S(2)}) collective-permute-start(bf16[1,8,64,128]{3,2,1,0:T(8,128)(2,1)} %get-tuple-element.11), channel_id=1, source_target_pairs={{0,32},{32,64},{64,96},{96,128},{128,160},{160,192},{192,224},{224... | collective-permute-start | bytes 393224 | tf_op jit(solution)/shard_map/ppermute | solution.py:186
  8.3 20.8 %collective-permute-start.1 = (bf16[1,8,64,128]{3,2,1,0:T(8,128)(2,1)}, bf16[1,8,64,128]{3,2,1,0:T(8,128)(2,1)S(1)}, u32[]{:S(2)}, u32[]{:S(2)}) collective-permute-start(bf16[1,8,64,128]{3,2,1,0:T(8,128)(2,1)} %get-tuple-element.12), channel_id=1, source_target_pairs={{32,0},{64,32},{96,64},{128,96},{160,128},{192,160},{224,192},{256... | collective-permute-start | bytes 393224 | tf_op jit(solution)/shard_map/ppermute | solution.py:186
  20.9 6.2 %collective-permute-start.2 = (bf16[4,1,64,128]{3,2,1,0:T(8,128)(2,1)}, bf16[4,1,64,128]{3,2,1,0:T(8,128)(2,1)S(1)}, u32[]{:S(2)}, u32[]{:S(2)}) collective-permute-start(bf16[4,1,64,128]{3,2,1,0:T(8,128)(2,1)} %get-tuple-element.13), channel_id=1, source_target_pairs={{0,1},{1,2},{2,3},{3,4},{4,5},{5,6},{6,7},{7,8},{8,9},{9,10},{10,1... | collective-permute-start | bytes 196616 | tf_op jit(solution)/shard_map/ppermute | solution.py:186
  22.2 6.8 %collective-permute-start.3 = (bf16[4,1,64,128]{3,2,1,0:T(8,128)(2,1)}, bf16[4,1,64,128]{3,2,1,0:T(8,128)(2,1)S(1)}, u32[]{:S(2)}, u32[]{:S(2)}) collective-permute-start(bf16[4,1,64,128]{3,2,1,0:T(8,128)(2,1)} %get-tuple-element.14), channel_id=1, source_target_pairs={{1,0},{2,1},{3,2},{4,3},{5,4},{6,5},{7,6},{8,7},{9,8},{10,9},{11,1... | collective-permute-start | bytes 196616 | tf_op jit(solution)/shard_map/ppermute | solution.py:186
  27.2 1.9 %copy-start.2 = (bf16[4,1,64,128]{3,2,1,0:T(8,128)(2,1)}, bf16[4,1,64,128]{3,2,1,0:T(8,128)(2,1)S(1)}, u32[]{:S(2)}) copy-start(bf16[4,1,64,128]{3,2,1,0:T(8,128)(2,1)S(1)} %collective-permute-done.2.left_ref) | copy-start | bytes 196612
  29.1 0.6 %copy-start.3 = (bf16[4,1,64,128]{3,2,1,0:T(8,128)(2,1)}, bf16[4,1,64,128]{3,2,1,0:T(8,128)(2,1)S(1)}, u32[]{:S(2)}) copy-start(bf16[4,1,64,128]{3,2,1,0:T(8,128)(2,1)S(1)} %collective-permute-done.3.right_ref) | copy-start | bytes 196612
  29.1 0.7 %copy-start = (bf16[1,8,64,128]{3,2,1,0:T(8,128)(2,1)}, bf16[1,8,64,128]{3,2,1,0:T(8,128)(2,1)S(1)}, u32[]{:S(2)}) copy-start(bf16[1,8,64,128]{3,2,1,0:T(8,128)(2,1)S(1)} %collective-permute-done.above_ref) | copy-start | bytes 393220
  29.1 0.7 %copy-start.1 = (bf16[1,8,64,128]{3,2,1,0:T(8,128)(2,1)}, bf16[1,8,64,128]{3,2,1,0:T(8,128)(2,1)S(1)}, u32[]{:S(2)}) copy-start(bf16[1,8,64,128]{3,2,1,0:T(8,128)(2,1)S(1)} %collective-permute-done.1.below_ref) | copy-start | bytes 393220

commit v13 on v8

--- a/solution.py
+++ b/solution.py
@@ -15,17 +15,21 @@
     return 1.0 - 0.6 * mask_ref[x, y].astype(jnp.float32)
 
 
-def deposit_patches(anchor_ref, count_ref, src_ref, inv_ref, acc_ref):
+def deposit_patches(anchor_ref, count_ref, src_ref, inv_ref, acc_ref, inner=None):
     rows, columns, depth, loads = src_ref.shape
     slots = inv_ref.shape[0]
     count = count_ref[0]
     for number in range(slots):
-
-        @pl.when(number < count)
+        anchor = anchor_ref[number]
+        row = anchor // (columns - 1)
+        column = anchor % (columns - 1)
+        take = number < count
+        if inner is not None:
+            interior = (row > 0) & (row + 2 < rows) & (column > 0) & (column + 2 < columns)
+            take = take & (interior == inner)
+
+        @pl.when(take)
         def _():
-            anchor = anchor_ref[number]
-            row = anchor // (columns - 1)
-            column = anchor % (columns - 1)
             pieces = [
                 src_ref[row + i, column + j].astype(jnp.bfloat16)
                 for i in range(2)
@@ -56,7 +60,10 @@
         right_ref[x, 0] = (weight_of(mask_ref, x, columns - 1) * acc_ref[x, columns - 1]).astype(right_ref.dtype)
 
 
-def operator_kernel(mask_ref, stiffness_ref, load_ref, field_ref, operator_ref, pre_ref):
+def operator_kernel(
+    anchor_ref, count_ref, mask_ref, stiffness_ref, load_ref, field_ref, operator_ref, inv_ref,
+    pre_ref, base_ref, packed_ref,
+):
     rows, columns, depth, loads = field_ref.shape
 
     def weighted(x, y):
@@ -80,6 +87,9 @@
                 beside = beside + term
             operated = stiffness_ref[x, y] * local[:, y * loads : (y + 1) * loads]
             pre_ref[x, y] = load_ref[x, y] - (operated - weight_of(mask_ref, x, y) * beside)
+            packed_ref[x, y] = pre_ref[x, y].astype(jnp.bfloat16)
+    base_ref[...] = field_ref[...]
+    deposit_patches(anchor_ref, count_ref, packed_ref, inv_ref, base_ref, inner=True)
 
 
 def later_sweep_kernel(
@@ -106,7 +116,7 @@
                 value = value + weight_of(mask_ref, x, y) * halo
             packed_ref[x, y] = value.astype(jnp.bfloat16)
     out_ref[...] = field_ref[...]
-    deposit_patches(anchor_ref, count_ref, packed_ref, inv_ref, out_ref)
+    deposit_patches(anchor_ref, count_ref, packed_ref, inv_ref, out_ref, inner=False)
 
 
 SMEM = pl.BlockSpec(memory_space=pltpu.SMEM)
@@ -128,18 +138,22 @@
     )(anchors, count.reshape(1), mask, src, inverse)
 
 
-def operator_part(load, field, operator, stiffness, mask):
+def operator_part(load, field, operator, stiffness, mask, inverse, anchors, count):
     rows, columns, depth, loads = field.shape
     flops = 2 * rows * columns * depth * depth * loads * 6
     return pl.pallas_call(
         operator_kernel,
-        out_shape=jax.ShapeDtypeStruct(field.shape, jnp.float32),
-        in_specs=[SMEM, SMEM, VMEM, VMEM, VMEM],
-        out_specs=VMEM,
+        out_shape=(
+            jax.ShapeDtypeStruct(field.shape, jnp.float32),
+            jax.ShapeDtypeStruct(field.shape, jnp.float32),
+        ),
+        in_specs=[SMEM, SMEM, SMEM, SMEM, VMEM, VMEM, VMEM, VMEM],
+        out_specs=(VMEM, VMEM),
+        scratch_shapes=[pltpu.VMEM(field.shape, jnp.bfloat16)],
         cost_estimate=pl.CostEstimate(
             flops=flops, bytes_accessed=3 * field.size * 4, transcendentals=0
         ),
-    )(mask, stiffness, load, field, operator)
+    )(anchors, count.reshape(1), mask, stiffness, load, field, operator, inverse)
 
 
 def later_sweep(pre, field, halos, inverse, anchors, count, mask):
@@ -176,8 +190,10 @@
             shifted_in(right, "gy", True),
             shifted_in(left, "gy", False),
         )
-        pre = operator_part(load_field, field, column_operator, stiffness, fault_mask)
-        field = later_sweep(pre, field, halos, inverse, anchors, count, fault_mask)
+        pre, base = operator_part(
+            load_field, field, column_operator, stiffness, fault_mask, inverse, anchors, count
+        )
+        field = later_sweep(pre, base, halos, inverse, anchors, count, fault_mask)
     return field
 
 

time: 33.5 us -> 33.8 us (level)
  Pallas kernels: 9.85 us -> 10.8 us
  waiting for transfers between devices: 1.9 us -> 1.08 us
    ppermute x4, waiting for transfers between devices: 1.9 us -> 1.08 us  [shifted_in(): return lax.ppermute(edge, axis, pairs)]
    pallas_call x1, Pallas kernels: 3.61 us -> 4.42 us  [operator_part(): pl.pallas_call(operator_kernel, out_shape=(jax.ShapeDtypeStruct(field.sha...]
  transfers between devices with their start and end apart: 4 -> 4, of which waited for: 1 -> 1; matrix products, arithmetic and copies ran while one was open for 0% -> 0% of each run, Pallas kernels for 11% -> 13%
where the time goes in v13:
time: 33.8 us; the launch traced here: 33.4 us
  starting transfers between devices  20.1 us (59%)
  Pallas kernels  10.8 us (32%)
  waiting for transfers between devices  1.08 us (3%)
  local copies, waits for them, and re-layouts  0.71 us (2%)
  between operations  0.71 us (2%)
    ppermute x4, starting transfers between devices, shifted_in(): return lax.ppermute(edge, axis, pairs)  20.1 us
    pallas_call x1, Pallas kernels, operator_part(): pl.pallas_call(operator_kernel, out_shape=(jax.ShapeDtypeStruct(field.sha...  4.42 us
    pallas_call x1, Pallas kernels, later_sweep(): pl.pallas_call(later_sweep_kernel, out_shape=jax.ShapeDtypeStruct(field.s...  3.43 us
    pallas_call x1, Pallas kernels, first_sweep(): pl.pallas_call(first_sweep_kernel, out_shape=(jax.ShapeDtypeStruct(src.sh...  2.97 us
    ppermute x4, waiting for transfers between devices, shifted_in(): return lax.ppermute(edge, axis, pairs)  1.08 us
    unnamed x8, local copies, waits for them, and re-layouts  0.71 us
  transfers between devices with their start and end apart: 4, of which 1 were waited for; matrix products, arithmetic and copies ran while one was open for 0% of the time, Pallas kernels for 13%

profile of v13, /device:TPU:1, one launch (start us, length us, event | category | flops | bytes accessed | tf_op | source)
XLA Modules:
  0.0 33.4 jit_solution(4898651534508923588)
XLA Ops:
  0.7 3.0 %shard_map.73 = (f32[4,8,64,128]{3,2,1,0:T(8,128)}, bf16[1,8,64,128]{3,2,1,0:T(8,128)(2,1)}, bf16[1,8,64,128]{3,2,1,0:T(8,128)(2,1)}, bf16[4,1,64,128]{3,2,1,0:T(8,128)(2,1)}, bf16[4,1,64,128]{3,2,1,0:T(8,128)(2,1)}) custom-call(s32[8]{0:T(128)} %bitcast.9, s32[1]{0:T(128)} %bitcast.3.count_ref, s32[4,8]{1,0:T(4,128)} %mask_ref.5, ...), custom_call_target="tpu_custom_call" | custom-call | tf_op jit(solution)/shard_map/pallas_call | solution.py:130
  3.6 5.0 %collective-permute-start = (bf16[1,8,64,128]{3,2,1,0:T(8,128)(2,1)}, bf16[1,8,64,128]{3,2,1,0:T(8,128)(2,1)S(1)}, u32[]{:S(2)}, u32[]{:S(2)}) collective-permute-start(bf16[1,8,64,128]{3,2,1,0:T(8,128)(2,1)} %get-tuple-element.15), channel_id=1, source_target_pairs={{0,32},{32,64},{64,96},{96,128},{128,160},{160,192},{192,224},{224... | collective-permute-start | bytes 393224 | tf_op jit(solution)/shard_map/ppermute | solution.py:175
  8.7 12.5 %collective-permute-start.1 = (bf16[1,8,64,128]{3,2,1,0:T(8,128)(2,1)}, bf16[1,8,64,128]{3,2,1,0:T(8,128)(2,1)S(1)}, u32[]{:S(2)}, u32[]{:S(2)}) collective-permute-start(bf16[1,8,64,128]{3,2,1,0:T(8,128)(2,1)} %get-tuple-element.16), channel_id=1, source_target_pairs={{32,0},{64,32},{96,64},{128,96},{160,128},{192,160},{224,192},{256... | collective-permute-start | bytes 393224 | tf_op jit(solution)/shard_map/ppermute | solution.py:175
  21.2 1.3 %collective-permute-start.2 = (bf16[4,1,64,128]{3,2,1,0:T(8,128)(2,1)}, bf16[4,1,64,128]{3,2,1,0:T(8,128)(2,1)S(1)}, u32[]{:S(2)}, u32[]{:S(2)}) collective-permute-start(bf16[4,1,64,128]{3,2,1,0:T(8,128)(2,1)} %get-tuple-element.17), channel_id=1, source_target_pairs={{0,1},{1,2},{2,3},{3,4},{4,5},{5,6},{6,7},{7,8},{8,9},{9,10},{10,1... | collective-permute-start | bytes 196616 | tf_op jit(solution)/shard_map/ppermute | solution.py:175
  22.5 1.3 %collective-permute-start.3 = (bf16[4,1,64,128]{3,2,1,0:T(8,128)(2,1)}, bf16[4,1,64,128]{3,2,1,0:T(8,128)(2,1)S(1)}, u32[]{:S(2)}, u32[]{:S(2)}) collective-permute-start(bf16[4,1,64,128]{3,2,1,0:T(8,128)(2,1)} %get-tuple-element.18), channel_id=1, source_target_pairs={{1,0},{2,1},{3,2},{4,3},{5,4},{6,5},{7,6},{8,7},{9,8},{10,9},{11,1... | collective-permute-start | bytes 196616 | tf_op jit(solution)/shard_map/ppermute | solution.py:175
  23.8 4.4 %shard_map.74 = (f32[4,8,64,128]{3,2,1,0:T(8,128)}, f32[4,8,64,128]{3,2,1,0:T(8,128)}) custom-call(s32[8]{0:T(128)} %bitcast.10, s32[1]{0:T(128)} %bitcast.4.count_ref, s32[4,8]{1,0:T(4,128)} %mask_ref.5, f32[4,8]{1,0:T(4,128)} %stiffness_ref.1, f32[4,8,64,128]{3,2,1,0:T(8,128)} %load_ref.1, f32[4,8,64,128]{3,2,1,0:T(8,128)} %get-tuple-element.12.field_ref, ...), custom_call_target="tpu_custom_call" | custom-call | flops 201326592 | bytes 3145728 | tf_op jit(solution)/shard_map/pallas_call | solution.py:144
  28.2 0.0 collective-permute-done.2.left_ref
  28.2 0.0 copy-start.2
  28.2 1.1 %collective-permute-done.3.right_ref = bf16[4,1,64,128]{3,2,1,0:T(8,128)(2,1)S(1)} collective-permute-done((bf16[4,1,64,128]{3,2,1,0:T(8,128)(2,1)}, bf16[4,1,64,128]{3,2,1,0:T(8,128)(2,1)S(1)}, u32[]{:S(2)}, u32[]{:S(2)}) %collective-permute-start.3) | collective-permute-done | bytes 65568 | tf_op jit(solution)/shard_map/ppermute | solution.py:175
  29.3 0.0 copy-start.3
  29.3 0.0 collective-permute-done.above_ref
  29.3 0.0 copy-start
  29.3 0.0 collective-permute-done.1.below_ref
  29.3 0.0 copy-start.1
  29.3 0.0 copy-done.2
  29.3 0.6 %copy-done.3 = bf16[4,1,64,128]{3,2,1,0:T(8,128)(2,1)} copy-done((bf16[4,1,64,128]{3,2,1,0:T(8,128)(2,1)}, bf16[4,1,64,128]{3,2,1,0:T(8,128)(2,1)S(1)}, u32[]{:S(2)}) %copy-start.3) | copy-done | bytes 65560
  29.9 0.1 copy-done
  29.9 0.0 copy-done.1
  30.0 3.4 %shard_map.75 = f32[4,8,64,128]{3,2,1,0:T(8,128)} custom-call(s32[8]{0:T(128)} %bitcast.11, s32[1]{0:T(128)} %bitcast.5.count_ref, s32[4,8]{1,0:T(4,128)} %mask_ref.5, f32[4,8,64,128]{3,2,1,0:T(8,128)} %get-tuple-element.13.pre_ref, f32[4,8,64,128]{3,2,1,0:T(8,128)} %get-tuple-element.14.field_ref, bf16[1,8,64,128]{3,2,1,0:T(8,128)(2,1)} %copy-done, ...), custom_call_target="tpu_custom_call" | custom-call | tf_op jit(solution)/shard_map/pallas_call | solution.py:160
Async XLA Ops:
  3.6 25.6 %collective-permute-start = (bf16[1,8,64,128]{3,2,1,0:T(8,128)(2,1)}, bf16[1,8,64,128]{3,2,1,0:T(8,128)(2,1)S(1)}, u32[]{:S(2)}, u32[]{:S(2)}) collective-permute-start(bf16[1,8,64,128]{3,2,1,0:T(8,128)(2,1)} %get-tuple-element.15), channel_id=1, source_target_pairs={{0,32},{32,64},{64,96},{96,128},{128,160},{160,192},{192,224},{224... | collective-permute-start | bytes 393224 | tf_op jit(solution)/shard_map/ppermute | solution.py:175
  8.7 20.6 %collective-permute-start.1 = (bf16[1,8,64,128]{3,2,1,0:T(8,128)(2,1)}, bf16[1,8,64,128]{3,2,1,0:T(8,128)(2,1)S(1)}, u32[]{:S(2)}, u32[]{:S(2)}) collective-permute-start(bf16[1,8,64,128]{3,2,1,0:T(8,128)(2,1)} %get-tuple-element.16), channel_id=1, source_target_pairs={{32,0},{64,32},{96,64},{128,96},{160,128},{192,160},{224,192},{256... | collective-permute-start | bytes 393224 | tf_op jit(solution)/shard_map/ppermute | solution.py:175
  21.2 7.0 %collective-permute-start.2 = (bf16[4,1,64,128]{3,2,1,0:T(8,128)(2,1)}, bf16[4,1,64,128]{3,2,1,0:T(8,128)(2,1)S(1)}, u32[]{:S(2)}, u32[]{:S(2)}) collective-permute-start(bf16[4,1,64,128]{3,2,1,0:T(8,128)(2,1)} %get-tuple-element.17), channel_id=1, source_target_pairs={{0,1},{1,2},{2,3},{3,4},{4,5},{5,6},{6,7},{7,8},{8,9},{9,10},{10,1... | collective-permute-start | bytes 196616 | tf_op jit(solution)/shard_map/ppermute | solution.py:175
  22.5 6.8 %collective-permute-start.3 = (bf16[4,1,64,128]{3,2,1,0:T(8,128)(2,1)}, bf16[4,1,64,128]{3,2,1,0:T(8,128)(2,1)S(1)}, u32[]{:S(2)}, u32[]{:S(2)}) collective-permute-start(bf16[4,1,64,128]{3,2,1,0:T(8,128)(2,1)} %get-tuple-element.18), channel_id=1, source_target_pairs={{1,0},{2,1},{3,2},{4,3},{5,4},{6,5},{7,6},{8,7},{9,8},{10,9},{11,1... | collective-permute-start | bytes 196616 | tf_op jit(solution)/shard_map/ppermute | solution.py:175
  28.2 1.1 %copy-start.2 = (bf16[4,1,64,128]{3,2,1,0:T(8,128)(2,1)}, bf16[4,1,64,128]{3,2,1,0:T(8,128)(2,1)S(1)}, u32[]{:S(2)}) copy-start(bf16[4,1,64,128]{3,2,1,0:T(8,128)(2,1)S(1)} %collective-permute-done.2.left_ref) | copy-start | bytes 196612
  29.3 0.6 %copy-start.3 = (bf16[4,1,64,128]{3,2,1,0:T(8,128)(2,1)}, bf16[4,1,64,128]{3,2,1,0:T(8,128)(2,1)S(1)}, u32[]{:S(2)}) copy-start(bf16[4,1,64,128]{3,2,1,0:T(8,128)(2,1)S(1)} %collective-permute-done.3.right_ref) | copy-start | bytes 196612
  29.3 0.7 %copy-start = (bf16[1,8,64,128]{3,2,1,0:T(8,128)(2,1)}, bf16[1,8,64,128]{3,2,1,0:T(8,128)(2,1)S(1)}, u32[]{:S(2)}) copy-start(bf16[1,8,64,128]{3,2,1,0:T(8,128)(2,1)S(1)} %collective-permute-done.above_ref) | copy-start | bytes 393220
  29.3 0.7 %copy-start.1 = (bf16[1,8,64,128]{3,2,1,0:T(8,128)(2,1)}, bf16[1,8,64,128]{3,2,1,0:T(8,128)(2,1)S(1)}, u32[]{:S(2)}) copy-start(bf16[1,8,64,128]{3,2,1,0:T(8,128)(2,1)S(1)} %collective-permute-done.1.below_ref) | copy-start | bytes 393220
